TPU v7x, 256 devices: a whole 4x4x8 slice. The times are simulated.
256 devices in a mesh: chain: 16 (over z_lo, y), head: 16 (over z_hi, x, core).
Axes of the slice: x: 4, y: 4, z: 8 (z_hi: 2, z_lo: 4; z = z_hi * 4 + z_lo), core: 2. Of those that a mesh axis runs over, the one named last changes fastest.
Arguments:
- signal: bfloat16 [32768, 16384], P(('chain', 'head')), may hold values from -6 to 6
- input_map: bfloat16 [32768, 2048], P(('chain', 'head')), may hold values from -0.375 to 0.375
- output_map: bfloat16 [32768, 2048], P(('chain', 'head')), may hold values from -6 to 6
- step_size: bfloat16 [32768, 256], P(('chain', 'head')), may hold values from 0.000220970869 to 1.61
- decay_rate: float32 [256], replicated, may hold values from 0.077339804 to 0.3
- skip_gain: float32 [256], replicated, may hold values from 0.5 to 1.5
Outputs:
- mixed: bfloat16 [32768, 16384], P(('chain', 'head'))
All inputs are finite; a program needn't handle non-finite values.
Results may differ from a plain program's by a relative error of at most 0.0045.
Values may be sent and summed in bfloat16 or wider, within the bound.
No kernel may reach another device: no remote copies, remote signals or barrier semaphores. Data moves between devices by JAX's collectives and lax.ppermute only.
A program may use at most 192 MiB of HBM per device.

v0:
```python
import jax
import jax.numpy as jnp
from jax import lax
from jax.sharding import PartitionSpec as P

HEADS = 256
CHANNEL_WIDTH = 64
SSTATE = 256
HEAD_GROUPS = 8
BLOCK = 256


def from_behind(array, axis, by):
    size = lax.axis_size(axis)
    pairs = [(i, i + by) for i in range(size) if 0 <= i + by < size]
    return lax.ppermute(array, axis, pairs)


def prepare(input_c, output_c, step_c, decay_rate, local_heads, group_count):
    chain_rows = input_c.shape[0]
    blocks = chain_rows // BLOCK
    per_group = local_heads // group_count
    head_start = lax.axis_index("head") * local_heads
    head_rates = lax.dynamic_slice_in_dim(decay_rate, head_start, local_heads)
    step_rate = step_c.astype(jnp.float32).reshape(blocks, BLOCK, local_heads)
    cumul = jnp.cumsum(-head_rates * step_rate, axis=1)
    input_groups = input_c.reshape(blocks, BLOCK, group_count, SSTATE)
    output_groups = output_c.reshape(blocks, BLOCK, group_count, SSTATE)
    causal = jnp.arange(BLOCK)[:, None] >= jnp.arange(BLOCK)[None, :]

    def block_weights(pieces):
        cumul_k, step_k, input_k, output_k = pieces
        scores = jnp.einsum("tgn,sgn->gts", output_k, input_k, preferred_element_type=jnp.float32)
        cumul_heads = cumul_k.T.reshape(group_count, per_group, BLOCK)
        differ = jnp.where(causal, cumul_heads[:, :, :, None] - cumul_heads[:, :, None, :], 0.0)
        decays = jnp.where(causal, jnp.exp(differ), 0.0)
        step_heads = step_k.T.reshape(group_count, per_group, 1, BLOCK)
        weights = decays * scores[:, None] * step_heads
        return weights.astype(jnp.bfloat16).reshape(local_heads, BLOCK, BLOCK)

    weights = lax.map(block_weights, (cumul, step_rate, input_groups, output_groups))
    return (step_rate, cumul, input_groups, output_groups, weights)


def finish(signal_c, prepared, skip_gain, local_heads, group_count):
    step_rate, cumul, input_groups, output_groups, weights = prepared
    blocks = cumul.shape[0]
    per_group = local_heads // group_count
    values = signal_c.reshape(blocks, BLOCK, local_heads, CHANNEL_WIDTH)
    values_wide = values.astype(jnp.float32)
    within = jnp.einsum("khts,kshp->kthp", weights, values, preferred_element_type=jnp.float32)
    to_end = jnp.exp(cumul[:, -1:, :] - cumul) * step_rate
    update = (to_end[..., None] * values_wide).astype(jnp.bfloat16)
    update = update.reshape(blocks, BLOCK, group_count, per_group, CHANNEL_WIDTH)
    fresh_state = jnp.einsum(
        "ksgjp,ksgn->kgjpn", update, input_groups, preferred_element_type=jnp.float32
    )
    fresh_state = fresh_state.reshape(blocks, local_heads, CHANNEL_WIDTH, SSTATE)
    block_ends = cumul[:, -1, :]

    def carry_step(carry_state, pieces):
        block_end, fresh_block = pieces
        return (jnp.exp(block_end)[:, None, None] * carry_state + fresh_block, carry_state)

    empty_state = jnp.zeros((local_heads, CHANNEL_WIDTH, SSTATE), jnp.float32)
    final_state, starts = lax.scan(carry_step, empty_state, (block_ends, fresh_state))
    before = jnp.cumsum(block_ends, axis=0) - block_ends
    totals = jnp.sum(block_ends, axis=0)
    chain_len = lax.axis_size("chain")

    def relay_turn(turn_index, arriving):
        leaving = jnp.exp(totals)[:, None, None] * arriving + final_state
        return from_behind(leaving, "chain", 1)

    incoming_state = lax.fori_loop(0, chain_len - 1, relay_turn, jnp.zeros_like(final_state))
    starts = starts + jnp.exp(before)[:, :, None, None] * incoming_state
    rounded = starts.astype(jnp.bfloat16).reshape(
        blocks, group_count, per_group, CHANNEL_WIDTH, SSTATE
    )
    carried = jnp.einsum(
        "ktgn,kgjpn->ktgjp", output_groups, rounded, preferred_element_type=jnp.float32
    )
    carried = carried.reshape(blocks, BLOCK, local_heads, CHANNEL_WIDTH) * jnp.exp(cumul)[..., None]
    head_start = lax.axis_index("head") * local_heads
    gain_heads = lax.dynamic_slice_in_dim(skip_gain, head_start, local_heads)
    result = (within + carried + gain_heads[:, None] * values_wide).astype(jnp.bfloat16)
    result = result.reshape(blocks * BLOCK, local_heads * CHANNEL_WIDTH)
    return lax.all_to_all(result, "head", split_axis=0, concat_axis=1, tiled=True)


def shards(signal, input_map, output_map, step_size, decay_rate, skip_gain):
    head_count = lax.axis_size("head")
    local_heads = HEADS // head_count
    group_heads = HEADS // HEAD_GROUPS
    group_count = max(1, local_heads // group_heads)
    copies = max(1, group_heads // local_heads)
    row_count = signal.shape[0]
    input_rep = jnp.repeat(
        input_map.reshape(row_count, HEAD_GROUPS, SSTATE), copies, axis=1
    ).reshape(row_count, -1)
    output_rep = jnp.repeat(
        output_map.reshape(row_count, HEAD_GROUPS, SSTATE), copies, axis=1
    ).reshape(row_count, -1)
    signal_c, input_c, output_c, step_c = (
        lax.all_to_all(signal, "head", split_axis=1, concat_axis=0, tiled=True),
        lax.all_to_all(input_rep, "head", split_axis=1, concat_axis=0, tiled=True),
        lax.all_to_all(output_rep, "head", split_axis=1, concat_axis=0, tiled=True),
        lax.all_to_all(step_size, "head", split_axis=1, concat_axis=0, tiled=True),
    )
    prepared = prepare(input_c, output_c, step_c, decay_rate, local_heads, group_count)
    return finish(signal_c, prepared, skip_gain, local_heads, group_count)


def solution(mesh):
    return jax.shard_map(
        shards,
        mesh=mesh,
        in_specs=(
            P(("chain", "head"), None),
            P(("chain", "head"), None),
            P(("chain", "head"), None),
            P(("chain", "head"), None),
            P(),
            P(),
        ),
        out_specs=P(("chain", "head"), None),
        check_vma=False,
    )
```

profile of v0, /device:TPU:96, one launch (start us, length us, event | category | flops | bytes accessed | tf_op | source)
XLA Modules:
  0.0 758.7 jit_solution(17827331197873007120)
XLA Ops:
  25.8 21.8 %all-to-all-done.2 = bf16[128,16,256]{2,0,1:T(8,128)(2,1)S(1)} async-done(((bf16[128,16,256]{2,0,1:T(8,128)(2,1)}), bf16[128,16,256]{2,0,1:T(8,128)(2,1)S(1)}, u32[]{:S(2)}, u32[]{:S(2)}) %all-to-all-start.2) | async-done | bytes 1048608 | tf_op jit(solution)/shard_map/all_to_all | solution.py:106
  64.2 14.2 %all-to-all-done.1 = bf16[128,16,256]{2,0,1:T(8,128)(2,1)S(1)} async-done(((bf16[128,16,256]{2,0,1:T(8,128)(2,1)}), bf16[128,16,256]{2,0,1:T(8,128)(2,1)S(1)}, u32[]{:S(2)}, u32[]{:S(2)}) %all-to-all-start.1) | async-done | bytes 1048608 | tf_op jit(solution)/shard_map/all_to_all | solution.py:107
  78.4 12.5 %all-to-all-start.3 = ((bf16[128,16,1024]{0,2,1:T(8,128)(2,1)}), bf16[128,16,1024]{0,2,1:T(8,128)(2,1)}, u32[]{:S(2)}, u32[]{:S(2)}) async-start(bf16[128,16,1024]{0,2,1:T(8,128)(2,1)} %bitcast.119), calls=%async_computation.3 | async-start | bytes 8388608 | tf_op jit(solution)/shard_map/all_to_all | solution.py:105
  100.0 20.5 %while.38 = (s32[]{:T(128)}, bf16[8,16,256,256]{3,2,1,0:T(8,128)(2,1)}, f32[8,256,16]{1,0,2:T(8,128)S(1)}, bf16[8,256,1,256]{3,1,2,0:T(8,128)(2,1)S(1)}, bf16[8,...) while((s32[]{:T(128)}, ...), condition=%wide.region_3.4_spmd.clone.clone, body=%wide.region_2.3_spmd.clone.clone.sunk | while | flops 39911424 | bytes 3196497 | solution.py:41
  120.5 36.3 %all-to-all-done.3 = bf16[128,16,1024]{0,2,1:T(8,128)(2,1)} async-done(((bf16[128,16,1024]{0,2,1:T(8,128)(2,1)}), bf16[128,16,1024]{0,2,1:T(8,128)(2,1)}, u32[]{:S(2)}, u32[]{:S(2)}) %all-to-all-start.3) | async-done | bytes 4194336 | tf_op jit(solution)/shard_map/all_to_all | solution.py:105
  177.5 20.3 %while.39 = (s32[]{:T(128)}, f32[16,64,256]{2,1,0:T(8,128)S(1)}, f32[8,16,64,256]{3,2,1,0:T(8,128)}, f32[8,16]{1,0:T(8,128)S(1)}, f32[8,16,64,256]{3,2,1,0:T(8,128)}, /*index=5*/s32[]{:T(128)}, s32[]{:T(128)}) while((s32[]{:T(128)}, f32[16,64,256]{2,1,0:T(8,128)S(1)}, f32[8,16,64,256]{3,2,1,0:T(8,128)}, f32[8,16]{1,0:T(8,128)S(1)}, ...), condition=%wide.region_5.6_spmd.clone, body=%wide.region_4.5_spmd.clone.sunk | while | flops 1048579 | bytes 5243680 | solution.py:66
  198.0 406.1 %while.37 = (s32[]{:T(128)}, f32[16,64,256]{2,1,0:T(8,128)S(1)}, f32[16,1,1]{0,2,1:T(1,128)S(1)}, f32[16,64,256]{2,1,0:T(8,128)S(1)}, s32[]{:T(128)}) while((s32[]{:T(128)}, f32[16,64,256]{2,1,0:T(8,128)S(1)}, f32[16,1,1]{0,2,1:T(1,128)S(1)}, f32[16,64,256]{2,1,0:T(8,128)S(1)}, s32[]{:T(128)}) %tuple.73), condition=%wide.region_9.10_spmd, body=%wide.region_8.9_spmd.sunk | while | flops 524290 | bytes 7340197 | solution.py:75
  201.6 59.9 %collective-permute-done = f32[16,64,256]{2,1,0:T(8,128)S(1)} collective-permute-done((f32[16,64,256]{2,1,0:T(8,128)S(1)}, f32[16,64,256]{2,1,0:T(8,128)S(1)}, u32[]{:S(2)}, u32[]{:S(2)}) %collective-permute-start) | collective-permute-done | bytes 1048608 | tf_op jit(solution)/shard_map/while/body/eval_jaxpr/ppermute | solution.py:16
  263.6 26.6 %collective-permute-done = f32[16,64,256]{2,1,0:T(8,128)S(1)} collective-permute-done((f32[16,64,256]{2,1,0:T(8,128)S(1)}, f32[16,64,256]{2,1,0:T(8,128)S(1)}, u32[]{:S(2)}, u32[]{:S(2)}) %collective-permute-start) | collective-permute-done | bytes 1048608 | tf_op jit(solution)/shard_map/while/body/eval_jaxpr/ppermute | solution.py:16
  292.3 25.7 %collective-permute-done = f32[16,64,256]{2,1,0:T(8,128)S(1)} collective-permute-done((f32[16,64,256]{2,1,0:T(8,128)S(1)}, f32[16,64,256]{2,1,0:T(8,128)S(1)}, u32[]{:S(2)}, u32[]{:S(2)}) %collective-permute-start) | collective-permute-done | bytes 1048608 | tf_op jit(solution)/shard_map/while/body/eval_jaxpr/ppermute | solution.py:16
  320.1 24.9 %collective-permute-done = f32[16,64,256]{2,1,0:T(8,128)S(1)} collective-permute-done((f32[16,64,256]{2,1,0:T(8,128)S(1)}, f32[16,64,256]{2,1,0:T(8,128)S(1)}, u32[]{:S(2)}, u32[]{:S(2)}) %collective-permute-start) | collective-permute-done | bytes 1048608 | tf_op jit(solution)/shard_map/while/body/eval_jaxpr/ppermute | solution.py:16
  347.1 24.0 %collective-permute-done = f32[16,64,256]{2,1,0:T(8,128)S(1)} collective-permute-done((f32[16,64,256]{2,1,0:T(8,128)S(1)}, f32[16,64,256]{2,1,0:T(8,128)S(1)}, u32[]{:S(2)}, u32[]{:S(2)}) %collective-permute-start) | collective-permute-done | bytes 1048608 | tf_op jit(solution)/shard_map/while/body/eval_jaxpr/ppermute | solution.py:16
  373.2 23.1 %collective-permute-done = f32[16,64,256]{2,1,0:T(8,128)S(1)} collective-permute-done((f32[16,64,256]{2,1,0:T(8,128)S(1)}, f32[16,64,256]{2,1,0:T(8,128)S(1)}, u32[]{:S(2)}, u32[]{:S(2)}) %collective-permute-start) | collective-permute-done | bytes 1048608 | tf_op jit(solution)/shard_map/while/body/eval_jaxpr/ppermute | solution.py:16
  398.4 22.3 %collective-permute-done = f32[16,64,256]{2,1,0:T(8,128)S(1)} collective-permute-done((f32[16,64,256]{2,1,0:T(8,128)S(1)}, f32[16,64,256]{2,1,0:T(8,128)S(1)}, u32[]{:S(2)}, u32[]{:S(2)}) %collective-permute-start) | collective-permute-done | bytes 1048608 | tf_op jit(solution)/shard_map/while/body/eval_jaxpr/ppermute | solution.py:16
  422.8 21.4 %collective-permute-done = f32[16,64,256]{2,1,0:T(8,128)S(1)} collective-permute-done((f32[16,64,256]{2,1,0:T(8,128)S(1)}, f32[16,64,256]{2,1,0:T(8,128)S(1)}, u32[]{:S(2)}, u32[]{:S(2)}) %collective-permute-start) | collective-permute-done | bytes 1048608 | tf_op jit(solution)/shard_map/while/body/eval_jaxpr/ppermute | solution.py:16
  446.3 21.2 %collective-permute-done = f32[16,64,256]{2,1,0:T(8,128)S(1)} collective-permute-done((f32[16,64,256]{2,1,0:T(8,128)S(1)}, f32[16,64,256]{2,1,0:T(8,128)S(1)}, u32[]{:S(2)}, u32[]{:S(2)}) %collective-permute-start) | collective-permute-done | bytes 1048608 | tf_op jit(solution)/shard_map/while/body/eval_jaxpr/ppermute | solution.py:16
  469.7 21.2 %collective-permute-done = f32[16,64,256]{2,1,0:T(8,128)S(1)} collective-permute-done((f32[16,64,256]{2,1,0:T(8,128)S(1)}, f32[16,64,256]{2,1,0:T(8,128)S(1)}, u32[]{:S(2)}, u32[]{:S(2)}) %collective-permute-start) | collective-permute-done | bytes 1048608 | tf_op jit(solution)/shard_map/while/body/eval_jaxpr/ppermute | solution.py:16
  493.0 21.2 %collective-permute-done = f32[16,64,256]{2,1,0:T(8,128)S(1)} collective-permute-done((f32[16,64,256]{2,1,0:T(8,128)S(1)}, f32[16,64,256]{2,1,0:T(8,128)S(1)}, u32[]{:S(2)}, u32[]{:S(2)}) %collective-permute-start) | collective-permute-done | bytes 1048608 | tf_op jit(solution)/shard_map/while/body/eval_jaxpr/ppermute | solution.py:16
  516.3 21.2 %collective-permute-done = f32[16,64,256]{2,1,0:T(8,128)S(1)} collective-permute-done((f32[16,64,256]{2,1,0:T(8,128)S(1)}, f32[16,64,256]{2,1,0:T(8,128)S(1)}, u32[]{:S(2)}, u32[]{:S(2)}) %collective-permute-start) | collective-permute-done | bytes 1048608 | tf_op jit(solution)/shard_map/while/body/eval_jaxpr/ppermute | solution.py:16
  539.6 21.2 %collective-permute-done = f32[16,64,256]{2,1,0:T(8,128)S(1)} collective-permute-done((f32[16,64,256]{2,1,0:T(8,128)S(1)}, f32[16,64,256]{2,1,0:T(8,128)S(1)}, u32[]{:S(2)}, u32[]{:S(2)}) %collective-permute-start) | collective-permute-done | bytes 1048608 | tf_op jit(solution)/shard_map/while/body/eval_jaxpr/ppermute | solution.py:16
  563.0 22.1 %collective-permute-done = f32[16,64,256]{2,1,0:T(8,128)S(1)} collective-permute-done((f32[16,64,256]{2,1,0:T(8,128)S(1)}, f32[16,64,256]{2,1,0:T(8,128)S(1)}, u32[]{:S(2)}, u32[]{:S(2)}) %collective-permute-start) | collective-permute-done | bytes 1048608 | tf_op jit(solution)/shard_map/while/body/eval_jaxpr/ppermute | solution.py:16
  587.2 16.9 %collective-permute-done = f32[16,64,256]{2,1,0:T(8,128)S(1)} collective-permute-done((f32[16,64,256]{2,1,0:T(8,128)S(1)}, f32[16,64,256]{2,1,0:T(8,128)S(1)}, u32[]{:S(2)}, u32[]{:S(2)}) %collective-permute-start) | collective-permute-done | bytes 1048608 | tf_op jit(solution)/shard_map/while/body/eval_jaxpr/ppermute | solution.py:16
  612.3 12.1 %fusion.13 = bf16[8,256,16,64]{1,3,2,0:T(8,128)(2,1)} fusion(f32[8,16,64,256]{3,2,1,0:T(8,128)} %fusion.15, f32[16]{0:T(128)S(1)} %copy-done.3, f32[8,256,16]{1,2,0:T(8,128)S(1)} %copy-done.2, bf16[8,16,256,256]{3,2,1,0:T(8,128)(2,1)} %get-tuple-element.123, bf16[8,256,16,64]{1,0,3,2:T(8,128)(2,1)S(1)} %copy-done), kind=kOutput, calls=%fused_computation.24 | convolution fusion | flops 1086324736 | bytes 33685568 | tf_op jit(solution)/shard_map/khts,kshp->kthp/dot_general | solution.py:51
  641.9 110.5 %all_to_all.80 = bf16[16,128,1024]{1,2,0:T(8,128)(2,1)} all-to-all(bf16[16,128,1024]{1,2,0:T(8,128)(2,1)S(1)} %copy.80), channel_id=1, replica_groups=mesh['chain'=16,'head'=16] {'head'}, dimensions={0} | all-to-all | bytes 8388608 | tf_op jit(solution)/shard_map/all_to_all | solution.py:88
  (161 shorter events, 177.4 us)
Async XLA Ops:
  1.6 18.4 %all-to-all-start = ((bf16[128,16,16]{0,2,1:T(8,128)(2,1)}), bf16[128,16,16]{0,2,1:T(8,128)(2,1)S(1)}, u32[]{:S(2)}, u32[]{:S(2)}) async-start(bf16[128,16,16]{0,2,1:T(8,128)(2,1)} %bitcast.1), calls=%async_computation | async-start | bytes 131072 | tf_op jit(solution)/shard_map/all_to_all | solution.py:108
  21.1 26.5 %all-to-all-start.2 = ((bf16[128,16,256]{2,0,1:T(8,128)(2,1)}), bf16[128,16,256]{2,0,1:T(8,128)(2,1)S(1)}, u32[]{:S(2)}, u32[]{:S(2)}) async-start(bf16[128,16,256]{2,0,1:T(8,128)(2,1)} %bitcast.11), calls=%async_computation.2 | async-start | bytes 2097152 | tf_op jit(solution)/shard_map/all_to_all | solution.py:106
  48.7 29.7 %all-to-all-start.1 = ((bf16[128,16,256]{2,0,1:T(8,128)(2,1)}), bf16[128,16,256]{2,0,1:T(8,128)(2,1)S(1)}, u32[]{:S(2)}, u32[]{:S(2)}) async-start(bf16[128,16,256]{2,0,1:T(8,128)(2,1)} %bitcast.7), calls=%async_computation.1 | async-start | bytes 2097152 | tf_op jit(solution)/shard_map/all_to_all | solution.py:107
  57.8 33.1 %copy-start.4 = (f32[256]{0:T(256)S(1)}, f32[256]{0:T(256)}, u32[]{:S(2)}) copy-start(f32[256]{0:T(256)} %param.17) | copy-start | bytes 3076
  57.8 33.7 %copy-start.5 = (f32[256]{0:T(256)S(1)}, f32[256]{0:T(256)}, u32[]{:S(2)}) copy-start(f32[256]{0:T(256)} %param.16) | copy-start | bytes 3076
  78.4 78.5 %all-to-all-start.3 = ((bf16[128,16,1024]{0,2,1:T(8,128)(2,1)}), bf16[128,16,1024]{0,2,1:T(8,128)(2,1)}, u32[]{:S(2)}, u32[]{:S(2)}) async-start(bf16[128,16,1024]{0,2,1:T(8,128)(2,1)} %bitcast.119), calls=%async_computation.3 | async-start | bytes 8388608 | tf_op jit(solution)/shard_map/all_to_all | solution.py:105
  120.5 50.3 %copy-start.1 = (bf16[8,256,1,256]{3,1,2,0:T(8,128)(2,1)}, bf16[8,256,1,256]{3,1,2,0:T(8,128)(2,1)S(1)}, u32[]{:S(2)}) copy-start(bf16[8,256,1,256]{3,1,2,0:T(8,128)(2,1)S(1)} %get-tuple-element.398) | copy-start | bytes 3145732
  198.2 63.4 %collective-permute-start = (f32[16,64,256]{2,1,0:T(8,128)S(1)}, f32[16,64,256]{2,1,0:T(8,128)S(1)}, u32[]{:S(2)}, u32[]{:S(2)}) collective-permute-start(f32[16,64,256]{2,1,0:T(8,128)S(1)} %multiply_add_fusion.2), channel_id=1, source_target_pairs={{0,16},{16,32},{32,48},{48,64},{64,80},{80,96},{96,112},{112,128},... | collective-permute-start | bytes 3145736 | tf_op jit(solution)/shard_map/while/body/eval_jaxpr/ppermute | solution.py:16
  261.7 28.5 %collective-permute-start = (f32[16,64,256]{2,1,0:T(8,128)S(1)}, f32[16,64,256]{2,1,0:T(8,128)S(1)}, u32[]{:S(2)}, u32[]{:S(2)}) collective-permute-start(f32[16,64,256]{2,1,0:T(8,128)S(1)} %multiply_add_fusion.2), channel_id=1, source_target_pairs={{0,16},{16,32},{32,48},{48,64},{64,80},{80,96},{96,112},{112,128},... | collective-permute-start | bytes 3145736 | tf_op jit(solution)/shard_map/while/body/eval_jaxpr/ppermute | solution.py:16
  290.4 27.6 %collective-permute-start = (f32[16,64,256]{2,1,0:T(8,128)S(1)}, f32[16,64,256]{2,1,0:T(8,128)S(1)}, u32[]{:S(2)}, u32[]{:S(2)}) collective-permute-start(f32[16,64,256]{2,1,0:T(8,128)S(1)} %multiply_add_fusion.2), channel_id=1, source_target_pairs={{0,16},{16,32},{32,48},{48,64},{64,80},{80,96},{96,112},{112,128},... | collective-permute-start | bytes 3145736 | tf_op jit(solution)/shard_map/while/body/eval_jaxpr/ppermute | solution.py:16
  318.2 26.8 %collective-permute-start = (f32[16,64,256]{2,1,0:T(8,128)S(1)}, f32[16,64,256]{2,1,0:T(8,128)S(1)}, u32[]{:S(2)}, u32[]{:S(2)}) collective-permute-start(f32[16,64,256]{2,1,0:T(8,128)S(1)} %multiply_add_fusion.2), channel_id=1, source_target_pairs={{0,16},{16,32},{32,48},{48,64},{64,80},{80,96},{96,112},{112,128},... | collective-permute-start | bytes 3145736 | tf_op jit(solution)/shard_map/while/body/eval_jaxpr/ppermute | solution.py:16
  345.1 25.9 %collective-permute-start = (f32[16,64,256]{2,1,0:T(8,128)S(1)}, f32[16,64,256]{2,1,0:T(8,128)S(1)}, u32[]{:S(2)}, u32[]{:S(2)}) collective-permute-start(f32[16,64,256]{2,1,0:T(8,128)S(1)} %multiply_add_fusion.2), channel_id=1, source_target_pairs={{0,16},{16,32},{32,48},{48,64},{64,80},{80,96},{96,112},{112,128},... | collective-permute-start | bytes 3145736 | tf_op jit(solution)/shard_map/while/body/eval_jaxpr/ppermute | solution.py:16
  371.2 25.1 %collective-permute-start = (f32[16,64,256]{2,1,0:T(8,128)S(1)}, f32[16,64,256]{2,1,0:T(8,128)S(1)}, u32[]{:S(2)}, u32[]{:S(2)}) collective-permute-start(f32[16,64,256]{2,1,0:T(8,128)S(1)} %multiply_add_fusion.2), channel_id=1, source_target_pairs={{0,16},{16,32},{32,48},{48,64},{64,80},{80,96},{96,112},{112,128},... | collective-permute-start | bytes 3145736 | tf_op jit(solution)/shard_map/while/body/eval_jaxpr/ppermute | solution.py:16
  396.5 24.2 %collective-permute-start = (f32[16,64,256]{2,1,0:T(8,128)S(1)}, f32[16,64,256]{2,1,0:T(8,128)S(1)}, u32[]{:S(2)}, u32[]{:S(2)}) collective-permute-start(f32[16,64,256]{2,1,0:T(8,128)S(1)} %multiply_add_fusion.2), channel_id=1, source_target_pairs={{0,16},{16,32},{32,48},{48,64},{64,80},{80,96},{96,112},{112,128},... | collective-permute-start | bytes 3145736 | tf_op jit(solution)/shard_map/while/body/eval_jaxpr/ppermute | solution.py:16
  420.9 23.4 %collective-permute-start = (f32[16,64,256]{2,1,0:T(8,128)S(1)}, f32[16,64,256]{2,1,0:T(8,128)S(1)}, u32[]{:S(2)}, u32[]{:S(2)}) collective-permute-start(f32[16,64,256]{2,1,0:T(8,128)S(1)} %multiply_add_fusion.2), channel_id=1, source_target_pairs={{0,16},{16,32},{32,48},{48,64},{64,80},{80,96},{96,112},{112,128},... | collective-permute-start | bytes 3145736 | tf_op jit(solution)/shard_map/while/body/eval_jaxpr/ppermute | solution.py:16
  444.4 23.2 %collective-permute-start = (f32[16,64,256]{2,1,0:T(8,128)S(1)}, f32[16,64,256]{2,1,0:T(8,128)S(1)}, u32[]{:S(2)}, u32[]{:S(2)}) collective-permute-start(f32[16,64,256]{2,1,0:T(8,128)S(1)} %multiply_add_fusion.2), channel_id=1, source_target_pairs={{0,16},{16,32},{32,48},{48,64},{64,80},{80,96},{96,112},{112,128},... | collective-permute-start | bytes 3145736 | tf_op jit(solution)/shard_map/while/body/eval_jaxpr/ppermute | solution.py:16
  467.7 23.2 %collective-permute-start = (f32[16,64,256]{2,1,0:T(8,128)S(1)}, f32[16,64,256]{2,1,0:T(8,128)S(1)}, u32[]{:S(2)}, u32[]{:S(2)}) collective-permute-start(f32[16,64,256]{2,1,0:T(8,128)S(1)} %multiply_add_fusion.2), channel_id=1, source_target_pairs={{0,16},{16,32},{32,48},{48,64},{64,80},{80,96},{96,112},{112,128},... | collective-permute-start | bytes 3145736 | tf_op jit(solution)/shard_map/while/body/eval_jaxpr/ppermute | solution.py:16
  491.0 23.2 %collective-permute-start = (f32[16,64,256]{2,1,0:T(8,128)S(1)}, f32[16,64,256]{2,1,0:T(8,128)S(1)}, u32[]{:S(2)}, u32[]{:S(2)}) collective-permute-start(f32[16,64,256]{2,1,0:T(8,128)S(1)} %multiply_add_fusion.2), channel_id=1, source_target_pairs={{0,16},{16,32},{32,48},{48,64},{64,80},{80,96},{96,112},{112,128},... | collective-permute-start | bytes 3145736 | tf_op jit(solution)/shard_map/while/body/eval_jaxpr/ppermute | solution.py:16
  514.4 23.2 %collective-permute-start = (f32[16,64,256]{2,1,0:T(8,128)S(1)}, f32[16,64,256]{2,1,0:T(8,128)S(1)}, u32[]{:S(2)}, u32[]{:S(2)}) collective-permute-start(f32[16,64,256]{2,1,0:T(8,128)S(1)} %multiply_add_fusion.2), channel_id=1, source_target_pairs={{0,16},{16,32},{32,48},{48,64},{64,80},{80,96},{96,112},{112,128},... | collective-permute-start | bytes 3145736 | tf_op jit(solution)/shard_map/while/body/eval_jaxpr/ppermute | solution.py:16
  537.7 23.2 %collective-permute-start = (f32[16,64,256]{2,1,0:T(8,128)S(1)}, f32[16,64,256]{2,1,0:T(8,128)S(1)}, u32[]{:S(2)}, u32[]{:S(2)}) collective-permute-start(f32[16,64,256]{2,1,0:T(8,128)S(1)} %multiply_add_fusion.2), channel_id=1, source_target_pairs={{0,16},{16,32},{32,48},{48,64},{64,80},{80,96},{96,112},{112,128},... | collective-permute-start | bytes 3145736 | tf_op jit(solution)/shard_map/while/body/eval_jaxpr/ppermute | solution.py:16
  561.0 24.0 %collective-permute-start = (f32[16,64,256]{2,1,0:T(8,128)S(1)}, f32[16,64,256]{2,1,0:T(8,128)S(1)}, u32[]{:S(2)}, u32[]{:S(2)}) collective-permute-start(f32[16,64,256]{2,1,0:T(8,128)S(1)} %multiply_add_fusion.2), channel_id=1, source_target_pairs={{0,16},{16,32},{32,48},{48,64},{64,80},{80,96},{96,112},{112,128},... | collective-permute-start | bytes 3145736 | tf_op jit(solution)/shard_map/while/body/eval_jaxpr/ppermute | solution.py:16
  585.2 18.8 %collective-permute-start = (f32[16,64,256]{2,1,0:T(8,128)S(1)}, f32[16,64,256]{2,1,0:T(8,128)S(1)}, u32[]{:S(2)}, u32[]{:S(2)}) collective-permute-start(f32[16,64,256]{2,1,0:T(8,128)S(1)} %multiply_add_fusion.2), channel_id=1, source_target_pairs={{0,16},{16,32},{32,48},{48,64},{64,80},{80,96},{96,112},{112,128},... | collective-permute-start | bytes 3145736 | tf_op jit(solution)/shard_map/while/body/eval_jaxpr/ppermute | solution.py:16
  604.0 8.3 %copy-start.2 = (f32[8,256,16]{1,2,0:T(8,128)S(1)}, f32[8,256,16]{1,2,0:T(8,128)}, u32[]{:S(2)}) copy-start(f32[8,256,16]{1,2,0:T(8,128)} %copy.78) | copy-start | bytes 393220
  604.0 8.3 %copy-start.3 = (f32[16]{0:T(128)S(1)}, f32[16]{0:T(128)}, u32[]{:S(2)}) copy-start(f32[16]{0:T(128)} %dynamic_slice.29) | copy-start | bytes 196
  (1 other events, 8.3 us)
where the time goes:
time: 763 us; the launch traced here: 759 us
  waiting for transfers between devices  454 us (60%)
  blocking collectives  111 us (15%)
  starting transfers between devices  64 us (8%)
  local copies, waits for them, and re-layouts  53.6 us (7%)
  other arithmetic  46.6 us (6%)
  matrix products  28.9 us (4%)
    ppermute x15, waiting for transfers between devices, from_behind(): return lax.ppermute(array, axis, pairs)  373 us
    all_to_all x1, blocking collectives, finish(): lax.all_to_all(result, 'head', split_axis=0, concat_axis=1, tiled=True)  111 us
    all_to_all x1, waiting for transfers between devices, shards(): lax.all_to_all(signal, 'head', split_axis=1, concat_axis=0, tiled=True)  36.3 us
    ppermute x15, starting transfers between devices, from_behind(): return lax.ppermute(array, axis, pairs)  30.4 us
    all_to_all x1, waiting for transfers between devices, shards(): lax.all_to_all(input_rep, 'head', split_axis=1, concat_axis=0, tiled=True)  21.8 us
    dynamic_update_slice x8, other arithmetic, prepare(): lax.map(block_weights, (cumul, step_rate, input_groups, output_groups))  18 us
    all_to_all x3, local copies, waits for them, and re-layouts, finish(): lax.all_to_all(result, 'head', split_axis=0, concat_axis=1, tiled=True)  16.7 us
  transfers between devices with their start and end apart: 19, of which 19 were waited for; matrix products, arithmetic and copies ran while one was open for 5% of the time, Pallas kernels for 0%

commit v1 on v0

--- a/solution.py
+++ b/solution.py
@@ -67,12 +67,23 @@
     before = jnp.cumsum(block_ends, axis=0) - block_ends
     totals = jnp.sum(block_ends, axis=0)
     chain_len = lax.axis_size("chain")
-
-    def relay_turn(turn_index, arriving):
-        leaving = jnp.exp(totals)[:, None, None] * arriving + final_state
-        return from_behind(leaving, "chain", 1)
-
-    incoming_state = lax.fori_loop(0, chain_len - 1, relay_turn, jnp.zeros_like(final_state))
+    own_decay = jnp.exp(totals)
+    got_decay = from_behind(own_decay, "chain", 1)
+    got_state = from_behind(final_state, "chain", 1)
+    span_decay = got_decay * own_decay
+    span_state = own_decay[:, None, None] * got_state + final_state
+    incoming_state = got_state
+    incoming_decay = got_decay
+    shift = 2
+    while shift < chain_len:
+        got_decay = from_behind(span_decay, "chain", shift)
+        got_state = from_behind(span_state, "chain", shift)
+        incoming_state = incoming_decay[:, None, None] * got_state + incoming_state
+        incoming_decay = incoming_decay * got_decay
+        if 2 * shift < chain_len:
+            span_state = span_decay[:, None, None] * got_state + span_state
+            span_decay = span_decay * got_decay
+        shift *= 2
     starts = starts + jnp.exp(before)[:, :, None, None] * incoming_state
     rounded = starts.astype(jnp.bfloat16).reshape(
         blocks, group_count, per_group, CHANNEL_WIDTH, SSTATE

time: 763 us -> 494 us (0.65)
  waiting for transfers between devices: 454 us -> 179 us
  starting transfers between devices: 64 us -> 72.8 us
    ppermute x15 -> x7, waiting for transfers between devices: 373 us -> 110 us  [from_behind(): return lax.ppermute(array, axis, pairs)]
    all_to_all x1, starting transfers between devices: 3.66 us -> 35.4 us  [shards(): lax.all_to_all(input_rep, 'head', split_axis=1, concat_axis=0, tiled=True)]
    all_to_all x1, waiting for transfers between devices: 36.3 us -> 65.5 us  [shards(): lax.all_to_all(signal, 'head', split_axis=1, concat_axis=0, tiled=True)]
    all_to_all x1, waiting for transfers between devices: 21.8 us -> 0.01 us  [shards(): lax.all_to_all(input_rep, 'head', split_axis=1, concat_axis=0, tiled=True)]
    ppermute x15 -> x7, starting transfers between devices: 30.4 us -> 13.3 us  [from_behind(): return lax.ppermute(array, axis, pairs)]
    all_to_all x1, waiting for transfers between devices: 14.2 us -> 0.01 us  [shards(): lax.all_to_all(output_rep, 'head', split_axis=1, concat_axis=0, tiled=True)]
  transfers between devices with their start and end apart: 19 -> 11, of which waited for: 19 -> 8; matrix products, arithmetic and copies ran while one was open for 5% -> 13% of each run, Pallas kernels for 0% -> 0%
where the time goes in v1:
time: 494 us; the launch traced here: 492 us
  waiting for transfers between devices  179 us (36%)
  blocking collectives  105 us (21%)
  starting transfers between devices  72.8 us (15%)
  other arithmetic  52.7 us (11%)
  local copies, waits for them, and re-layouts  51.9 us (11%)
  matrix products  30 us (6%)
    ppermute x7, waiting for transfers between devices, from_behind(): return lax.ppermute(array, axis, pairs)  110 us
    all_to_all x1, blocking collectives, finish(): lax.all_to_all(result, 'head', split_axis=0, concat_axis=1, tiled=True)  105 us
    all_to_all x1, waiting for transfers between devices, shards(): lax.all_to_all(signal, 'head', split_axis=1, concat_axis=0, tiled=True)  65.5 us
    all_to_all x1, starting transfers between devices, shards(): lax.all_to_all(input_rep, 'head', split_axis=1, concat_axis=0, tiled=True)  35.4 us
    dynamic_update_slice x8, other arithmetic, prepare(): lax.map(block_weights, (cumul, step_rate, input_groups, output_groups))  18.3 us
    all_to_all x3, local copies, waits for them, and re-layouts, finish(): lax.all_to_all(result, 'head', split_axis=0, concat_axis=1, tiled=True)  16.7 us
    ppermute x7, starting transfers between devices, from_behind(): return lax.ppermute(array, axis, pairs)  13.3 us
    dot_general x1, matrix products, finish(): jnp.einsum('khts,kshp->kthp', weights, values, preferred_element_type=jnp...  11.5 us
  transfers between devices with their start and end apart: 11, of which 8 were waited for; matrix products, arithmetic and copies ran while one was open for 13% of the time, Pallas kernels for 0%

profile of v1, /device:TPU:96, one launch (start us, length us, event | category | flops | bytes accessed | tf_op | source)
XLA Modules:
  0.0 492.1 jit_solution(16696309757755112549)
XLA Ops:
  1.6 8.3 %all-to-all-start = ((bf16[128,16,16]{0,2,1:T(8,128)(2,1)}), bf16[128,16,16]{0,2,1:T(8,128)(2,1)S(1)}, u32[]{:S(2)}, u32[]{:S(2)}) async-start(bf16[128,16,16]{0,2,1:T(8,128)(2,1)} %bitcast), calls=%async_computation | async-start | bytes 131072 | tf_op jit(solution)/shard_map/all_to_all | solution.py:119
  9.9 6.4 %copy.71 = bf16[128,16384]{0,1:T(8,128)(2,1)} copy(bf16[128,16384]{1,0:T(8,128)(2,1)} %param.10) | data formatting | bytes 8388608 | tf_op args[0]
  16.3 3.6 all-to-all-done
  20.0 6.2 %all-to-all-start.3 = ((bf16[128,16,1024]{0,2,1:T(8,128)(2,1)}), bf16[128,16,1024]{0,2,1:T(8,128)(2,1)}, u32[]{:S(2)}, u32[]{:S(2)}) async-start(bf16[128,16,1024]{0,2,1:T(8,128)(2,1)} %bitcast.114), calls=%async_computation.3 | async-start | bytes 8388608 | tf_op jit(solution)/shard_map/all_to_all | solution.py:116
  26.2 65.5 %all-to-all-done.3 = bf16[128,16,1024]{0,2,1:T(8,128)(2,1)} async-done(((bf16[128,16,1024]{0,2,1:T(8,128)(2,1)}), bf16[128,16,1024]{0,2,1:T(8,128)(2,1)}, u32[]{:S(2)}, u32[]{:S(2)}) %all-to-all-start.3) | async-done | bytes 4194336 | tf_op jit(solution)/shard_map/all_to_all | solution.py:116
  92.9 35.4 %all-to-all-start.2 = ((bf16[128,16,256]{2,0,1:T(8,128)(2,1)}), bf16[128,16,256]{2,0,1:T(8,128)(2,1)S(1)}, u32[]{:S(2)}, u32[]{:S(2)}) async-start(bf16[128,16,256]{2,0,1:T(8,128)(2,1)} %bitcast.10), calls=%async_computation.2 | async-start | bytes 2097152 | tf_op jit(solution)/shard_map/all_to_all | solution.py:117
  128.7 4.6 reduce-window.6
  135.2 6.9 %copy.72 = bf16[16,128,1024]{1,0,2:T(8,128)(2,1)} copy(bf16[16,128,1024]{1,2,0:T(8,128)(2,1)} %bitcast.15) | data formatting | bytes 8388608 | tf_op jit(solution)/shard_map/all_to_all | solution.py:116
  142.1 7.1 %reshape.174 = bf16[8,256,16,64]{1,0,3,2:T(8,128)(2,1)} reshape(bf16[16,128,1024]{1,0,2:T(8,128)(2,1)} %copy.72) | data formatting | bytes 8388608 | tf_op jit(solution)/shard_map/reshape | solution.py:49
  149.2 6.7 %fusion.16 = f32[8,16,64,256]{3,2,1,0:T(8,128)} fusion(bf16[8,256,256,1]{2,1,3,0:T(8,128)(2,1)S(1)} %bitcast.116, f32[8,256,16]{1,2,0:T(8,128)S(1)} %copy.76, bf16[8,256,16,64]{1,0,3,2:T(8,128)(2,1)} %reshape.174), kind=kOutput, calls=%fused_computation.28 | convolution fusion | flops 1080033280 | bytes 13762560 | tf_op jit(solution)/shard_map/ksgjp,ksgn->kgjpn/dot_general | solution.py:55
  155.9 20.4 %while.26 = (s32[]{:T(128)}, f32[16,64,256]{2,1,0:T(8,128)S(1)}, f32[8,16,64,256]{3,2,1,0:T(8,128)}, f32[8,16]{1,0:T(8,128)S(1)}, f32[8,16,64,256]{3,2,1,0:T(8,128)}, /*index=5*/s32[]{:T(128)}, s32[]{:T(128)}) while((s32[]{:T(128)}, f32[16,64,256]{2,1,0:T(8,128)S(1)}, f32[8,16,64,256]{3,2,1,0:T(8,128)}, f32[8,16]{1,0:T(8,128)S(1)}, ...), condition=%wide.region_5.6_spmd.clone, body=%wide.region_4.5_spmd.clone.sunk | while | flops 1048579 | bytes 5243180 | solution.py:66
  181.0 9.6 %all-to-all-start.1 = ((bf16[128,16,256]{2,0,1:T(8,128)(2,1)}), bf16[128,16,256]{2,0,1:T(8,128)(2,1)S(1)}, u32[]{:S(2)}, u32[]{:S(2)}) async-start(bf16[128,16,256]{2,0,1:T(8,128)(2,1)} %bitcast.120), calls=%async_computation.1 | async-start | bytes 2097152 | tf_op jit(solution)/shard_map/all_to_all | solution.py:118
  190.6 24.7 %collective-permute-done.3 = f32[16,64,256]{2,1,0:T(8,128)} collective-permute-done((f32[16,64,256]{2,1,0:T(8,128)S(1)}, f32[16,64,256]{2,1,0:T(8,128)}, u32[]{:S(2)}, u32[]{:S(2)}) %collective-permute-start.3) | collective-permute-done | bytes 1048608 | tf_op jit(solution)/shard_map/ppermute | solution.py:16
  222.3 37.6 %collective-permute-done = f32[16]{0:T(128)S(1)} collective-permute-done((f32[16]{0:T(128)S(1)}, f32[16]{0:T(128)S(1)}, u32[]{:S(2)}, u32[]{:S(2)}) %collective-permute-start) | collective-permute-done | bytes 96 | tf_op jit(solution)/shard_map/ppermute | solution.py:16
  261.8 5.9 %collective-permute-done.1 = f32[16]{0:T(128)S(1)} collective-permute-done((f32[16]{0:T(128)S(1)}, f32[16]{0:T(128)S(1)}, u32[]{:S(2)}, u32[]{:S(2)}) %collective-permute-start.1) | collective-permute-done | bytes 96 | tf_op jit(solution)/shard_map/ppermute | solution.py:16
  270.0 4.8 collective-permute-done.2
  277.8 20.9 %while.25 = (s32[]{:T(128)}, bf16[8,16,256,256]{3,2,1,0:T(8,128)(2,1)}, f32[8,256,16]{1,0,2:T(8,128)S(1)}, bf16[8,256,1,256]{3,1,2,0:T(8,128)(2,1)S(1)}, bf16[8,...) while((s32[]{:T(128)}, ...), condition=%wide.region_3.4_spmd.clone.clone, body=%wide.region_2.3_spmd.clone.clone.sunk | while | flops 39911424 | bytes 3195997 | solution.py:41
  304.2 11.5 %fusion.22 = f32[8,16,256,64]{2,3,1,0:T(8,128)} fusion(bf16[8,16,256,256]{3,2,1,0:T(8,128)(2,1)} %get-tuple-element.73, bf16[8,256,16,64]{1,0,3,2:T(8,128)(2,1)} %reshape.174), kind=kOutput, calls=%fused_computation.33 | convolution fusion | flops 1073741824 | bytes 29360128 | tf_op jit(solution)/shard_map/khts,kshp->kthp/dot_general | solution.py:51
  315.6 34.2 %collective-permute-done.6 = f32[16,64,256]{2,1,0:T(8,128)S(1)} collective-permute-done((f32[16,64,256]{2,1,0:T(8,128)S(1)}, f32[16,64,256]{2,1,0:T(8,128)S(1)}, u32[]{:S(2)}, u32[]{:S(2)}) %collective-permute-start.6) | collective-permute-done | bytes 1048608 | tf_op jit(solution)/shard_map/ppermute | solution.py:16
  353.4 10.1 %fusion.13 = bf16[8,256,16,64]{1,3,2,0:T(8,128)(2,1)} fusion(f32[8,16,256,64]{2,3,1,0:T(8,128)} %fusion.22, f32[16]{0:T(128)S(1)} %copy-done.3, f32[8,256,16]{1,2,0:T(8,128)S(1)} %copy.78, bf16[8,256,16,64]{1,0,3,2:T(8,128)(2,1)} %reshape.174, bf16[8,256,256,1]{2,1,3,0:T(8,128)(2,1)S(1)} %bitcast.119, f32[8,16,64,256]{3,2,1,0:T(8,128)} %get-tuple-element.74, ...), kind=kOutput, calls=%fused_computation.23 | convolution fusion | flops 1092616192 | bytes 27394624 | tf_op jit(solution)/shard_map/ktgn,kgjpn->ktgjp/dot_general | solution.py:91
  363.5 7.0 %copy.79 = bf16[8,256,16,64]{1,0,3,2:T(8,128)(2,1)} copy(bf16[8,256,16,64]{1,3,2,0:T(8,128)(2,1)} %fusion.13) | data formatting | bytes 8388608 | tf_op jit(solution)/shard_map/convert_element_type | solution.py:97
  370.5 7.1 %all_to_all.71 = bf16[16,128,1024]{1,0,2:T(8,128)(2,1)} reshape(bf16[8,256,16,64]{1,0,3,2:T(8,128)(2,1)} %copy.79) | data formatting | bytes 8388608 | tf_op jit(solution)/shard_map/all_to_all | solution.py:99
  380.8 104.8 %all_to_all.80 = bf16[16,128,1024]{1,2,0:T(8,128)(2,1)} all-to-all(bf16[16,128,1024]{1,2,0:T(8,128)(2,1)S(1)} %copy.80), channel_id=1, replica_groups=mesh['chain'=16,'head'=16] {'head'}, dimensions={0} | all-to-all | bytes 8388608 | tf_op jit(solution)/shard_map/all_to_all | solution.py:99
  485.7 6.4 %copy.81 = bf16[128,16384]{1,0:T(8,128)(2,1)} copy(bf16[128,16384]{0,1:T(8,128)(2,1)} %bitcast.115) | data formatting | bytes 8388608 | tf_op jit(solution)/shard_map/all_to_all | solution.py:99
  (137 shorter events, 76.8 us)
Async XLA Ops:
  1.6 18.4 %all-to-all-start = ((bf16[128,16,16]{0,2,1:T(8,128)(2,1)}), bf16[128,16,16]{0,2,1:T(8,128)(2,1)S(1)}, u32[]{:S(2)}, u32[]{:S(2)}) async-start(bf16[128,16,16]{0,2,1:T(8,128)(2,1)} %bitcast), calls=%async_computation | async-start | bytes 131072 | tf_op jit(solution)/shard_map/all_to_all | solution.py:119
  9.9 16.2 %copy-start.1 = (bf16[128,2048]{1,0:T(8,128)(2,1)S(1)}, bf16[128,2048]{1,0:T(8,128)(2,1)}, u32[]{:S(2)}) copy-start(bf16[128,2048]{1,0:T(8,128)(2,1)} %param.11) | copy-start | bytes 1572868
  16.3 112.0 %copy-start.5 = (f32[256]{0:T(256)S(1)}, f32[256]{0:T(256)}, u32[]{:S(2)}) copy-start(f32[256]{0:T(256)} %param.14) | copy-start | bytes 3076
  20.0 71.7 %all-to-all-start.3 = ((bf16[128,16,1024]{0,2,1:T(8,128)(2,1)}), bf16[128,16,1024]{0,2,1:T(8,128)(2,1)}, u32[]{:S(2)}, u32[]{:S(2)}) async-start(bf16[128,16,1024]{0,2,1:T(8,128)(2,1)} %bitcast.114), calls=%async_computation.3 | async-start | bytes 8388608 | tf_op jit(solution)/shard_map/all_to_all | solution.py:116
  92.9 56.4 %all-to-all-start.2 = ((bf16[128,16,256]{2,0,1:T(8,128)(2,1)}), bf16[128,16,256]{2,0,1:T(8,128)(2,1)S(1)}, u32[]{:S(2)}, u32[]{:S(2)}) async-start(bf16[128,16,256]{2,0,1:T(8,128)(2,1)} %bitcast.10), calls=%async_computation.2 | async-start | bytes 2097152 | tf_op jit(solution)/shard_map/all_to_all | solution.py:117
  155.9 23.9 %copy-start.2 = (bf16[128,2048]{1,0:T(8,128)(2,1)S(1)}, bf16[128,2048]{1,0:T(8,128)(2,1)}, u32[]{:S(2)}) copy-start(bf16[128,2048]{1,0:T(8,128)(2,1)} %param.12) | copy-start | bytes 1572868
  155.9 63.7 %copy-start.6 = (f32[256]{0:T(256)S(1)}, f32[256]{0:T(256)}, u32[]{:S(2)}) copy-start(f32[256]{0:T(256)} %param.15) | copy-start | bytes 3076
  176.3 38.9 %collective-permute-start.3 = (f32[16,64,256]{2,1,0:T(8,128)S(1)}, f32[16,64,256]{2,1,0:T(8,128)}, u32[]{:S(2)}, u32[]{:S(2)}) collective-permute-start(f32[16,64,256]{2,1,0:T(8,128)S(1)} %get-tuple-element.75), channel_id=1, source_target_pairs={{0,16},{16,32},{32,48},{48,64},{64,80},{80,96},{96,112},{112,128},... | collective-permute-start | bytes 3145736 | tf_op jit(solution)/shard_map/ppermute | solution.py:16
  181.0 96.8 %all-to-all-start.1 = ((bf16[128,16,256]{2,0,1:T(8,128)(2,1)}), bf16[128,16,256]{2,0,1:T(8,128)(2,1)S(1)}, u32[]{:S(2)}, u32[]{:S(2)}) async-start(bf16[128,16,256]{2,0,1:T(8,128)(2,1)} %bitcast.120), calls=%async_computation.1 | async-start | bytes 2097152 | tf_op jit(solution)/shard_map/all_to_all | solution.py:118
  217.7 57.1 %collective-permute-start.4 = (f32[16,64,256]{2,1,0:T(8,128)}, f32[16,64,256]{2,1,0:T(8,128)}, u32[]{:S(2)}, u32[]{:S(2)}) collective-permute-start(f32[16,64,256]{2,1,0:T(8,128)} %multiply_add_fusion.2), channel_id=1, source_target_pairs={{0,32},{16,48},{32,64},{48,80},{64,96},{80,112},{96,128},{112,144}... | collective-permute-start | bytes 3145736 | tf_op jit(solution)/shard_map/ppermute | solution.py:16
  220.3 39.5 %collective-permute-start = (f32[16]{0:T(128)S(1)}, f32[16]{0:T(128)S(1)}, u32[]{:S(2)}, u32[]{:S(2)}) collective-permute-start(f32[16]{0:T(128)S(1)} %exp.43), channel_id=1, source_target_pairs={{0,16},{16,32},{32,48},{48,64},{64,80},{80,96},{96,112},{112,128},... | collective-permute-start | bytes 200 | tf_op jit(solution)/shard_map/ppermute | solution.py:16
  259.8 7.9 %collective-permute-start.1 = (f32[16]{0:T(128)S(1)}, f32[16]{0:T(128)S(1)}, u32[]{:S(2)}, u32[]{:S(2)}) collective-permute-start(f32[16]{0:T(128)S(1)} %exponential_multiply_fusion.1), channel_id=1, source_target_pairs={{0,32},{16,48},{32,64},{48,80},{64,96},{80,112},{96,128},{112,144}... | collective-permute-start | bytes 200 | tf_op jit(solution)/shard_map/ppermute | solution.py:16
  267.7 7.1 %copy-start.4 = (f32[16]{0:T(128)}, f32[16]{0:T(128)S(1)}, u32[]{:S(2)}) copy-start(f32[16]{0:T(128)S(1)} %mul.163) | copy-start | bytes 196
  267.7 7.1 %collective-permute-start.2 = (f32[16]{0:T(128)S(1)}, f32[16]{0:T(128)S(1)}, u32[]{:S(2)}, u32[]{:S(2)}) collective-permute-start(f32[16]{0:T(128)S(1)} %mul.163), channel_id=1, source_target_pairs={{0,64},{16,80},{32,96},{48,112},{64,128},{80,144},{96,160},{112,17... | collective-permute-start | bytes 200 | tf_op jit(solution)/shard_map/ppermute | solution.py:16
  276.5 24.8 %collective-permute-start.5 = (f32[16,64,256]{2,1,0:T(8,128)S(1)}, f32[16,64,256]{2,1,0:T(8,128)}, u32[]{:S(2)}, u32[]{:S(2)}) collective-permute-start(f32[16,64,256]{2,1,0:T(8,128)S(1)} %multiply_add_fusion.1), channel_id=1, source_target_pairs={{0,64},{16,80},{32,96},{48,112},{64,128},{80,144},{96,160},{112,17... | collective-permute-start | bytes 3145736 | tf_op jit(solution)/shard_map/ppermute | solution.py:16
  302.7 47.2 %collective-permute-start.6 = (f32[16,64,256]{2,1,0:T(8,128)S(1)}, f32[16,64,256]{2,1,0:T(8,128)S(1)}, u32[]{:S(2)}, u32[]{:S(2)}) collective-permute-start(f32[16,64,256]{2,1,0:T(8,128)S(1)} %multiply_add_fusion), channel_id=1, source_target_pairs={{0,128},{16,144},{32,160},{48,176},{64,192},{80,208},{96,224},{112... | collective-permute-start | bytes 3145736 | tf_op jit(solution)/shard_map/ppermute | solution.py:16
  304.1 49.2 %copy-start.3 = (f32[16]{0:T(128)S(1)}, f32[16]{0:T(128)}, u32[]{:S(2)}) copy-start(f32[16]{0:T(128)} %dynamic_slice.29) | copy-start | bytes 196
  349.8 1.0 copy-start

commit v2 on v1

--- a/solution.py
+++ b/solution.py
@@ -67,22 +67,25 @@
     before = jnp.cumsum(block_ends, axis=0) - block_ends
     totals = jnp.sum(block_ends, axis=0)
     chain_len = lax.axis_size("chain")
-    own_decay = jnp.exp(totals)
-    got_decay = from_behind(own_decay, "chain", 1)
+    chain_pos = lax.axis_index("chain")
+    shard_totals = lax.all_gather(totals, "chain")
+    order = jnp.arange(chain_len)
+
+    def span_decay(first, last):
+        inside = (order >= first) & (order <= last)
+        return jnp.exp(jnp.sum(jnp.where(inside[:, None], shard_totals, 0.0), axis=0))
+
     got_state = from_behind(final_state, "chain", 1)
-    span_decay = got_decay * own_decay
-    span_state = own_decay[:, None, None] * got_state + final_state
+    span_state = jnp.exp(totals)[:, None, None] * got_state + final_state
     incoming_state = got_state
-    incoming_decay = got_decay
     shift = 2
     while shift < chain_len:
-        got_decay = from_behind(span_decay, "chain", shift)
         got_state = from_behind(span_state, "chain", shift)
+        incoming_decay = span_decay(chain_pos - shift + 1, chain_pos - 1)
         incoming_state = incoming_decay[:, None, None] * got_state + incoming_state
-        incoming_decay = incoming_decay * got_decay
         if 2 * shift < chain_len:
-            span_state = span_decay[:, None, None] * got_state + span_state
-            span_decay = span_decay * got_decay
+            own_decay = span_decay(chain_pos - shift + 1, chain_pos)
+            span_state = own_decay[:, None, None] * got_state + span_state
         shift *= 2
     starts = starts + jnp.exp(before)[:, :, None, None] * incoming_state
     rounded = starts.astype(jnp.bfloat16).reshape(
@@ -95,8 +98,10 @@
     head_start = lax.axis_index("head") * local_heads
     gain_heads = lax.dynamic_slice_in_dim(skip_gain, head_start, local_heads)
     result = (within + carried + gain_heads[:, None] * values_wide).astype(jnp.bfloat16)
-    result = result.reshape(blocks * BLOCK, local_heads * CHANNEL_WIDTH)
-    return lax.all_to_all(result, "head", split_axis=0, concat_axis=1, tiled=True)
+    head_count = lax.axis_size("head")
+    result = result.reshape(head_count, -1, local_heads * CHANNEL_WIDTH).transpose(1, 0, 2)
+    result = lax.all_to_all(result, "head", split_axis=1, concat_axis=1, tiled=True)
+    return result.reshape(result.shape[0], -1)
 
 
 def shards(signal, input_map, output_map, step_size, decay_rate, skip_gain):

time: 494 us -> 500 us (1.012)
  blocking collectives: 105 us -> 166 us
  waiting for transfers between devices: 179 us -> 127 us
  starting transfers between devices: 72.8 us -> 67.7 us
    unnamed x0 -> x1, blocking collectives: none -> 61.1 us
    ppermute x7 -> x4, waiting for transfers between devices: 110 us -> 58.1 us  [from_behind(): return lax.ppermute(array, axis, pairs)]
    all_to_all x3 -> x0, local copies, waits for them, and re-layouts: 16.7 us -> none  [finish(): lax.all_to_all(result, 'head', split_axis=0, concat_axis=1, tiled=True)]
    reshape x1 -> x3, local copies, waits for them, and re-layouts: 0.05 us -> 13.5 us  [the longest x1 7.07 us: finish(): result.reshape(head_count, -1, local_heads * CHANNEL_WIDTH)]
    ppermute x7 -> x4, starting transfers between devices: 13.3 us -> 8.16 us  [from_behind(): return lax.ppermute(array, axis, pairs)]
  transfers between devices with their start and end apart: 11 -> 8, of which waited for: 8 -> 5; matrix products, arithmetic and copies ran while one was open for 13% -> 14% of each run, Pallas kernels for 0% -> 0%
where the time goes in v2:
time: 500 us; the launch traced here: 498 us
  blocking collectives  166 us (33%)
  waiting for transfers between devices  127 us (25%)
  starting transfers between devices  67.7 us (14%)
  local copies, waits for them, and re-layouts  52.8 us (11%)
  other arithmetic  52.4 us (10%)
  matrix products  30 us (6%)
    all_to_all x1, blocking collectives, finish(): lax.all_to_all(result, 'head', split_axis=1, concat_axis=1, tiled=True)  105 us
    all_to_all x1, waiting for transfers between devices, shards(): lax.all_to_all(signal, 'head', split_axis=1, concat_axis=0, tiled=True)  65.5 us
    unnamed x1, blocking collectives  61.1 us
    ppermute x4, waiting for transfers between devices, from_behind(): return lax.ppermute(array, axis, pairs)  58.1 us
    all_to_all x1, starting transfers between devices, shards(): lax.all_to_all(input_rep, 'head', split_axis=1, concat_axis=0, tiled=True)  35.4 us
    dynamic_update_slice x8, other arithmetic, prepare(): lax.map(block_weights, (cumul, step_rate, input_groups, output_groups))  18 us
    dot_general x1, matrix products, finish(): jnp.einsum('khts,kshp->kthp', weights, values, preferred_element_type=jnp...  11.5 us
    add x8, other arithmetic, carry_step(): jnp.exp(block_end)[:, None, None] * carry_state + fresh_block  11.4 us
  transfers between devices with their start and end apart: 8, of which 5 were waited for; matrix products, arithmetic and copies ran while one was open for 14% of the time, Pallas kernels for 0%

profile of v2, /device:TPU:96, one launch (start us, length us, event | category | flops | bytes accessed | tf_op | source)
XLA Modules:
  0.0 497.6 jit_solution(11474384148069211668)
XLA Ops:
  1.6 8.3 %all-to-all-start = ((bf16[128,16,16]{0,2,1:T(8,128)(2,1)}), bf16[128,16,16]{0,2,1:T(8,128)(2,1)S(1)}, u32[]{:S(2)}, u32[]{:S(2)}) async-start(bf16[128,16,16]{0,2,1:T(8,128)(2,1)} %bitcast), calls=%async_computation | async-start | bytes 131072 | tf_op jit(solution)/shard_map/all_to_all | solution.py:124
  9.9 6.4 %copy.95 = bf16[128,16384]{0,1:T(8,128)(2,1)} copy(bf16[128,16384]{1,0:T(8,128)(2,1)} %param.10) | data formatting | bytes 8388608 | tf_op args[0]
  16.3 3.6 all-to-all-done
  20.0 6.2 %all-to-all-start.3 = ((bf16[128,16,1024]{0,2,1:T(8,128)(2,1)}), bf16[128,16,1024]{0,2,1:T(8,128)(2,1)}, u32[]{:S(2)}, u32[]{:S(2)}) async-start(bf16[128,16,1024]{0,2,1:T(8,128)(2,1)} %bitcast.114), calls=%async_computation.3 | async-start | bytes 8388608 | tf_op jit(solution)/shard_map/all_to_all | solution.py:121
  26.2 65.5 %all-to-all-done.3 = bf16[128,16,1024]{0,2,1:T(8,128)(2,1)} async-done(((bf16[128,16,1024]{0,2,1:T(8,128)(2,1)}), bf16[128,16,1024]{0,2,1:T(8,128)(2,1)}, u32[]{:S(2)}, u32[]{:S(2)}) %all-to-all-start.3) | async-done | bytes 4194336 | tf_op jit(solution)/shard_map/all_to_all | solution.py:121
  92.8 35.4 %all-to-all-start.2 = ((bf16[128,16,256]{2,0,1:T(8,128)(2,1)}), bf16[128,16,256]{2,0,1:T(8,128)(2,1)S(1)}, u32[]{:S(2)}, u32[]{:S(2)}) async-start(bf16[128,16,256]{2,0,1:T(8,128)(2,1)} %bitcast.10), calls=%async_computation.2 | async-start | bytes 2097152 | tf_op jit(solution)/shard_map/all_to_all | solution.py:122
  128.6 4.6 reduce-window.6
  135.1 6.9 %copy.96 = bf16[16,128,1024]{1,0,2:T(8,128)(2,1)} copy(bf16[16,128,1024]{1,2,0:T(8,128)(2,1)} %bitcast.15) | data formatting | bytes 8388608 | tf_op jit(solution)/shard_map/all_to_all | solution.py:121
  142.0 7.1 %reshape.213 = bf16[8,256,16,64]{1,0,3,2:T(8,128)(2,1)} reshape(bf16[16,128,1024]{1,0,2:T(8,128)(2,1)} %copy.96) | data formatting | bytes 8388608 | tf_op jit(solution)/shard_map/reshape | solution.py:49
  149.2 6.7 %fusion.16 = f32[8,16,64,256]{3,2,1,0:T(8,128)} fusion(bf16[8,256,256,1]{2,1,3,0:T(8,128)(2,1)S(1)} %bitcast.117, f32[8,256,16]{1,2,0:T(8,128)S(1)} %copy.100, bf16[8,256,16,64]{1,0,3,2:T(8,128)(2,1)} %reshape.213), kind=kOutput, calls=%fused_computation.28 | convolution fusion | flops 1080033280 | bytes 13762560 | tf_op jit(solution)/shard_map/ksgjp,ksgn->kgjpn/dot_general | solution.py:55
  155.8 20.4 %while.26 = (s32[]{:T(128)}, f32[16,64,256]{2,1,0:T(8,128)S(1)}, f32[8,16,64,256]{3,2,1,0:T(8,128)}, f32[8,16]{1,0:T(8,128)S(1)}, f32[8,16,64,256]{3,2,1,0:T(8,128)}, /*index=5*/s32[]{:T(128)}, s32[]{:T(128)}) while((s32[]{:T(128)}, f32[16,64,256]{2,1,0:T(8,128)S(1)}, f32[8,16,64,256]{3,2,1,0:T(8,128)}, f32[8,16]{1,0:T(8,128)S(1)}, ...), condition=%wide.region_5.6_spmd.clone, body=%wide.region_4.5_spmd.clone.sunk | while | flops 1048579 | bytes 5243180 | solution.py:66
  176.2 3.5 collective-permute-start
  180.9 9.6 %all-to-all-start.1 = ((bf16[128,16,256]{2,0,1:T(8,128)(2,1)}), bf16[128,16,256]{2,0,1:T(8,128)(2,1)S(1)}, u32[]{:S(2)}, u32[]{:S(2)}) async-start(bf16[128,16,256]{2,0,1:T(8,128)(2,1)} %bitcast.121), calls=%async_computation.1 | async-start | bytes 2097152 | tf_op jit(solution)/shard_map/all_to_all | solution.py:123
  190.5 24.7 %collective-permute-done = f32[16,64,256]{2,1,0:T(8,128)} collective-permute-done((f32[16,64,256]{2,1,0:T(8,128)S(1)}, f32[16,64,256]{2,1,0:T(8,128)}, u32[]{:S(2)}, u32[]{:S(2)}) %collective-permute-start) | collective-permute-done | bytes 1048608 | tf_op jit(solution)/shard_map/ppermute | solution.py:16
  222.1 61.1 %all-reduce = f32[256]{0:T(256)S(1)} all-reduce(f32[256]{0:T(256)S(1)} %dynamic-update-slice), channel_id=2, replica_groups=mesh['chain'=16,'head'=16] {'chain'}, use_global_device_ids=true, to_apply=%add | all-reduce | flops 256 | bytes 2048
  288.1 20.6 %while.25 = (s32[]{:T(128)}, bf16[8,16,256,256]{3,2,1,0:T(8,128)(2,1)}, f32[8,256,16]{1,0,2:T(8,128)S(1)}, bf16[8,256,1,256]{3,1,2,0:T(8,128)(2,1)S(1)}, bf16[8,...) while((s32[]{:T(128)}, ...), condition=%wide.region_3.4_spmd.clone.clone, body=%wide.region_2.3_spmd.clone.clone.sunk | while | flops 39911424 | bytes 3195997 | solution.py:41
  312.5 11.5 %fusion.22 = f32[8,16,256,64]{2,3,1,0:T(8,128)} fusion(bf16[8,16,256,256]{3,2,1,0:T(8,128)(2,1)} %get-tuple-element.73, bf16[8,256,16,64]{1,0,3,2:T(8,128)(2,1)} %reshape.213), kind=kOutput, calls=%fused_computation.33 | convolution fusion | flops 1073741824 | bytes 29360128 | tf_op jit(solution)/shard_map/khts,kshp->kthp/dot_general | solution.py:51
  323.9 32.5 %collective-permute-done.3 = f32[16,64,256]{2,1,0:T(8,128)} collective-permute-done((f32[16,64,256]{2,1,0:T(8,128)S(1)}, f32[16,64,256]{2,1,0:T(8,128)}, u32[]{:S(2)}, u32[]{:S(2)}) %collective-permute-start.3) | collective-permute-done | bytes 1048608 | tf_op jit(solution)/shard_map/ppermute | solution.py:16
  359.0 10.1 %fusion.13 = bf16[8,256,16,64]{1,3,2,0:T(8,128)(2,1)} fusion(f32[8,16,256,64]{2,3,1,0:T(8,128)} %fusion.22, f32[16]{0:T(128)S(1)} %dynamic_slice.29, f32[8,256,16]{1,2,0:T(8,128)S(1)} %copy.102, bf16[8,256,16,64]{1,0,3,2:T(8,128)(2,1)} %reshape.213, bf16[8,256,256,1]{2,1,3,0:T(8,128)(2,1)S(1)} %bitcast.120, f32[8,16,64,256]{3,2,1,0:T(8,128)} %get-tuple-element.74, ...), kind=kOutput, calls=%fused_computation.23 | convolution fusion | flops 1092616192 | bytes 27394624 | tf_op jit(solution)/shard_map/ktgn,kgjpn->ktgjp/dot_general | solution.py:94
  369.1 7.0 %copy.103 = bf16[8,256,16,64]{1,0,3,2:T(8,128)(2,1)} copy(bf16[8,256,16,64]{1,3,2,0:T(8,128)(2,1)} %fusion.13) | data formatting | bytes 8388608 | tf_op jit(solution)/shard_map/convert_element_type | solution.py:100
  376.1 7.1 %reshape.217 = bf16[16,128,1024]{1,0,2:T(8,128)(2,1)} reshape(bf16[8,256,16,64]{1,0,3,2:T(8,128)(2,1)} %copy.103) | data formatting | bytes 8388608 | tf_op jit(solution)/shard_map/reshape | solution.py:102
  383.2 3.3 copy.104
  386.5 104.8 %all_to_all.66 = bf16[128,16,1024]{0,2,1:T(8,128)(2,1)} all-to-all(bf16[128,16,1024]{0,2,1:T(8,128)(2,1)S(1)} %copy.104), channel_id=1, replica_groups=mesh['chain'=16,'head'=16] {'head'}, dimensions={1} | all-to-all | bytes 8388608 | tf_op jit(solution)/shard_map/all_to_all | solution.py:103
  491.3 6.4 %copy.105 = bf16[128,16384]{1,0:T(8,128)(2,1)} copy(bf16[128,16384]{0,1:T(8,128)(2,1)} %bitcast.116) | data formatting | bytes 8388608 | tf_op jit(solution)/shard_map/reshape | solution.py:104
  (144 shorter events, 63.9 us)
Async XLA Ops:
  1.6 18.4 %all-to-all-start = ((bf16[128,16,16]{0,2,1:T(8,128)(2,1)}), bf16[128,16,16]{0,2,1:T(8,128)(2,1)S(1)}, u32[]{:S(2)}, u32[]{:S(2)}) async-start(bf16[128,16,16]{0,2,1:T(8,128)(2,1)} %bitcast), calls=%async_computation | async-start | bytes 131072 | tf_op jit(solution)/shard_map/all_to_all | solution.py:124
  9.9 16.2 %copy-start = (bf16[128,2048]{1,0:T(8,128)(2,1)S(1)}, bf16[128,2048]{1,0:T(8,128)(2,1)}, u32[]{:S(2)}) copy-start(bf16[128,2048]{1,0:T(8,128)(2,1)} %param.11) | copy-start | bytes 1572868
  16.3 111.9 %copy-start.5 = (f32[256]{0:T(256)S(1)}, f32[256]{0:T(256)}, u32[]{:S(2)}) copy-start(f32[256]{0:T(256)} %param.14) | copy-start | bytes 3076
  20.0 71.7 %all-to-all-start.3 = ((bf16[128,16,1024]{0,2,1:T(8,128)(2,1)}), bf16[128,16,1024]{0,2,1:T(8,128)(2,1)}, u32[]{:S(2)}, u32[]{:S(2)}) async-start(bf16[128,16,1024]{0,2,1:T(8,128)(2,1)} %bitcast.114), calls=%async_computation.3 | async-start | bytes 8388608 | tf_op jit(solution)/shard_map/all_to_all | solution.py:121
  92.8 56.4 %all-to-all-start.2 = ((bf16[128,16,256]{2,0,1:T(8,128)(2,1)}), bf16[128,16,256]{2,0,1:T(8,128)(2,1)S(1)}, u32[]{:S(2)}, u32[]{:S(2)}) async-start(bf16[128,16,256]{2,0,1:T(8,128)(2,1)} %bitcast.10), calls=%async_computation.2 | async-start | bytes 2097152 | tf_op jit(solution)/shard_map/all_to_all | solution.py:122
  155.8 23.9 %copy-start.1 = (bf16[128,2048]{1,0:T(8,128)(2,1)S(1)}, bf16[128,2048]{1,0:T(8,128)(2,1)}, u32[]{:S(2)}) copy-start(bf16[128,2048]{1,0:T(8,128)(2,1)} %param.12) | copy-start | bytes 1572868
  155.8 63.7 %copy-start.6 = (f32[256]{0:T(256)S(1)}, f32[256]{0:T(256)}, u32[]{:S(2)}) copy-start(f32[256]{0:T(256)} %param.15) | copy-start | bytes 3076
  155.8 63.7 %copy-start.7 = (u32[256]{0:T(256)S(1)}, u32[256]{0:T(256)}, u32[]{:S(2)}) copy-start(u32[256]{0:T(256)} %constant.71) | copy-start | bytes 3076
  176.2 38.9 %collective-permute-start = (f32[16,64,256]{2,1,0:T(8,128)S(1)}, f32[16,64,256]{2,1,0:T(8,128)}, u32[]{:S(2)}, u32[]{:S(2)}) collective-permute-start(f32[16,64,256]{2,1,0:T(8,128)S(1)} %get-tuple-element.75), channel_id=1, source_target_pairs={{0,16},{16,32},{32,48},{48,64},{64,80},{80,96},{96,112},{112,128},... | collective-permute-start | bytes 3145736 | tf_op jit(solution)/shard_map/ppermute | solution.py:16
  180.9 107.2 %all-to-all-start.1 = ((bf16[128,16,256]{2,0,1:T(8,128)(2,1)}), bf16[128,16,256]{2,0,1:T(8,128)(2,1)S(1)}, u32[]{:S(2)}, u32[]{:S(2)}) async-start(bf16[128,16,256]{2,0,1:T(8,128)(2,1)} %bitcast.121), calls=%async_computation.1 | async-start | bytes 2097152 | tf_op jit(solution)/shard_map/all_to_all | solution.py:123
  217.6 67.5 %collective-permute-start.1 = (f32[16,64,256]{2,1,0:T(8,128)}, f32[16,64,256]{2,1,0:T(8,128)}, u32[]{:S(2)}, u32[]{:S(2)}) collective-permute-start(f32[16,64,256]{2,1,0:T(8,128)} %multiply_add_fusion.2), channel_id=1, source_target_pairs={{0,32},{16,48},{32,64},{48,80},{64,96},{80,112},{96,128},{112,144}... | collective-permute-start | bytes 3145736 | tf_op jit(solution)/shard_map/ppermute | solution.py:16
  286.8 22.8 %copy-start.4 = (f32[16]{0:T(128)S(1)}, f32[16]{0:T(128)}, u32[]{:S(2)}) copy-start(f32[16]{0:T(128)} %exp.79) | copy-start | bytes 196
  286.8 22.8 %collective-permute-start.2 = (f32[16,64,256]{2,1,0:T(8,128)S(1)}, f32[16,64,256]{2,1,0:T(8,128)}, u32[]{:S(2)}, u32[]{:S(2)}) collective-permute-start(f32[16,64,256]{2,1,0:T(8,128)S(1)} %multiply_add_fusion.1), channel_id=1, source_target_pairs={{0,64},{16,80},{32,96},{48,112},{64,128},{80,144},{96,160},{112,17... | collective-permute-start | bytes 3145736 | tf_op jit(solution)/shard_map/ppermute | solution.py:16
  311.0 45.5 %collective-permute-start.3 = (f32[16,64,256]{2,1,0:T(8,128)S(1)}, f32[16,64,256]{2,1,0:T(8,128)}, u32[]{:S(2)}, u32[]{:S(2)}) collective-permute-start(f32[16,64,256]{2,1,0:T(8,128)S(1)} %multiply_add_fusion), channel_id=1, source_target_pairs={{0,128},{16,144},{32,160},{48,176},{64,192},{80,208},{96,224},{112... | collective-permute-start | bytes 3145736 | tf_op jit(solution)/shard_map/ppermute | solution.py:16
  312.4 44.0 %copy-start.2 = (f32[16]{0:T(128)S(1)}, f32[16]{0:T(128)}, u32[]{:S(2)}) copy-start(f32[16]{0:T(128)} %exp.82) | copy-start | bytes 196
  312.5 44.0 %copy-start.3 = (f32[16]{0:T(128)S(1)}, f32[16]{0:T(128)}, u32[]{:S(2)}) copy-start(f32[16]{0:T(128)} %exp.78) | copy-start | bytes 196

commit v3 on v1

--- a/solution.py
+++ b/solution.py
@@ -67,17 +67,26 @@
     before = jnp.cumsum(block_ends, axis=0) - block_ends
     totals = jnp.sum(block_ends, axis=0)
     chain_len = lax.axis_size("chain")
+    state_rows = local_heads * CHANNEL_WIDTH
+
+    def pack(decay, state):
+        decay_row = jnp.broadcast_to(decay[None, :], (8, local_heads))
+        decay_row = jnp.pad(decay_row, ((0, 0), (0, SSTATE - local_heads)))
+        return jnp.concatenate([state.reshape(state_rows, SSTATE), decay_row], axis=0)
+
+    def unpack(packed):
+        state = packed[:state_rows].reshape(local_heads, CHANNEL_WIDTH, SSTATE)
+        return packed[state_rows, :local_heads], state
+
     own_decay = jnp.exp(totals)
-    got_decay = from_behind(own_decay, "chain", 1)
-    got_state = from_behind(final_state, "chain", 1)
+    got_decay, got_state = unpack(from_behind(pack(own_decay, final_state), "chain", 1))
     span_decay = got_decay * own_decay
     span_state = own_decay[:, None, None] * got_state + final_state
     incoming_state = got_state
     incoming_decay = got_decay
     shift = 2
     while shift < chain_len:
-        got_decay = from_behind(span_decay, "chain", shift)
-        got_state = from_behind(span_state, "chain", shift)
+        got_decay, got_state = unpack(from_behind(pack(span_decay, span_state), "chain", shift))
         incoming_state = incoming_decay[:, None, None] * got_state + incoming_state
         incoming_decay = incoming_decay * got_decay
         if 2 * shift < chain_len:
@@ -95,8 +104,10 @@
     head_start = lax.axis_index("head") * local_heads
     gain_heads = lax.dynamic_slice_in_dim(skip_gain, head_start, local_heads)
     result = (within + carried + gain_heads[:, None] * values_wide).astype(jnp.bfloat16)
-    result = result.reshape(blocks * BLOCK, local_heads * CHANNEL_WIDTH)
-    return lax.all_to_all(result, "head", split_axis=0, concat_axis=1, tiled=True)
+    head_count = lax.axis_size("head")
+    result = result.reshape(head_count, -1, local_heads * CHANNEL_WIDTH).transpose(1, 0, 2)
+    result = lax.all_to_all(result, "head", split_axis=1, concat_axis=1, tiled=True)
+    return result.reshape(result.shape[0], -1)
 
 
 def shards(signal, input_map, output_map, step_size, decay_rate, skip_gain):

time: 494 us -> 490 us (level); the launches traced: 492 us -> 483 us
  waiting for transfers between devices: 179 us -> 159 us
  matrix products: 30 us -> 40.2 us
  starting transfers between devices: 72.8 us -> 67.5 us
    ppermute x7 -> x4, waiting for transfers between devices: 110 us -> 89.9 us  [from_behind(): return lax.ppermute(array, axis, pairs)]
    all_to_all x3 -> x0, local copies, waits for them, and re-layouts: 16.7 us -> none  [finish(): lax.all_to_all(result, 'head', split_axis=0, concat_axis=1, tiled=True)]
    reshape x1 -> x3, local copies, waits for them, and re-layouts: 0.05 us -> 13.5 us  [the longest x1 7.07 us: finish(): result.reshape(head_count, -1, local_heads * CHANNEL_WIDTH)]
    dot_general x8, matrix products: 1.77 us -> 9.5 us  [block_weights(): jnp.einsum('tgn,sgn->gts', output_k, input_k, preferred_element_type=jnp....]
    ppermute x7 -> x4, starting transfers between devices: 13.3 us -> 8.27 us  [from_behind(): return lax.ppermute(array, axis, pairs)]
  transfers between devices with their start and end apart: 11 -> 8, of which waited for: 8 -> 5; matrix products, arithmetic and copies ran while one was open for 13% -> 15% of each run, Pallas kernels for 0% -> 0%
where the time goes in v3:
time: 490 us; the launch traced here: 483 us
  waiting for transfers between devices  159 us (32%)
  blocking collectives  106 us (22%)
  starting transfers between devices  67.5 us (14%)
  local copies, waits for them, and re-layouts  54.8 us (11%)
  other arithmetic  53.7 us (11%)
  matrix products  40.2 us (8%)
    all_to_all x1, blocking collectives, finish(): lax.all_to_all(result, 'head', split_axis=1, concat_axis=1, tiled=True)  106 us
    ppermute x4, waiting for transfers between devices, from_behind(): return lax.ppermute(array, axis, pairs)  89.9 us
    all_to_all x1, waiting for transfers between devices, shards(): lax.all_to_all(signal, 'head', split_axis=1, concat_axis=0, tiled=True)  65.5 us
    all_to_all x1, starting transfers between devices, shards(): lax.all_to_all(input_rep, 'head', split_axis=1, concat_axis=0, tiled=True)  35.4 us
    dynamic_update_slice x8, other arithmetic, prepare(): lax.map(block_weights, (cumul, step_rate, input_groups, output_groups))  18.2 us
    dot_general x1, matrix products, finish(): jnp.einsum('ktgn,kgjpn->ktgjp', output_groups, rounded, preferred_element...  12.1 us
    dot_general x1, matrix products, finish(): jnp.einsum('khts,kshp->kthp', weights, values, preferred_element_type=jnp...  11.6 us
    add x8, other arithmetic, carry_step(): jnp.exp(block_end)[:, None, None] * carry_state + fresh_block  11.4 us
  transfers between devices with their start and end apart: 8, of which 5 were waited for; matrix products, arithmetic and copies ran while one was open for 15% of the time, Pallas kernels for 0%

profile of v3, /device:TPU:96, one launch (start us, length us, event | category | flops | bytes accessed | tf_op | source)
XLA Modules:
  0.0 482.6 jit_solution(14735442699739599850)
XLA Ops:
  1.6 8.3 %all-to-all-start = ((bf16[128,16,16]{0,2,1:T(8,128)(2,1)}), bf16[128,16,16]{0,2,1:T(8,128)(2,1)S(1)}, u32[]{:S(2)}, u32[]{:S(2)}) async-start(bf16[128,16,16]{0,2,1:T(8,128)(2,1)} %bitcast), calls=%async_computation | async-start | bytes 131072 | tf_op jit(solution)/shard_map/all_to_all | solution.py:130
  9.9 6.4 %copy.71 = bf16[128,16384]{0,1:T(8,128)(2,1)} copy(bf16[128,16384]{1,0:T(8,128)(2,1)} %param.10) | data formatting | bytes 8388608 | tf_op args[0]
  16.3 3.7 all-to-all-done
  20.0 6.1 %all-to-all-start.3 = ((bf16[128,16,1024]{0,2,1:T(8,128)(2,1)}), bf16[128,16,1024]{0,2,1:T(8,128)(2,1)}, u32[]{:S(2)}, u32[]{:S(2)}) async-start(bf16[128,16,1024]{0,2,1:T(8,128)(2,1)} %bitcast.150), calls=%async_computation.3 | async-start | bytes 8388608 | tf_op jit(solution)/shard_map/all_to_all | solution.py:127
  26.2 65.5 %all-to-all-done.3 = bf16[128,16,1024]{0,2,1:T(8,128)(2,1)} async-done(((bf16[128,16,1024]{0,2,1:T(8,128)(2,1)}), bf16[128,16,1024]{0,2,1:T(8,128)(2,1)}, u32[]{:S(2)}, u32[]{:S(2)}) %all-to-all-start.3) | async-done | bytes 4194336 | tf_op jit(solution)/shard_map/all_to_all | solution.py:127
  92.7 35.4 %all-to-all-start.2 = ((bf16[128,16,256]{2,0,1:T(8,128)(2,1)}), bf16[128,16,256]{2,0,1:T(8,128)(2,1)S(1)}, u32[]{:S(2)}, u32[]{:S(2)}) async-start(bf16[128,16,256]{2,0,1:T(8,128)(2,1)} %bitcast.10), calls=%async_computation.2 | async-start | bytes 2097152 | tf_op jit(solution)/shard_map/all_to_all | solution.py:128
  128.6 4.6 reduce-window.6
  135.1 6.9 %copy.72 = bf16[16,128,1024]{1,0,2:T(8,128)(2,1)} copy(bf16[16,128,1024]{1,2,0:T(8,128)(2,1)} %bitcast.15) | data formatting | bytes 8388608 | tf_op jit(solution)/shard_map/all_to_all | solution.py:127
  142.0 7.1 %reshape.264 = bf16[8,256,16,64]{1,0,3,2:T(8,128)(2,1)} reshape(bf16[16,128,1024]{1,0,2:T(8,128)(2,1)} %copy.72) | data formatting | bytes 8388608 | tf_op jit(solution)/shard_map/reshape | solution.py:49
  149.2 7.1 %fusion.16 = f32[8,16,64,256]{3,2,1,0:T(8,128)} fusion(bf16[8,256,256,1]{2,1,3,0:T(8,128)(2,1)S(1)} %bitcast.161, f32[8,256,16]{1,2,0:T(8,128)S(1)} %copy.76, bf16[8,256,16,64]{1,0,3,2:T(8,128)(2,1)} %reshape.264), kind=kOutput, calls=%fused_computation.28 | convolution fusion | flops 1080033280 | bytes 13762560 | tf_op jit(solution)/shard_map/ksgjp,ksgn->kgjpn/dot_general | solution.py:55
  156.2 20.4 %while.26 = (s32[]{:T(128)}, f32[16,64,256]{2,1,0:T(8,128)S(1)}, f32[8,16,64,256]{3,2,1,0:T(8,128)}, f32[8,16]{1,0:T(8,128)S(1)}, f32[8,16,64,256]{3,2,1,0:T(8,128)}, /*index=5*/s32[]{:T(128)}, s32[]{:T(128)}) while((s32[]{:T(128)}, f32[16,64,256]{2,1,0:T(8,128)S(1)}, f32[8,16,64,256]{3,2,1,0:T(8,128)}, f32[8,16]{1,0:T(8,128)S(1)}, ...), condition=%wide.region_5.6_spmd.clone, body=%wide.region_4.5_spmd.clone.sunk | while | flops 1048579 | bytes 5243180 | solution.py:66
  176.8 3.6 collective-permute-start
  180.4 35.2 %collective-permute-done = f32[1032,256]{1,0:T(8,128)S(1)} collective-permute-done((f32[1032,256]{1,0:T(8,128)S(1)}, f32[1032,256]{1,0:T(8,128)S(1)}, u32[]{:S(2)}, u32[]{:S(2)}) %collective-permute-start) | collective-permute-done | bytes 1056800 | tf_op jit(solution)/shard_map/ppermute | solution.py:16
  220.9 9.4 %all-to-all-start.1 = ((bf16[128,16,256]{2,0,1:T(8,128)(2,1)}), bf16[128,16,256]{2,0,1:T(8,128)(2,1)}, u32[]{:S(2)}, u32[]{:S(2)}) async-start(bf16[128,16,256]{2,0,1:T(8,128)(2,1)} %bitcast.6), calls=%async_computation.1 | async-start | bytes 2097152 | tf_op jit(solution)/shard_map/all_to_all | solution.py:129
  231.1 18.1 %collective-permute-done.1 = f32[1032,256]{1,0:T(8,128)} collective-permute-done((f32[1032,256]{1,0:T(8,128)}, f32[1032,256]{1,0:T(8,128)}, u32[]{:S(2)}, u32[]{:S(2)}) %collective-permute-start.1) | collective-permute-done | bytes 1056800 | tf_op jit(solution)/shard_map/ppermute | solution.py:16
  255.1 28.5 %while.25 = (s32[]{:T(128)}, bf16[8,16,256,256]{3,2,1,0:T(8,128)(2,1)}, f32[8,256,16]{1,0,2:T(8,128)S(1)}, bf16[8,256,1,256]{3,1,2,0:T(8,128)(2,1)}, bf16[8,256,...) while((s32[]{:T(128)}, bf16[8,16,256,256]{3,2,1,0:T(8,128)(2,1)}, ...), condition=%wide.region_3.4_spmd.clone.clone, body=%wide.region_2.3_spmd.clone.clone.sunk | while | flops 39911424 | bytes 3195997 | solution.py:41
  288.9 11.6 %fusion.22 = f32[8,16,256,64]{2,3,1,0:T(8,128)} fusion(bf16[8,16,256,256]{3,2,1,0:T(8,128)(2,1)} %get-tuple-element.73, bf16[8,256,16,64]{1,0,3,2:T(8,128)(2,1)} %reshape.264), kind=kOutput, calls=%fused_computation.33 | convolution fusion | flops 1073741824 | bytes 29360128 | tf_op jit(solution)/shard_map/khts,kshp->kthp/dot_general | solution.py:51
  301.2 36.5 %collective-permute-done.3 = f32[1032,256]{1,0:T(8,128)} collective-permute-done((f32[1032,256]{1,0:T(8,128)}, f32[1032,256]{1,0:T(8,128)}, u32[]{:S(2)}, u32[]{:S(2)}) %collective-permute-start.3) | collective-permute-done | bytes 1056800 | tf_op jit(solution)/shard_map/ppermute | solution.py:16
  340.4 12.1 %fusion.13 = bf16[8,256,16,64]{1,3,2,0:T(8,128)(2,1)} fusion(f32[8,16,256,64]{2,3,1,0:T(8,128)} %fusion.22, f32[16]{0:T(128)S(1)} %copy-done.7, f32[8,256,16]{1,2,0:T(8,128)S(1)} %copy.78, bf16[8,256,16,64]{1,0,3,2:T(8,128)(2,1)} %reshape.264, bf16[8,256,256,1]{2,1,3,0:T(8,128)(2,1)} %bitcast.39, f32[8,16,64,256]{3,2,1,0:T(8,128)} %get-tuple-element.74, ...), kind=kOutput, calls=%fused_computation.23 | convolution fusion | flops 1092616192 | bytes 27394624 | tf_op jit(solution)/shard_map/ktgn,kgjpn->ktgjp/dot_general | solution.py:100
  352.5 7.0 %copy.79 = bf16[8,256,16,64]{1,0,3,2:T(8,128)(2,1)} copy(bf16[8,256,16,64]{1,3,2,0:T(8,128)(2,1)} %fusion.13) | data formatting | bytes 8388608 | tf_op jit(solution)/shard_map/convert_element_type | solution.py:106
  359.5 7.1 %reshape.276 = bf16[16,128,1024]{1,0,2:T(8,128)(2,1)} reshape(bf16[8,256,16,64]{1,0,3,2:T(8,128)(2,1)} %copy.79) | data formatting | bytes 8388608 | tf_op jit(solution)/shard_map/reshape | solution.py:108
  366.6 3.3 copy.80
  369.9 106.4 %all_to_all.66 = bf16[128,16,1024]{0,2,1:T(8,128)(2,1)} all-to-all(bf16[128,16,1024]{0,2,1:T(8,128)(2,1)S(1)} %copy.80), channel_id=1, replica_groups=mesh['chain'=16,'head'=16] {'head'}, dimensions={1} | all-to-all | bytes 8388608 | tf_op jit(solution)/shard_map/all_to_all | solution.py:109
  476.3 6.4 %copy.81 = bf16[128,16384]{1,0:T(8,128)(2,1)} copy(bf16[128,16384]{0,1:T(8,128)(2,1)} %bitcast.152) | data formatting | bytes 8388608 | tf_op jit(solution)/shard_map/reshape | solution.py:110
  (155 shorter events, 74.0 us)
Async XLA Ops:
  1.6 18.4 %all-to-all-start = ((bf16[128,16,16]{0,2,1:T(8,128)(2,1)}), bf16[128,16,16]{0,2,1:T(8,128)(2,1)S(1)}, u32[]{:S(2)}, u32[]{:S(2)}) async-start(bf16[128,16,16]{0,2,1:T(8,128)(2,1)} %bitcast), calls=%async_computation | async-start | bytes 131072 | tf_op jit(solution)/shard_map/all_to_all | solution.py:130
  20.0 6.1 %copy-start.4 = (bf16[128,2048]{1,0:T(8,128)(2,1)S(1)}, bf16[128,2048]{1,0:T(8,128)(2,1)}, u32[]{:S(2)}) copy-start(bf16[128,2048]{1,0:T(8,128)(2,1)} %param.11) | copy-start | bytes 1572868
  20.0 71.7 %all-to-all-start.3 = ((bf16[128,16,1024]{0,2,1:T(8,128)(2,1)}), bf16[128,16,1024]{0,2,1:T(8,128)(2,1)}, u32[]{:S(2)}, u32[]{:S(2)}) async-start(bf16[128,16,1024]{0,2,1:T(8,128)(2,1)} %bitcast.150), calls=%async_computation.3 | async-start | bytes 8388608 | tf_op jit(solution)/shard_map/all_to_all | solution.py:127
  26.1 102.1 %copy-start.8 = (f32[256]{0:T(256)S(1)}, f32[256]{0:T(256)}, u32[]{:S(2)}) copy-start(f32[256]{0:T(256)} %param.14) | copy-start | bytes 3076
  92.7 56.4 %all-to-all-start.2 = ((bf16[128,16,256]{2,0,1:T(8,128)(2,1)}), bf16[128,16,256]{2,0,1:T(8,128)(2,1)S(1)}, u32[]{:S(2)}, u32[]{:S(2)}) async-start(bf16[128,16,256]{2,0,1:T(8,128)(2,1)} %bitcast.10), calls=%async_computation.2 | async-start | bytes 2097152 | tf_op jit(solution)/shard_map/all_to_all | solution.py:128
  149.2 7.1 %copy-start.2 = (bf16[128,16,256]{2,0,1:T(8,128)(2,1)}, bf16[128,16,256]{2,0,1:T(8,128)(2,1)S(1)}, u32[]{:S(2)}) copy-start(bf16[128,16,256]{2,0,1:T(8,128)(2,1)S(1)} %all-to-all-done.2) | copy-start | bytes 3145732
  176.8 43.0 %copy-start.5 = (bf16[128,2048]{1,0:T(8,128)(2,1)S(1)}, bf16[128,2048]{1,0:T(8,128)(2,1)}, u32[]{:S(2)}) copy-start(bf16[128,2048]{1,0:T(8,128)(2,1)} %param.12) | copy-start | bytes 1572868
  176.8 38.8 %collective-permute-start = (f32[1032,256]{1,0:T(8,128)S(1)}, f32[1032,256]{1,0:T(8,128)S(1)}, u32[]{:S(2)}, u32[]{:S(2)}) collective-permute-start(f32[1032,256]{1,0:T(8,128)S(1)} %pad_maximum_fusion), channel_id=1, source_target_pairs={{0,16},{16,32},{32,48},{48,64},{64,80},{80,96},{96,112},{112,128},... | collective-permute-start | bytes 3170312 | tf_op jit(solution)/shard_map/ppermute | solution.py:16
  215.6 1.0 copy-start.3
  216.7 13.6 %copy-start.9 = (f32[256]{0:T(256)S(1)}, f32[256]{0:T(256)}, u32[]{:S(2)}) copy-start(f32[256]{0:T(256)} %param.15) | copy-start | bytes 3076
  216.8 14.3 %copy-start.6 = (f32[8,256,16]{1,0,2:T(8,128)S(1)}, f32[8,256,16]{1,0,2:T(8,128)}, u32[]{:S(2)}) copy-start(f32[8,256,16]{1,0,2:T(8,128)} %get-tuple-element.183) | copy-start | bytes 393220
  217.8 31.4 %collective-permute-start.1 = (f32[1032,256]{1,0:T(8,128)}, f32[1032,256]{1,0:T(8,128)}, u32[]{:S(2)}, u32[]{:S(2)}) collective-permute-start(f32[1032,256]{1,0:T(8,128)} %pad_maximum_fusion.1), channel_id=1, source_target_pairs={{0,32},{16,48},{32,64},{48,80},{64,96},{80,112},{96,128},{112,144}... | collective-permute-start | bytes 3170312 | tf_op jit(solution)/shard_map/ppermute | solution.py:16
  220.9 34.1 %all-to-all-start.1 = ((bf16[128,16,256]{2,0,1:T(8,128)(2,1)}), bf16[128,16,256]{2,0,1:T(8,128)(2,1)}, u32[]{:S(2)}, u32[]{:S(2)}) async-start(bf16[128,16,256]{2,0,1:T(8,128)(2,1)} %bitcast.6), calls=%async_computation.1 | async-start | bytes 2097152 | tf_op jit(solution)/shard_map/all_to_all | solution.py:129
  251.2 1.5 copy-start
  253.8 29.8 %collective-permute-start.2 = (f32[1032,256]{1,0:T(8,128)}, f32[1032,256]{1,0:T(8,128)}, u32[]{:S(2)}, u32[]{:S(2)}) collective-permute-start(f32[1032,256]{1,0:T(8,128)} %pad_maximum_fusion.2), channel_id=1, source_target_pairs={{0,64},{16,80},{32,96},{48,112},{64,128},{80,144},{96,160},{112,17... | collective-permute-start | bytes 3170312 | tf_op jit(solution)/shard_map/ppermute | solution.py:16
  287.5 50.3 %collective-permute-start.3 = (f32[1032,256]{1,0:T(8,128)}, f32[1032,256]{1,0:T(8,128)}, u32[]{:S(2)}, u32[]{:S(2)}) collective-permute-start(f32[1032,256]{1,0:T(8,128)} %pad_maximum_fusion.3), channel_id=1, source_target_pairs={{0,128},{16,144},{32,160},{48,176},{64,192},{80,208},{96,224},{112... | collective-permute-start | bytes 3170312 | tf_op jit(solution)/shard_map/ppermute | solution.py:16
  288.9 50.1 %copy-start.1 = (f32[1024,256]{1,0:T(8,128)S(1)}, f32[1024,256]{1,0:T(8,128)}, u32[]{:S(2)}) copy-start(f32[1024,256]{1,0:T(8,128)} %copy-done) | copy-start | bytes 3145732
  300.5 39.9 %copy-start.7 = (f32[16]{0:T(128)S(1)}, f32[16]{0:T(128)}, u32[]{:S(2)}) copy-start(f32[16]{0:T(128)} %dynamic_slice.29) | copy-start | bytes 196

commit v4 on v3

--- a/solution.py
+++ b/solution.py
@@ -10,8 +10,12 @@
 BLOCK = 256
 
 
+SEQ = ("chain", "half")
+LANE = "lane"
+
+
 def from_behind(array, axis, by):
-    size = lax.axis_size(axis)
+    size = lax.psum(1, axis)
     pairs = [(i, i + by) for i in range(size) if 0 <= i + by < size]
     return lax.ppermute(array, axis, pairs)
 
@@ -20,7 +24,7 @@
     chain_rows = input_c.shape[0]
     blocks = chain_rows // BLOCK
     per_group = local_heads // group_count
-    head_start = lax.axis_index("head") * local_heads
+    head_start = lax.axis_index(LANE) * local_heads
     head_rates = lax.dynamic_slice_in_dim(decay_rate, head_start, local_heads)
     step_rate = step_c.astype(jnp.float32).reshape(blocks, BLOCK, local_heads)
     cumul = jnp.cumsum(-head_rates * step_rate, axis=1)
@@ -66,7 +70,7 @@
     final_state, starts = lax.scan(carry_step, empty_state, (block_ends, fresh_state))
     before = jnp.cumsum(block_ends, axis=0) - block_ends
     totals = jnp.sum(block_ends, axis=0)
-    chain_len = lax.axis_size("chain")
+    chain_len = lax.psum(1, SEQ)
     state_rows = local_heads * CHANNEL_WIDTH
 
     def pack(decay, state):
@@ -79,14 +83,14 @@
         return packed[state_rows, :local_heads], state
 
     own_decay = jnp.exp(totals)
-    got_decay, got_state = unpack(from_behind(pack(own_decay, final_state), "chain", 1))
+    got_decay, got_state = unpack(from_behind(pack(own_decay, final_state), SEQ, 1))
     span_decay = got_decay * own_decay
     span_state = own_decay[:, None, None] * got_state + final_state
     incoming_state = got_state
     incoming_decay = got_decay
     shift = 2
     while shift < chain_len:
-        got_decay, got_state = unpack(from_behind(pack(span_decay, span_state), "chain", shift))
+        got_decay, got_state = unpack(from_behind(pack(span_decay, span_state), SEQ, shift))
         incoming_state = incoming_decay[:, None, None] * got_state + incoming_state
         incoming_decay = incoming_decay * got_decay
         if 2 * shift < chain_len:
@@ -101,17 +105,17 @@
         "ktgn,kgjpn->ktgjp", output_groups, rounded, preferred_element_type=jnp.float32
     )
     carried = carried.reshape(blocks, BLOCK, local_heads, CHANNEL_WIDTH) * jnp.exp(cumul)[..., None]
-    head_start = lax.axis_index("head") * local_heads
+    head_start = lax.axis_index(LANE) * local_heads
     gain_heads = lax.dynamic_slice_in_dim(skip_gain, head_start, local_heads)
     result = (within + carried + gain_heads[:, None] * values_wide).astype(jnp.bfloat16)
-    head_count = lax.axis_size("head")
+    head_count = lax.axis_size(LANE)
     result = result.reshape(head_count, -1, local_heads * CHANNEL_WIDTH).transpose(1, 0, 2)
-    result = lax.all_to_all(result, "head", split_axis=1, concat_axis=1, tiled=True)
+    result = lax.all_to_all(result, LANE, split_axis=1, concat_axis=1, tiled=True)
     return result.reshape(result.shape[0], -1)
 
 
 def shards(signal, input_map, output_map, step_size, decay_rate, skip_gain):
-    head_count = lax.axis_size("head")
+    head_count = lax.axis_size(LANE)
     local_heads = HEADS // head_count
     group_heads = HEADS // HEAD_GROUPS
     group_count = max(1, local_heads // group_heads)
@@ -124,27 +128,26 @@
         output_map.reshape(row_count, HEAD_GROUPS, SSTATE), copies, axis=1
     ).reshape(row_count, -1)
     signal_c, input_c, output_c, step_c = (
-        lax.all_to_all(signal, "head", split_axis=1, concat_axis=0, tiled=True),
-        lax.all_to_all(input_rep, "head", split_axis=1, concat_axis=0, tiled=True),
-        lax.all_to_all(output_rep, "head", split_axis=1, concat_axis=0, tiled=True),
-        lax.all_to_all(step_size, "head", split_axis=1, concat_axis=0, tiled=True),
+        lax.all_to_all(signal, LANE, split_axis=1, concat_axis=0, tiled=True),
+        lax.all_to_all(input_rep, LANE, split_axis=1, concat_axis=0, tiled=True),
+        lax.all_to_all(output_rep, LANE, split_axis=1, concat_axis=0, tiled=True),
+        lax.all_to_all(step_size, LANE, split_axis=1, concat_axis=0, tiled=True),
     )
     prepared = prepare(input_c, output_c, step_c, decay_rate, local_heads, group_count)
     return finish(signal_c, prepared, skip_gain, local_heads, group_count)
 
 
 def solution(mesh):
+    chain_count, head_count = mesh.devices.shape
+    halves = 2 if head_count % 2 == 0 else 1
+    split_mesh = jax.sharding.Mesh(
+        mesh.devices.reshape(chain_count, halves, head_count // halves), ("chain", "half", LANE)
+    )
+    rows = P(("chain", "half", LANE), None)
     return jax.shard_map(
         shards,
-        mesh=mesh,
-        in_specs=(
-            P(("chain", "head"), None),
-            P(("chain", "head"), None),
-            P(("chain", "head"), None),
-            P(("chain", "head"), None),
-            P(),
-            P(),
-        ),
-        out_specs=P(("chain", "head"), None),
+        mesh=split_mesh,
+        in_specs=(rows, rows, rows, rows, P(), P()),
+        out_specs=rows,
         check_vma=False,
     )

time: 490 us -> 608 us (1.24)
  waiting for transfers between devices: 159 us -> 380 us
  blocking collectives: 106 us -> 53 us
  starting transfers between devices: 67.5 us -> 35.9 us
  other arithmetic: 53.7 us -> 43.7 us
  matrix products: 40.2 us -> 32.2 us
  local copies, waits for them, and re-layouts: 54.8 us -> 61.2 us
    ppermute x4 -> x5, waiting for transfers between devices: 89.9 us -> 318 us  [from_behind(): return lax.ppermute(array, axis, pairs)]
    all_to_all x1, blocking collectives: 106 us -> 53 us  [finish(): lax.all_to_all(result, LANE, split_axis=1, concat_axis=1, tiled=True)]
    all_to_all x4, starting transfers between devices: 59.3 us -> 16 us  [the longest x1 4.7 us: shards(): lax.all_to_all(signal, LANE, split_axis=1, concat_axis=0, tiled=True)]
    ppermute x4 -> x5, starting transfers between devices: 8.27 us -> 19.9 us  [from_behind(): return lax.ppermute(array, axis, pairs)]
    dot_general x8 -> x4, matrix products: 9.5 us -> 0.86 us  [block_weights(): jnp.einsum('tgn,sgn->gts', output_k, input_k, preferred_element_type=jnp....]
    unnamed x22 -> x40, local copies, waits for them, and re-layouts: 8.85 us -> 16.5 us
    all_to_all x4, waiting for transfers between devices: 69.2 us -> 62.2 us  [the longest x1 45.2 us: shards(): lax.all_to_all(signal, LANE, split_axis=1, concat_axis=0, tiled=True)]
    dynamic_update_slice x8 -> x4, other arithmetic: 18.2 us -> 15.6 us  [prepare(): lax.map(block_weights, (cumul, step_rate, input_groups, output_groups))]
  transfers between devices with their start and end apart: 8 -> 9, of which waited for: 5 -> 9; matrix products, arithmetic and copies ran while one was open for 15% -> 8% of each run, Pallas kernels for 0% -> 0%
where the time goes in v4:
time: 608 us; the launch traced here: 606 us
  waiting for transfers between devices  380 us (62%)
  local copies, waits for them, and re-layouts  61.2 us (10%)
  blocking collectives  53 us (9%)
  other arithmetic  43.7 us (7%)
  starting transfers between devices  35.9 us (6%)
  matrix products  32.2 us (5%)
    ppermute x5, waiting for transfers between devices, from_behind(): return lax.ppermute(array, axis, pairs)  318 us
    all_to_all x1, blocking collectives, finish(): lax.all_to_all(result, LANE, split_axis=1, concat_axis=1, tiled=True)  53 us
    all_to_all x1, waiting for transfers between devices, shards(): lax.all_to_all(signal, LANE, split_axis=1, concat_axis=0, tiled=True)  45.2 us
    ppermute x5, starting transfers between devices, from_behind(): return lax.ppermute(array, axis, pairs)  19.9 us
    unnamed x40, local copies, waits for them, and re-layouts  16.5 us
    dynamic_update_slice x4, other arithmetic, prepare(): lax.map(block_weights, (cumul, step_rate, input_groups, output_groups))  15.6 us
    dot_general x1, matrix products, finish(): jnp.einsum('khts,kshp->kthp', weights, values, preferred_element_type=jnp...  12.9 us
  transfers between devices with their start and end apart: 9, of which 9 were waited for; matrix products, arithmetic and copies ran while one was open for 8% of the time, Pallas kernels for 0%

profile of v4, /device:TPU:96, one launch (start us, length us, event | category | flops | bytes accessed | tf_op | source)
XLA Modules:
  0.0 606.4 jit_solution(4884932233288801624)
XLA Ops:
  1.6 4.3 all-to-all-start
  15.0 6.4 %copy.97 = bf16[128,16384]{0,1:T(8,128)(2,1)} copy(bf16[128,16384]{1,0:T(8,128)(2,1)} %param.10) | data formatting | bytes 8388608 | tf_op args[0]
  25.2 4.7 all-to-all-start.3
  34.4 45.2 %all-to-all-done.3 = bf16[128,8,2048]{0,2,1:T(8,128)(2,1)} async-done(((bf16[128,8,2048]{0,2,1:T(8,128)(2,1)}), bf16[128,8,2048]{0,2,1:T(8,128)(2,1)}, u32[]{:S(2)}, u32[]{:S(2)}) %all-to-all-start.3) | async-done | bytes 4194336 | tf_op jit(solution)/shard_map/all_to_all | solution.py:131
  79.6 6.2 %copy.98 = bf16[8,128,2048]{1,0,2:T(8,128)(2,1)} copy(bf16[8,128,2048]{1,2,0:T(8,128)(2,1)} %bitcast.14) | data formatting | bytes 8388608 | tf_op jit(solution)/shard_map/all_to_all | solution.py:131
  85.8 7.6 %reshape.294 = bf16[4,256,32,64]{1,0,3,2:T(4,128)(2,1)} reshape(bf16[8,128,2048]{1,0,2:T(8,128)(2,1)} %copy.98) | data formatting | bytes 8388608 | tf_op jit(solution)/shard_map/reshape | solution.py:53
  93.4 6.7 %fusion.16 = f32[4,32,64,256]{3,2,1,0:T(8,128)} fusion(bf16[4,256,256,1]{2,1,3,0:T(8,128)(2,1)S(1)} %bitcast.163, f32[4,256,32]{1,2,0:T(8,128)S(1)} %copy-done.11, bf16[4,256,32,64]{1,0,3,2:T(4,128)(2,1)} %reshape.294), kind=kOutput, calls=%fused_computation.26 | convolution fusion | flops 1080033280 | bytes 13238272 | tf_op jit(solution)/shard_map/ksgjp,ksgn->kgjpn/dot_general | solution.py:59
  100.1 14.0 %while.26 = (s32[]{:T(128)}, f32[32,64,256]{2,1,0:T(8,128)S(1)}, f32[4,32,64,256]{3,2,1,0:T(8,128)}, f32[4,32]{1,0:T(4,128)S(1)}, f32[4,32,64,256]{3,2,1,0:T(8,128)}, /*index=5*/s32[]{:T(128)}, s32[]{:T(128)}) while((s32[]{:T(128)}, f32[32,64,256]{2,1,0:T(8,128)S(1)}, f32[4,32,64,256]{3,2,1,0:T(8,128)}, f32[4,32]{1,0:T(4,128)S(1)}, ...), condition=%wide.region_5.6_spmd.clone, body=%wide.region_4.5_spmd.clone.sunk | while | flops 2097155 | bytes 10486252 | solution.py:70
  114.3 6.4 %collective-permute-start = (f32[2056,256]{1,0:T(8,128)S(1)}, f32[2056,256]{1,0:T(8,128)S(1)}, u32[]{:S(2)}, u32[]{:S(2)}) collective-permute-start(f32[2056,256]{1,0:T(8,128)S(1)} %pad_maximum_fusion), channel_id=1, source_target_pairs={{0,8},{8,16},{16,24},{24,32},{32,40},{40,48},{48,56},{56,64},{64,7... | collective-permute-start | bytes 6316040 | tf_op jit(solution)/shard_map/ppermute | solution.py:20
  120.7 89.5 %collective-permute-done = f32[2056,256]{1,0:T(8,128)S(1)} collective-permute-done((f32[2056,256]{1,0:T(8,128)S(1)}, f32[2056,256]{1,0:T(8,128)S(1)}, u32[]{:S(2)}, u32[]{:S(2)}) %collective-permute-start) | collective-permute-done | bytes 2105376 | tf_op jit(solution)/shard_map/ppermute | solution.py:20
  212.0 7.2 %collective-permute-start.1 = (f32[2056,256]{1,0:T(8,128)S(1)}, f32[2056,256]{1,0:T(8,128)S(1)}, u32[]{:S(2)}, u32[]{:S(2)}) collective-permute-start(f32[2056,256]{1,0:T(8,128)S(1)} %pad_maximum_fusion.1), channel_id=1, source_target_pairs={{0,16},{8,24},{16,32},{24,40},{32,48},{40,56},{48,64},{56,72},{64,... | collective-permute-start | bytes 6316040 | tf_op jit(solution)/shard_map/ppermute | solution.py:20
  219.2 46.3 %collective-permute-done.1 = f32[2056,256]{1,0:T(8,128)S(1)} collective-permute-done((f32[2056,256]{1,0:T(8,128)S(1)}, f32[2056,256]{1,0:T(8,128)S(1)}, u32[]{:S(2)}, u32[]{:S(2)}) %collective-permute-start.1) | collective-permute-done | bytes 2105376 | tf_op jit(solution)/shard_map/ppermute | solution.py:20
  271.2 47.7 %collective-permute-done.2 = f32[2056,256]{1,0:T(8,128)S(1)} collective-permute-done((f32[2056,256]{1,0:T(8,128)S(1)}, f32[2056,256]{1,0:T(8,128)S(1)}, u32[]{:S(2)}, u32[]{:S(2)}) %collective-permute-start.2) | collective-permute-done | bytes 2105376 | tf_op jit(solution)/shard_map/ppermute | solution.py:20
  328.9 9.6 %all-to-all-done.1 = bf16[128,8,256]{0,2,1:T(8,128)(2,1)S(1)} async-done(((bf16[128,8,256]{0,2,1:T(8,128)(2,1)}), bf16[128,8,256]{0,2,1:T(8,128)(2,1)S(1)}, u32[]{:S(2)}, u32[]{:S(2)}) %all-to-all-start.1) | async-done | bytes 524320 | tf_op jit(solution)/shard_map/all_to_all | solution.py:133
  340.5 30.2 %collective-permute-done.3 = f32[2056,256]{1,0:T(8,128)} collective-permute-done((f32[2056,256]{1,0:T(8,128)}, f32[2056,256]{1,0:T(8,128)}, u32[]{:S(2)}, u32[]{:S(2)}) %collective-permute-start.3) | collective-permute-done | bytes 2105376 | tf_op jit(solution)/shard_map/ppermute | solution.py:20
  377.4 16.7 %while.25 = (s32[]{:T(128)}, bf16[4,32,256,256]{3,2,1,0:T(8,128)(2,1)}, f32[4,256,32]{1,2,0:T(8,128)S(1)}, bf16[4,256,1,256]{3,1,2,0:T(8,128)(2,1)S(1)}, bf16[4,...) while((s32[]{:T(128)}, ...), condition=%wide.region_3.4_spmd.clone.clone, body=%wide.region_2.3_spmd.clone.clone.sunk | while | flops 46202880 | bytes 5342301 | solution.py:45
  381.9 3.9 fusion.41
  394.1 12.9 %fusion.22 = f32[4,32,256,64]{2,3,1,0:T(8,128)} fusion(bf16[4,32,256,256]{3,2,1,0:T(8,128)(2,1)} %get-tuple-element.73, bf16[4,256,32,64]{1,0,3,2:T(4,128)(2,1)} %reshape.294), kind=kOutput, calls=%fused_computation.31 | convolution fusion | flops 1073741824 | bytes 29360128 | tf_op jit(solution)/shard_map/khts,kshp->kthp/dot_general | solution.py:55
  407.8 103.9 %collective-permute-done.4 = f32[2056,256]{1,0:T(8,128)} collective-permute-done((f32[2056,256]{1,0:T(8,128)}, f32[2056,256]{1,0:T(8,128)}, u32[]{:S(2)}, u32[]{:S(2)}) %collective-permute-start.4) | collective-permute-done | bytes 2105376 | tf_op jit(solution)/shard_map/ppermute | solution.py:20
  517.3 11.8 %fusion.13 = bf16[4,256,32,64]{1,3,2,0:T(8,128)(2,1)} fusion(f32[4,32,256,64]{2,3,1,0:T(8,128)} %fusion.22, f32[32]{0:T(128)S(1)} %copy-done.15, f32[4,256,32]{1,2,0:T(8,128)S(1)} %get-tuple-element.184, bf16[4,256,32,64]{1,0,3,2:T(4,128)(2,1)} %reshape.294, bf16[4,256,256,1]{2,1,3,0:T(8,128)(2,1)S(1)} %bitcast.166, ...), kind=kOutput, calls=%fused_computation.21 | convolution fusion | flops 1092616192 | bytes 27918976 | tf_op jit(solution)/shard_map/ktgn,kgjpn->ktgjp/dot_general | solution.py:104
  529.1 8.1 %copy.104 = bf16[4,256,32,64]{1,0,3,2:T(4,128)(2,1)} copy(bf16[4,256,32,64]{1,3,2,0:T(8,128)(2,1)} %fusion.13) | data formatting | bytes 8388608 | tf_op jit(solution)/shard_map/convert_element_type | solution.py:110
  537.2 7.2 %reshape.308 = bf16[8,128,2048]{1,0,2:T(8,128)(2,1)} reshape(bf16[4,256,32,64]{1,0,3,2:T(4,128)(2,1)} %copy.104) | data formatting | bytes 8388608 | tf_op jit(solution)/shard_map/reshape | solution.py:112
  547.1 53.0 %all_to_all.66 = bf16[128,8,2048]{0,2,1:T(8,128)(2,1)} all-to-all(bf16[128,8,2048]{0,2,1:T(8,128)(2,1)S(1)} %copy.105), channel_id=1, replica_groups=mesh['chain'=16,'half'=2,'lane'=8] {'lane'}, dimensions={1} | all-to-all | bytes 8388608 | tf_op jit(solution)/shard_map/all_to_all | solution.py:113
  600.1 6.4 %copy.106 = bf16[128,16384]{1,0:T(8,128)(2,1)} copy(bf16[128,16384]{0,1:T(8,128)(2,1)} %bitcast.160) | data formatting | bytes 8388608 | tf_op jit(solution)/shard_map/reshape | solution.py:114
  (131 shorter events, 80.7 us)
Async XLA Ops:
  1.6 9.9 %all-to-all-start = ((bf16[128,8,32]{0,2,1:T(8,128)(2,1)}), bf16[128,8,32]{0,2,1:T(8,128)(2,1)S(1)}, u32[]{:S(2)}, u32[]{:S(2)}) async-start(bf16[128,8,32]{0,2,1:T(8,128)(2,1)} %bitcast), calls=%async_computation | async-start | bytes 131072 | tf_op jit(solution)/shard_map/all_to_all | solution.py:134
  11.5 13.7 %all-to-all-start.2 = ((bf16[128,8,256]{0,2,1:T(8,128)(2,1)}), bf16[128,8,256]{0,2,1:T(8,128)(2,1)S(1)}, u32[]{:S(2)}, u32[]{:S(2)}) async-start(bf16[128,8,256]{0,2,1:T(8,128)(2,1)} %bitcast.9), calls=%async_computation.2 | async-start | bytes 1048576 | tf_op jit(solution)/shard_map/all_to_all | solution.py:132
  25.2 4.7 copy-start.16
  25.2 54.3 %all-to-all-start.3 = ((bf16[128,8,2048]{0,2,1:T(8,128)(2,1)}), bf16[128,8,2048]{0,2,1:T(8,128)(2,1)}, u32[]{:S(2)}, u32[]{:S(2)}) async-start(bf16[128,8,2048]{0,2,1:T(8,128)(2,1)} %bitcast.158), calls=%async_computation.3 | async-start | bytes 8388608 | tf_op jit(solution)/shard_map/all_to_all | solution.py:131
  85.8 7.6 %copy-start.11 = (f32[4,256,32]{1,2,0:T(8,128)S(1)}, f32[4,256,32]{1,2,0:T(8,128)}, u32[]{:S(2)}) copy-start(f32[4,256,32]{1,2,0:T(8,128)} %get-tuple-element.183) | copy-start | bytes 393220
  114.3 95.9 %collective-permute-start = (f32[2056,256]{1,0:T(8,128)S(1)}, f32[2056,256]{1,0:T(8,128)S(1)}, u32[]{:S(2)}, u32[]{:S(2)}) collective-permute-start(f32[2056,256]{1,0:T(8,128)S(1)} %pad_maximum_fusion), channel_id=1, source_target_pairs={{0,8},{8,16},{16,24},{24,32},{32,40},{40,48},{48,56},{56,64},{64,7... | collective-permute-start | bytes 6316040 | tf_op jit(solution)/shard_map/ppermute | solution.py:20
  210.2 108.8 %copy-start.9 = (f32[2056,256]{1,0:T(8,128)}, f32[2056,256]{1,0:T(8,128)S(1)}, u32[]{:S(2)}) copy-start(f32[2056,256]{1,0:T(8,128)S(1)} %collective-permute-done) | copy-start | bytes 6316036
  210.3 1.5 copy-start
  212.0 53.5 %collective-permute-start.1 = (f32[2056,256]{1,0:T(8,128)S(1)}, f32[2056,256]{1,0:T(8,128)S(1)}, u32[]{:S(2)}, u32[]{:S(2)}) collective-permute-start(f32[2056,256]{1,0:T(8,128)S(1)} %pad_maximum_fusion.1), channel_id=1, source_target_pairs={{0,16},{8,24},{16,32},{24,40},{32,48},{40,56},{48,64},{56,72},{64,... | collective-permute-start | bytes 6316040 | tf_op jit(solution)/shard_map/ppermute | solution.py:20
  265.5 53.6 %copy-start.8 = (f32[2056,256]{1,0:T(8,128)}, f32[2056,256]{1,0:T(8,128)S(1)}, u32[]{:S(2)}) copy-start(f32[2056,256]{1,0:T(8,128)S(1)} %collective-permute-done.1) | copy-start | bytes 6316036
  267.7 51.3 %collective-permute-start.2 = (f32[2056,256]{1,0:T(8,128)S(1)}, f32[2056,256]{1,0:T(8,128)S(1)}, u32[]{:S(2)}, u32[]{:S(2)}) collective-permute-start(f32[2056,256]{1,0:T(8,128)S(1)} %pad_maximum_fusion.2), channel_id=1, source_target_pairs={{0,32},{8,40},{16,48},{24,56},{32,64},{40,72},{48,80},{56,88},{64,... | collective-permute-start | bytes 6316040 | tf_op jit(solution)/shard_map/ppermute | solution.py:20
  319.0 1.4 copy-start.10
  319.0 1.6 copy-start.13
  319.1 1.8 copy-start.4
  321.0 2.8 copy-start.12
  321.0 7.3 %copy-start.17 = (f32[256]{0:T(256)S(1)}, f32[256]{0:T(256)}, u32[]{:S(2)}) copy-start(f32[256]{0:T(256)} %param.15) | copy-start | bytes 3076
  322.4 48.3 %collective-permute-start.3 = (f32[2056,256]{1,0:T(8,128)}, f32[2056,256]{1,0:T(8,128)}, u32[]{:S(2)}, u32[]{:S(2)}) collective-permute-start(f32[2056,256]{1,0:T(8,128)} %pad_maximum_fusion.3), channel_id=1, source_target_pairs={{0,64},{8,72},{16,80},{24,88},{32,96},{40,104},{48,112},{56,120},{... | collective-permute-start | bytes 6316040 | tf_op jit(solution)/shard_map/ppermute | solution.py:20
  324.7 13.7 %all-to-all-start.1 = ((bf16[128,8,256]{0,2,1:T(8,128)(2,1)}), bf16[128,8,256]{0,2,1:T(8,128)(2,1)S(1)}, u32[]{:S(2)}, u32[]{:S(2)}) async-start(bf16[128,8,256]{0,2,1:T(8,128)(2,1)} %bitcast.169), calls=%async_computation.1 | async-start | bytes 1048576 | tf_op jit(solution)/shard_map/all_to_all | solution.py:133
  376.0 135.8 %collective-permute-start.4 = (f32[2056,256]{1,0:T(8,128)}, f32[2056,256]{1,0:T(8,128)}, u32[]{:S(2)}, u32[]{:S(2)}) collective-permute-start(f32[2056,256]{1,0:T(8,128)} %pad_maximum_fusion.4), channel_id=1, source_target_pairs={{0,128},{8,136},{16,144},{24,152},{32,160},{40,168},{48,176},{56,1... | collective-permute-start | bytes 6316040 | tf_op jit(solution)/shard_map/ppermute | solution.py:20
  394.1 119.4 %copy-start.5 = (f32[2048,256]{1,0:T(8,128)S(1)}, f32[2048,256]{1,0:T(8,128)}, u32[]{:S(2)}) copy-start(f32[2048,256]{1,0:T(8,128)} %copy-done.4) | copy-start | bytes 6291460
  407.0 106.5 %copy-start.1 = (f32[2048,256]{1,0:T(8,128)S(1)}, f32[2048,256]{1,0:T(8,128)}, u32[]{:S(2)}) copy-start(f32[2048,256]{1,0:T(8,128)} %copy-done) | copy-start | bytes 6291460
  407.0 106.6 %copy-start.3 = (f32[2048,256]{1,0:T(8,128)S(1)}, f32[2048,256]{1,0:T(8,128)}, u32[]{:S(2)}) copy-start(f32[2048,256]{1,0:T(8,128)} %copy-done.2) | copy-start | bytes 6291460
  407.0 106.6 %copy-start.14 = (f32[32]{0:T(128)S(1)}, f32[32]{0:T(128)}, u32[]{:S(2)}) copy-start(f32[32]{0:T(128)} %get-tuple-element.181) | copy-start | bytes 388
  513.5 3.8 copy-start.15
  (3 other events, 3.4 us)

commit v5 on v4

--- a/solution.py
+++ b/solution.py
@@ -70,33 +70,71 @@
     final_state, starts = lax.scan(carry_step, empty_state, (block_ends, fresh_state))
     before = jnp.cumsum(block_ends, axis=0) - block_ends
     totals = jnp.sum(block_ends, axis=0)
-    chain_len = lax.psum(1, SEQ)
-    state_rows = local_heads * CHANNEL_WIDTH
+    chain_len = lax.axis_size("chain")
+    half_count = lax.axis_size("half")
+    part = local_heads // half_count
+    half = lax.axis_index("half")
 
     def pack(decay, state):
-        decay_row = jnp.broadcast_to(decay[None, :], (8, local_heads))
-        decay_row = jnp.pad(decay_row, ((0, 0), (0, SSTATE - local_heads)))
-        return jnp.concatenate([state.reshape(state_rows, SSTATE), decay_row], axis=0)
+        rows = state.shape[0] * CHANNEL_WIDTH
+        decay_row = jnp.broadcast_to(decay[None, :], (8, decay.shape[0]))
+        decay_row = jnp.pad(decay_row, ((0, 0), (0, SSTATE - decay.shape[0])))
+        return jnp.concatenate([state.reshape(rows, SSTATE), decay_row], axis=0)
 
-    def unpack(packed):
-        state = packed[:state_rows].reshape(local_heads, CHANNEL_WIDTH, SSTATE)
-        return packed[state_rows, :local_heads], state
+    def unpack(packed, heads, decays):
+        rows = heads * CHANNEL_WIDTH
+        state = packed[:rows].reshape(heads, CHANNEL_WIDTH, SSTATE)
+        return packed[rows, :decays], state
+
+    def heads_of(array, which):
+        return lax.dynamic_slice_in_dim(array, which * part, part)
+
+    def swap(array):
+        return lax.ppermute(array, "half", [(0, 1), (1, 0)])
 
     own_decay = jnp.exp(totals)
-    got_decay, got_state = unpack(from_behind(pack(own_decay, final_state), SEQ, 1))
-    span_decay = got_decay * own_decay
-    span_state = own_decay[:, None, None] * got_state + final_state
+    if half_count == 2:
+        sent = pack(own_decay, heads_of(final_state, 1 - half))
+        other_decay, other_state = unpack(swap(sent), part, local_heads)
+        mine_state = heads_of(final_state, half)
+        first = half == 0
+        first_decay = jnp.where(first, own_decay, other_decay)
+        second_decay = jnp.where(first, other_decay, own_decay)
+        first_state = jnp.where(first, mine_state, other_state)
+        second_state = jnp.where(first, other_state, mine_state)
+        link_decay = heads_of(first_decay * second_decay, half)
+        link_state = heads_of(second_decay, half)[:, None, None] * first_state + second_state
+    else:
+        link_decay, link_state = own_decay, final_state
+
+    got_decay, got_state = unpack(
+        from_behind(pack(link_decay, link_state), "chain", 1), part, part
+    )
+    span_decay = got_decay * link_decay
+    span_state = link_decay[:, None, None] * got_state + link_state
     incoming_state = got_state
     incoming_decay = got_decay
     shift = 2
     while shift < chain_len:
-        got_decay, got_state = unpack(from_behind(pack(span_decay, span_state), SEQ, shift))
+        got_decay, got_state = unpack(
+            from_behind(pack(span_decay, span_state), "chain", shift), part, part
+        )
         incoming_state = incoming_decay[:, None, None] * got_state + incoming_state
         incoming_decay = incoming_decay * got_decay
         if 2 * shift < chain_len:
             span_state = span_decay[:, None, None] * got_state + span_state
             span_decay = span_decay * got_decay
         shift *= 2
+
+    if half_count == 2:
+        into_second = heads_of(first_decay, half)[:, None, None] * incoming_state + first_state
+        mine_start = jnp.where(first, incoming_state, into_second)
+        other_start = swap(jnp.where(first, into_second, incoming_state))
+        incoming_state = jnp.where(
+            first,
+            jnp.concatenate([mine_start, other_start], axis=0),
+            jnp.concatenate([other_start, mine_start], axis=0),
+        )
     starts = starts + jnp.exp(before)[:, :, None, None] * incoming_state
     rounded = starts.astype(jnp.bfloat16).reshape(
         blocks, group_count, per_group, CHANNEL_WIDTH, SSTATE

time: 608 us -> 482 us (0.79)
  waiting for transfers between devices: 380 us -> 247 us
    ppermute x5 -> x4, waiting for transfers between devices: 318 us -> 110 us  [from_behind(): return lax.ppermute(array, axis, pairs)]
    ppermute x0 -> x2, waiting for transfers between devices: none -> 74 us  [swap(): return lax.ppermute(array, 'half', [(0, 1), (1, 0)])]
    ppermute x5 -> x4, starting transfers between devices: 19.9 us -> 8.14 us  [from_behind(): return lax.ppermute(array, axis, pairs)]
    ppermute x0 -> x2, starting transfers between devices: none -> 9.2 us  [swap(): return lax.ppermute(array, 'half', [(0, 1), (1, 0)])]
    select_n x0 -> x3, other arithmetic: none -> 7.14 us  [the longest x1 3.36 us: finish(): mine_start = jnp.where(first, incoming_state, into_second)]
    unnamed x40 -> x38, local copies, waits for them, and re-layouts: 16.5 us -> 16.9 us
  transfers between devices with their start and end apart: 9 -> 10, of which waited for: 9 -> 10; matrix products, arithmetic and copies ran while one was open for 8% -> 11% of each run, Pallas kernels for 0% -> 0%
where the time goes in v5:
time: 482 us; the launch traced here: 480 us
  waiting for transfers between devices  247 us (51%)
  local copies, waits for them, and re-layouts  64.2 us (13%)
  blocking collectives  53 us (11%)
  other arithmetic  47.6 us (10%)
  matrix products  34.2 us (7%)
  starting transfers between devices  34 us (7%)
    ppermute x4, waiting for transfers between devices, from_behind(): return lax.ppermute(array, axis, pairs)  110 us
    ppermute x2, waiting for transfers between devices, swap(): return lax.ppermute(array, 'half', [(0, 1), (1, 0)])  74 us
    all_to_all x1, blocking collectives, finish(): lax.all_to_all(result, LANE, split_axis=1, concat_axis=1, tiled=True)  53 us
    all_to_all x1, waiting for transfers between devices, shards(): lax.all_to_all(signal, LANE, split_axis=1, concat_axis=0, tiled=True)  45.2 us
    unnamed x38, local copies, waits for them, and re-layouts  16.9 us
    dynamic_update_slice x4, other arithmetic, prepare(): lax.map(block_weights, (cumul, step_rate, input_groups, output_groups))  15.6 us
    dot_general x1, matrix products, finish(): jnp.einsum('khts,kshp->kthp', weights, values, preferred_element_type=jnp...  12.7 us
    dot_general x1, matrix products, finish(): jnp.einsum('ktgn,kgjpn->ktgjp', output_groups, rounded, preferred_element...  10.1 us
  transfers between devices with their start and end apart: 10, of which 10 were waited for; matrix products, arithmetic and copies ran while one was open for 11% of the time, Pallas kernels for 0%

profile of v5, /device:TPU:96, one launch (start us, length us, event | category | flops | bytes accessed | tf_op | source)
XLA Modules:
  0.0 480.3 jit_solution(13781041810551270130)
XLA Ops:
  1.6 4.3 all-to-all-start
  15.0 6.4 %copy.97 = bf16[128,16384]{0,1:T(8,128)(2,1)} copy(bf16[128,16384]{1,0:T(8,128)(2,1)} %param.10) | data formatting | bytes 8388608 | tf_op args[0]
  25.2 4.7 all-to-all-start.3
  34.4 45.2 %all-to-all-done.3 = bf16[128,8,2048]{0,2,1:T(8,128)(2,1)} async-done(((bf16[128,8,2048]{0,2,1:T(8,128)(2,1)}), bf16[128,8,2048]{0,2,1:T(8,128)(2,1)}, u32[]{:S(2)}, u32[]{:S(2)}) %all-to-all-start.3) | async-done | bytes 4194336 | tf_op jit(solution)/shard_map/all_to_all | solution.py:169
  79.6 6.2 %copy.98 = bf16[8,128,2048]{1,0,2:T(8,128)(2,1)} copy(bf16[8,128,2048]{1,2,0:T(8,128)(2,1)} %bitcast.14) | data formatting | bytes 8388608 | tf_op jit(solution)/shard_map/all_to_all | solution.py:169
  85.8 7.6 %reshape.248 = bf16[4,256,32,64]{1,0,3,2:T(4,128)(2,1)} reshape(bf16[8,128,2048]{1,0,2:T(8,128)(2,1)} %copy.98) | data formatting | bytes 8388608 | tf_op jit(solution)/shard_map/reshape | solution.py:53
  93.4 6.7 %fusion.16 = f32[4,32,64,256]{3,2,1,0:T(8,128)} fusion(bf16[4,256,256,1]{2,1,3,0:T(8,128)(2,1)S(1)} %bitcast.156, f32[4,256,32]{1,2,0:T(8,128)S(1)} %copy-done.9, bf16[4,256,32,64]{1,0,3,2:T(4,128)(2,1)} %reshape.248), kind=kOutput, calls=%fused_computation.26 | convolution fusion | flops 1080033280 | bytes 13238272 | tf_op jit(solution)/shard_map/ksgjp,ksgn->kgjpn/dot_general | solution.py:59
  100.1 14.2 %while.26 = (s32[]{:T(128)}, f32[32,64,256]{2,1,0:T(8,128)S(1)}, f32[4,32,64,256]{3,2,1,0:T(8,128)}, f32[4,32]{1,0:T(4,128)S(1)}, f32[4,32,64,256]{3,2,1,0:T(8,128)}, /*index=5*/s32[]{:T(128)}, s32[]{:T(128)}) while((s32[]{:T(128)}, f32[32,64,256]{2,1,0:T(8,128)S(1)}, f32[4,32,64,256]{3,2,1,0:T(8,128)}, f32[4,32]{1,0:T(4,128)S(1)}, ...), condition=%wide.region_5.6_spmd.clone, body=%wide.region_4.5_spmd.clone.sunk | while | flops 2097155 | bytes 10486252 | solution.py:70
  114.6 4.6 collective-permute-start
  119.1 39.4 %collective-permute-done = f32[1032,256]{1,0:T(8,128)} collective-permute-done((f32[1032,256]{1,0:T(8,128)S(1)}, f32[1032,256]{1,0:T(8,128)}, u32[]{:S(2)}, u32[]{:S(2)}) %collective-permute-start) | collective-permute-done | bytes 1056800 | tf_op jit(solution)/shard_map/ppermute | solution.py:93
  165.1 31.3 %collective-permute-done.1 = f32[1032,256]{1,0:T(8,128)S(1)} collective-permute-done((f32[1032,256]{1,0:T(8,128)S(1)}, f32[1032,256]{1,0:T(8,128)S(1)}, u32[]{:S(2)}, u32[]{:S(2)}) %collective-permute-start.1) | collective-permute-done | bytes 1056800 | tf_op jit(solution)/shard_map/ppermute | solution.py:20
  199.6 26.3 %collective-permute-done.2 = f32[1032,256]{1,0:T(8,128)S(1)} collective-permute-done((f32[1032,256]{1,0:T(8,128)S(1)}, f32[1032,256]{1,0:T(8,128)S(1)}, u32[]{:S(2)}, u32[]{:S(2)}) %collective-permute-start.2) | collective-permute-done | bytes 1056800 | tf_op jit(solution)/shard_map/ppermute | solution.py:20
  237.6 9.7 %all-to-all-done.1 = bf16[128,8,256]{0,2,1:T(8,128)(2,1)} async-done(((bf16[128,8,256]{0,2,1:T(8,128)(2,1)}), bf16[128,8,256]{0,2,1:T(8,128)(2,1)}, u32[]{:S(2)}, u32[]{:S(2)}) %all-to-all-start.1) | async-done | bytes 524320 | tf_op jit(solution)/shard_map/all_to_all | solution.py:171
  249.3 5.4 %collective-permute-done.3 = f32[1032,256]{1,0:T(8,128)} collective-permute-done((f32[1032,256]{1,0:T(8,128)}, f32[1032,256]{1,0:T(8,128)}, u32[]{:S(2)}, u32[]{:S(2)}) %collective-permute-start.3) | collective-permute-done | bytes 1056800 | tf_op jit(solution)/shard_map/ppermute | solution.py:20
  262.1 20.5 %while.25 = (s32[]{:T(128)}, bf16[4,32,256,256]{3,2,1,0:T(8,128)(2,1)}, f32[4,256,32]{1,2,0:T(8,128)S(1)}, bf16[4,256,1,256]{3,1,2,0:T(8,128)(2,1)}, bf16[4,256,...) while((s32[]{:T(128)}, bf16[4,32,256,256]{3,2,1,0:T(8,128)(2,1)}, ...), condition=%wide.region_3.4_spmd.clone.clone, body=%wide.region_2.3_spmd.clone.clone.sunk | while | flops 46202880 | bytes 5342301 | solution.py:45
  284.0 47.5 %collective-permute-done.4 = f32[1032,256]{1,0:T(8,128)} collective-permute-done((f32[1032,256]{1,0:T(8,128)}, f32[1032,256]{1,0:T(8,128)}, u32[]{:S(2)}, u32[]{:S(2)}) %collective-permute-start.4) | collective-permute-done | bytes 1056800 | tf_op jit(solution)/shard_map/ppermute | solution.py:20
  337.4 4.6 collective-permute-start.5
  342.1 12.7 %fusion.22 = f32[4,32,256,64]{2,3,1,0:T(8,128)} fusion(bf16[4,32,256,256]{3,2,1,0:T(8,128)(2,1)} %get-tuple-element.73, bf16[4,256,32,64]{1,0,3,2:T(4,128)(2,1)} %reshape.248), kind=kOutput, calls=%fused_computation.31 | convolution fusion | flops 1073741824 | bytes 29360128 | tf_op jit(solution)/shard_map/khts,kshp->kthp/dot_general | solution.py:55
  354.8 34.5 %collective-permute-done.5 = f32[16,64,256]{2,1,0:T(8,128)S(1)} collective-permute-done((f32[16,64,256]{2,1,0:T(8,128)}, f32[16,64,256]{2,1,0:T(8,128)S(1)}, u32[]{:S(2)}, u32[]{:S(2)}) %collective-permute-start.5) | collective-permute-done | bytes 1048608 | tf_op jit(solution)/shard_map/ppermute | solution.py:93
  392.9 10.1 %fusion.13 = bf16[4,256,32,64]{1,3,2,0:T(8,128)(2,1)} fusion(f32[4,32,256,64]{2,3,1,0:T(8,128)} %fusion.22, f32[32]{0:T(128)S(1)} %copy-done.14, f32[4,256,32]{1,2,0:T(8,128)S(1)} %get-tuple-element.185, bf16[4,256,32,64]{1,0,3,2:T(4,128)(2,1)} %reshape.248, bf16[4,256,256,1]{2,1,3,0:T(8,128)(2,1)S(1)} %bitcast.159, ...), kind=kOutput, calls=%fused_computation.21 | convolution fusion | flops 1092616192 | bytes 27918976 | tf_op jit(solution)/shard_map/ktgn,kgjpn->ktgjp/dot_general | solution.py:142
  403.0 8.1 %copy.104 = bf16[4,256,32,64]{1,0,3,2:T(4,128)(2,1)} copy(bf16[4,256,32,64]{1,3,2,0:T(8,128)(2,1)} %fusion.13) | data formatting | bytes 8388608 | tf_op jit(solution)/shard_map/convert_element_type | solution.py:148
  411.1 7.2 %reshape.262 = bf16[8,128,2048]{1,0,2:T(8,128)(2,1)} reshape(bf16[4,256,32,64]{1,0,3,2:T(4,128)(2,1)} %copy.104) | data formatting | bytes 8388608 | tf_op jit(solution)/shard_map/reshape | solution.py:150
  421.0 53.0 %all_to_all.66 = bf16[128,8,2048]{0,2,1:T(8,128)(2,1)} all-to-all(bf16[128,8,2048]{0,2,1:T(8,128)(2,1)S(1)} %copy.105), channel_id=1, replica_groups=mesh['chain'=16,'half'=2,'lane'=8] {'lane'}, dimensions={1} | all-to-all | bytes 8388608 | tf_op jit(solution)/shard_map/all_to_all | solution.py:151
  473.9 6.4 %copy.106 = bf16[128,16384]{1,0:T(8,128)(2,1)} copy(bf16[128,16384]{0,1:T(8,128)(2,1)} %bitcast.146) | data formatting | bytes 8388608 | tf_op jit(solution)/shard_map/reshape | solution.py:152
  (135 shorter events, 98.0 us)
Async XLA Ops:
  1.6 9.9 %all-to-all-start = ((bf16[128,8,32]{0,2,1:T(8,128)(2,1)}), bf16[128,8,32]{0,2,1:T(8,128)(2,1)S(1)}, u32[]{:S(2)}, u32[]{:S(2)}) async-start(bf16[128,8,32]{0,2,1:T(8,128)(2,1)} %bitcast), calls=%async_computation | async-start | bytes 131072 | tf_op jit(solution)/shard_map/all_to_all | solution.py:172
  11.5 13.7 %all-to-all-start.2 = ((bf16[128,8,256]{0,2,1:T(8,128)(2,1)}), bf16[128,8,256]{0,2,1:T(8,128)(2,1)S(1)}, u32[]{:S(2)}, u32[]{:S(2)}) async-start(bf16[128,8,256]{0,2,1:T(8,128)(2,1)} %bitcast.9), calls=%async_computation.2 | async-start | bytes 1048576 | tf_op jit(solution)/shard_map/all_to_all | solution.py:170
  25.2 4.7 copy-start.15
  25.2 54.3 %all-to-all-start.3 = ((bf16[128,8,2048]{0,2,1:T(8,128)(2,1)}), bf16[128,8,2048]{0,2,1:T(8,128)(2,1)}, u32[]{:S(2)}, u32[]{:S(2)}) async-start(bf16[128,8,2048]{0,2,1:T(8,128)(2,1)} %bitcast.144), calls=%async_computation.3 | async-start | bytes 8388608 | tf_op jit(solution)/shard_map/all_to_all | solution.py:169
  34.4 59.0 %copy-start.4 = (bf16[8,128,256]{2,1,0:T(8,128)(2,1)}, bf16[8,128,256]{2,1,0:T(8,128)(2,1)S(1)}, u32[]{:S(2)}) copy-start(bf16[8,128,256]{2,1,0:T(8,128)(2,1)S(1)} %copy.93) | copy-start | bytes 1572868
  85.8 7.6 %copy-start.9 = (f32[4,256,32]{1,2,0:T(8,128)S(1)}, f32[4,256,32]{1,2,0:T(8,128)}, u32[]{:S(2)}) copy-start(f32[4,256,32]{1,2,0:T(8,128)} %get-tuple-element.184) | copy-start | bytes 393220
  114.6 44.0 %collective-permute-start = (f32[1032,256]{1,0:T(8,128)S(1)}, f32[1032,256]{1,0:T(8,128)}, u32[]{:S(2)}, u32[]{:S(2)}) collective-permute-start(f32[1032,256]{1,0:T(8,128)S(1)} %pad_maximum_fusion), channel_id=1, source_target_pairs={{0,8},{8,0},{1,9},{9,1},{2,10},{10,2},{3,11},{11,3},{4,12},{12,4},... | collective-permute-start | bytes 3170312 | tf_op jit(solution)/shard_map/ppermute | solution.py:93
  161.6 34.9 %collective-permute-start.1 = (f32[1032,256]{1,0:T(8,128)S(1)}, f32[1032,256]{1,0:T(8,128)S(1)}, u32[]{:S(2)}, u32[]{:S(2)}) collective-permute-start(f32[1032,256]{1,0:T(8,128)S(1)} %pad_maximum_fusion.1), channel_id=1, source_target_pairs={{0,16},{16,32},{32,48},{48,64},{64,80},{80,96},{96,112},{112,128},... | collective-permute-start | bytes 3170312 | tf_op jit(solution)/shard_map/ppermute | solution.py:20
  197.4 29.7 %copy-start = (f32[1024,256]{1,0:T(8,128)}, f32[1024,256]{1,0:T(8,128)S(1)}, u32[]{:S(2)}) copy-start(f32[1024,256]{1,0:T(8,128)S(1)} %slice.55) | copy-start | bytes 3145732
  197.7 28.2 %collective-permute-start.2 = (f32[1032,256]{1,0:T(8,128)S(1)}, f32[1032,256]{1,0:T(8,128)S(1)}, u32[]{:S(2)}, u32[]{:S(2)}) collective-permute-start(f32[1032,256]{1,0:T(8,128)S(1)} %pad_maximum_fusion.2), channel_id=1, source_target_pairs={{0,32},{16,48},{32,64},{48,80},{64,96},{80,112},{96,128},{112,144}... | collective-permute-start | bytes 3170312 | tf_op jit(solution)/shard_map/ppermute | solution.py:20
  225.9 1.1 copy-start.8
  225.9 1.1 copy-start.10
  226.9 1.0 copy-start.1
  226.9 10.0 %copy-start.16 = (f32[256]{0:T(256)S(1)}, f32[256]{0:T(256)}, u32[]{:S(2)}) copy-start(f32[256]{0:T(256)} %param.15) | copy-start | bytes 3076
  227.1 1.1 copy-start.3
  229.3 29.0 %copy-start.11 = (f32[16]{0:T(128)S(1)}, f32[16]{0:T(128)}, u32[]{:S(2)}) copy-start(f32[16]{0:T(128)} %copy-done.10) | copy-start | bytes 196
  229.3 25.4 %collective-permute-start.3 = (f32[1032,256]{1,0:T(8,128)}, f32[1032,256]{1,0:T(8,128)}, u32[]{:S(2)}, u32[]{:S(2)}) collective-permute-start(f32[1032,256]{1,0:T(8,128)} %pad_maximum_fusion.3), channel_id=1, source_target_pairs={{0,64},{16,80},{32,96},{48,112},{64,128},{80,144},{96,160},{112,17... | collective-permute-start | bytes 3170312 | tf_op jit(solution)/shard_map/ppermute | solution.py:20
  232.7 14.5 %all-to-all-start.1 = ((bf16[128,8,256]{0,2,1:T(8,128)(2,1)}), bf16[128,8,256]{0,2,1:T(8,128)(2,1)}, u32[]{:S(2)}, u32[]{:S(2)}) async-start(bf16[128,8,256]{0,2,1:T(8,128)(2,1)} %bitcast.164), calls=%async_computation.1 | async-start | bytes 1048576 | tf_op jit(solution)/shard_map/all_to_all | solution.py:171
  260.8 70.8 %collective-permute-start.4 = (f32[1032,256]{1,0:T(8,128)}, f32[1032,256]{1,0:T(8,128)}, u32[]{:S(2)}, u32[]{:S(2)}) collective-permute-start(f32[1032,256]{1,0:T(8,128)} %pad_maximum_fusion.4), channel_id=1, source_target_pairs={{0,128},{16,144},{32,160},{48,176},{64,192},{80,208},{96,224},{112... | collective-permute-start | bytes 3170312 | tf_op jit(solution)/shard_map/ppermute | solution.py:20
  262.1 70.8 %copy-start.12 = (f32[16]{0:T(128)S(1)}, f32[16]{0:T(128)}, u32[]{:S(2)}) copy-start(f32[16]{0:T(128)} %get-tuple-element.176) | copy-start | bytes 196
  262.1 70.8 %copy-start.13 = (f32[16]{0:T(128)S(1)}, f32[16]{0:T(128)}, u32[]{:S(2)}) copy-start(f32[16]{0:T(128)} %get-tuple-element.177) | copy-start | bytes 196
  337.4 51.9 %collective-permute-start.5 = (f32[16,64,256]{2,1,0:T(8,128)}, f32[16,64,256]{2,1,0:T(8,128)S(1)}, u32[]{:S(2)}, u32[]{:S(2)}) collective-permute-start(f32[16,64,256]{2,1,0:T(8,128)} %fusion.24), channel_id=1, source_target_pairs={{0,8},{8,0},{1,9},{9,1},{2,10},{10,2},{3,11},{11,3},{4,12},{12,4},... | collective-permute-start | bytes 3145736 | tf_op jit(solution)/shard_map/ppermute | solution.py:93
  354.8 38.1 %copy-start.5 = (bf16[4,256,1,256]{3,1,2,0:T(8,128)(2,1)S(1)}, bf16[4,256,1,256]{3,1,2,0:T(8,128)(2,1)}, u32[]{:S(2)}) copy-start(bf16[4,256,1,256]{3,1,2,0:T(8,128)(2,1)} %get-tuple-element.303) | copy-start | bytes 1572868
  354.8 38.1 %copy-start.14 = (f32[32]{0:T(128)S(1)}, f32[32]{0:T(128)}, u32[]{:S(2)}) copy-start(f32[32]{0:T(128)} %dynamic_slice.49) | copy-start | bytes 388
  (3 other events, 2.9 us)

commit v6 on v5

--- a/solution.py
+++ b/solution.py
@@ -77,14 +77,20 @@
 
     def pack(decay, state):
         rows = state.shape[0] * CHANNEL_WIDTH
-        decay_row = jnp.broadcast_to(decay[None, :], (8, decay.shape[0]))
-        decay_row = jnp.pad(decay_row, ((0, 0), (0, SSTATE - decay.shape[0])))
-        return jnp.concatenate([state.reshape(rows, SSTATE), decay_row], axis=0)
+        high = decay.astype(jnp.bfloat16)
+        low = (decay - high.astype(jnp.float32)).astype(jnp.bfloat16)
+        decay_rows = jnp.broadcast_to(jnp.stack([high, low])[:, None, :], (2, 8, decay.shape[0]))
+        decay_rows = jnp.pad(decay_rows.reshape(16, -1), ((0, 0), (0, SSTATE - decay.shape[0])))
+        wire = state.reshape(rows, SSTATE).astype(jnp.bfloat16)
+        return jnp.concatenate([wire, decay_rows], axis=0)
 
     def unpack(packed, heads, decays):
         rows = heads * CHANNEL_WIDTH
-        state = packed[:rows].reshape(heads, CHANNEL_WIDTH, SSTATE)
-        return packed[rows, :decays], state
+        state = packed[:rows].reshape(heads, CHANNEL_WIDTH, SSTATE).astype(jnp.float32)
+        decay = packed[rows, :decays].astype(jnp.float32) + packed[rows + 8, :decays].astype(
+            jnp.float32
+        )
+        return decay, state
 
     def heads_of(array, which):
         return lax.dynamic_slice_in_dim(array, which * part, part)
@@ -129,7 +135,9 @@
     if half_count == 2:
         into_second = heads_of(first_decay, half)[:, None, None] * incoming_state + first_state
         mine_start = jnp.where(first, incoming_state, into_second)
-        other_start = swap(jnp.where(first, into_second, incoming_state))
+        other_start = swap(
+            jnp.where(first, into_second, incoming_state).astype(jnp.bfloat16)
+        ).astype(jnp.float32)
         incoming_state = jnp.where(
             first,
             jnp.concatenate([mine_start, other_start], axis=0),
@@ -147,9 +155,18 @@
     gain_heads = lax.dynamic_slice_in_dim(skip_gain, head_start, local_heads)
     result = (within + carried + gain_heads[:, None] * values_wide).astype(jnp.bfloat16)
     head_count = lax.axis_size(LANE)
-    result = result.reshape(head_count, -1, local_heads * CHANNEL_WIDTH).transpose(1, 0, 2)
-    result = lax.all_to_all(result, LANE, split_axis=1, concat_axis=1, tiled=True)
-    return result.reshape(result.shape[0], -1)
+    result = result.reshape(head_count, -1, local_heads * CHANNEL_WIDTH)
+    lane = lax.axis_index(LANE)
+    width = result.shape[2]
+    output = jnp.zeros((result.shape[1], head_count * width), result.dtype)
+    for shift in range(head_count):
+        piece = lax.dynamic_index_in_dim(result, (lane + shift) % head_count, keepdims=False)
+        if shift:
+            pairs = [(i, (i + shift) % head_count) for i in range(head_count)]
+            piece = lax.ppermute(piece, LANE, pairs)
+        source = (lane - shift) % head_count
+        output = lax.dynamic_update_slice_in_dim(output, piece, source * width, axis=1)
+    return output
 
 
 def shards(signal, input_map, output_map, step_size, decay_rate, skip_gain):
@@ -165,12 +182,22 @@
     output_rep = jnp.repeat(
         output_map.reshape(row_count, HEAD_GROUPS, SSTATE), copies, axis=1
     ).reshape(row_count, -1)
-    signal_c, input_c, output_c, step_c = (
-        lax.all_to_all(signal, LANE, split_axis=1, concat_axis=0, tiled=True),
-        lax.all_to_all(input_rep, LANE, split_axis=1, concat_axis=0, tiled=True),
-        lax.all_to_all(output_rep, LANE, split_axis=1, concat_axis=0, tiled=True),
-        lax.all_to_all(step_size, LANE, split_axis=1, concat_axis=0, tiled=True),
-    )
+    per_lane = [input_rep.shape[1] // head_count, output_rep.shape[1] // head_count]
+    per_lane.append(step_size.shape[1] // head_count)
+    side = jnp.concatenate(
+        [
+            input_rep.reshape(row_count, head_count, per_lane[0]),
+            output_rep.reshape(row_count, head_count, per_lane[1]),
+            step_size.reshape(row_count, head_count, per_lane[2]),
+        ],
+        axis=2,
+    )
+    side = lax.all_to_all(side, LANE, split_axis=1, concat_axis=0, tiled=True)
+    side = side.reshape(side.shape[0], -1)
+    input_c = side[:, : per_lane[0]]
+    output_c = side[:, per_lane[0] : per_lane[0] + per_lane[1]]
+    step_c = side[:, per_lane[0] + per_lane[1] :]
+    signal_c = lax.all_to_all(signal, LANE, split_axis=1, concat_axis=0, tiled=True)
     prepared = prepare(input_c, output_c, step_c, decay_rate, local_heads, group_count)
     return finish(signal_c, prepared, skip_gain, local_heads, group_count)
 

time: 482 us -> 378 us (0.78)
  waiting for transfers between devices: 247 us -> 143 us
  blocking collectives: 53 us -> 0 us
  local copies, waits for them, and re-layouts: 64.2 us -> 113 us
    ppermute x4, waiting for transfers between devices: 110 us -> 43.9 us  [from_behind(): return lax.ppermute(array, axis, pairs)]
    all_to_all x1 -> x0, blocking collectives: 53 us -> none  [finish(): lax.all_to_all(result, LANE, split_axis=1, concat_axis=1, tiled=True)]
    ppermute x2, waiting for transfers between devices: 74 us -> 31.1 us  [swap(): return lax.ppermute(array, 'half', [(0, 1), (1, 0)])]
    dynamic_slice x0 -> x9, local copies, waits for them, and re-layouts: none -> 42.7 us  [finish(): lax.dynamic_index_in_dim(result, (lane + shift) % head_count, keepdims=Fa...]
    ppermute x0 -> x7, waiting for transfers between devices: none -> 23.1 us  [finish(): piece = lax.ppermute(piece, LANE, pairs)]
    dynamic_update_slice x0 -> x8, local copies, waits for them, and re-layouts: none -> 10.9 us  [finish(): lax.dynamic_update_slice_in_dim(output, piece, source * width, axis=1)]
    all_to_all x1, waiting for transfers between devices: 45.2 us -> 35.1 us  [shards(): lax.all_to_all(signal, LANE, split_axis=1, concat_axis=0, tiled=True)]
    all_to_all x3 -> x1, starting transfers between devices: 11.9 us -> 4.3 us  [shards(): side = lax.all_to_all(side, LANE, split_axis=1, concat_axis=0, tiled=True)]
  transfers between devices with their start and end apart: 10 -> 15, of which waited for: 10 -> 13; matrix products, arithmetic and copies ran while one was open for 11% -> 24% of each run, Pallas kernels for 0% -> 0%
where the time goes in v6:
time: 378 us; the launch traced here: 372 us
  waiting for transfers between devices  143 us (38%)
  local copies, waits for them, and re-layouts  113 us (30%)
  other arithmetic  47.7 us (13%)
  matrix products  34.2 us (9%)
  starting transfers between devices  33.3 us (9%)
    ppermute x4, waiting for transfers between devices, from_behind(): return lax.ppermute(array, axis, pairs)  43.9 us
    dynamic_slice x9, local copies, waits for them, and re-layouts, finish(): lax.dynamic_index_in_dim(result, (lane + shift) % head_count, keepdims=Fa...  42.7 us
    all_to_all x1, waiting for transfers between devices, shards(): lax.all_to_all(signal, LANE, split_axis=1, concat_axis=0, tiled=True)  35.1 us
    ppermute x2, waiting for transfers between devices, swap(): return lax.ppermute(array, 'half', [(0, 1), (1, 0)])  31.1 us
    ppermute x7, waiting for transfers between devices, finish(): piece = lax.ppermute(piece, LANE, pairs)  23.1 us
    dynamic_update_slice x4, other arithmetic, prepare(): lax.map(block_weights, (cumul, step_rate, input_groups, output_groups))  15.3 us
    dot_general x1, matrix products, finish(): jnp.einsum('khts,kshp->kthp', weights, values, preferred_element_type=jnp...  12.7 us
    unnamed x25, local copies, waits for them, and re-layouts  12.6 us
  transfers between devices with their start and end apart: 15, of which 13 were waited for; matrix products, arithmetic and copies ran while one was open for 24% of the time, Pallas kernels for 0%

profile of v6, /device:TPU:96, one launch (start us, length us, event | category | flops | bytes accessed | tf_op | source)
XLA Modules:
  0.0 372.3 jit_solution(11981844737998150673)
XLA Ops:
  9.0 6.4 %copy.105 = bf16[128,16384]{0,1:T(8,128)(2,1)} copy(bf16[128,16384]{1,0:T(8,128)(2,1)} %param.10) | data formatting | bytes 8388608 | tf_op args[0]
  15.4 10.3 %all-to-all-done = bf16[128,8,544]{0,2,1:T(8,128)(2,1)S(1)} async-done(((bf16[128,8,544]{0,2,1:T(8,128)(2,1)}), bf16[128,8,544]{0,2,1:T(8,128)(2,1)S(1)}, u32[]{:S(2)}, u32[]{:S(2)}) %all-to-all-start) | async-done | bytes 1114144 | tf_op jit(solution)/shard_map/all_to_all | solution.py:195
  25.6 4.7 %all-to-all-start.1 = ((bf16[128,8,2048]{0,2,1:T(8,128)(2,1)}), bf16[128,8,2048]{0,2,1:T(8,128)(2,1)}, u32[]{:S(2)}, u32[]{:S(2)}) async-start(bf16[128,8,2048]{0,2,1:T(8,128)(2,1)} %bitcast.202), calls=%async_computation.1 | async-start | bytes 8388608 | tf_op jit(solution)/shard_map/all_to_all | solution.py:200
  44.9 35.1 %all-to-all-done.1 = bf16[128,8,2048]{0,2,1:T(8,128)(2,1)} async-done(((bf16[128,8,2048]{0,2,1:T(8,128)(2,1)}), bf16[128,8,2048]{0,2,1:T(8,128)(2,1)}, u32[]{:S(2)}, u32[]{:S(2)}) %all-to-all-start.1) | async-done | bytes 4194336 | tf_op jit(solution)/shard_map/all_to_all | solution.py:200
  80.0 6.2 %copy.106 = bf16[8,128,2048]{1,0,2:T(8,128)(2,1)} copy(bf16[8,128,2048]{1,2,0:T(8,128)(2,1)} %bitcast.13) | data formatting | bytes 8388608 | tf_op jit(solution)/shard_map/all_to_all | solution.py:200
  86.2 7.6 %reshape.323 = bf16[4,256,32,64]{1,0,3,2:T(4,128)(2,1)} reshape(bf16[8,128,2048]{1,0,2:T(8,128)(2,1)} %copy.106) | data formatting | bytes 8388608 | tf_op jit(solution)/shard_map/reshape | solution.py:53
  93.7 6.7 %fusion.16 = f32[4,32,64,256]{3,2,1,0:T(8,128)} fusion(bf16[4,256,256,1]{2,1,3,0:T(8,128)(2,1)S(1)} %bitcast.210, f32[4,256,32]{1,2,0:T(8,128)S(1)} %get-tuple-element.204, bf16[4,256,32,64]{1,0,3,2:T(4,128)(2,1)} %reshape.323), kind=kOutput, calls=%fused_computation.26 | convolution fusion | flops 1080033280 | bytes 13238272 | tf_op jit(solution)/shard_map/ksgjp,ksgn->kgjpn/dot_general | solution.py:59
  100.5 14.3 %while.26 = (s32[]{:T(128)}, f32[32,64,256]{2,1,0:T(8,128)S(1)}, f32[4,32,64,256]{3,2,1,0:T(8,128)}, f32[4,32]{1,0:T(4,128)S(1)}, f32[4,32,64,256]{3,2,1,0:T(8,128)}, /*index=5*/s32[]{:T(128)}, s32[]{:T(128)}) while((s32[]{:T(128)}, f32[32,64,256]{2,1,0:T(8,128)S(1)}, f32[4,32,64,256]{3,2,1,0:T(8,128)}, f32[4,32]{1,0:T(4,128)S(1)}, ...), condition=%wide.region_5.6_spmd.clone, body=%wide.region_4.5_spmd.clone.sunk | while | flops 2097155 | bytes 10486252 | solution.py:70
  114.9 4.6 %collective-permute-start = (bf16[1040,256]{1,0:T(8,128)(2,1)S(1)}, bf16[1040,256]{1,0:T(8,128)(2,1)S(1)}, u32[]{:S(2)}, u32[]{:S(2)}) collective-permute-start(bf16[1040,256]{1,0:T(8,128)(2,1)S(1)} %fusion.38), channel_id=1, source_target_pairs={{0,8},{8,0},{1,9},{9,1},{2,10},{10,2},{3,11},{11,3},{4,12},{12,4},... | collective-permute-start | bytes 1597448 | tf_op jit(solution)/shard_map/ppermute | solution.py:99
  119.4 19.2 %collective-permute-done = bf16[1040,256]{1,0:T(8,128)(2,1)S(1)} collective-permute-done((bf16[1040,256]{1,0:T(8,128)(2,1)S(1)}, bf16[1040,256]{1,0:T(8,128)(2,1)S(1)}, u32[]{:S(2)}, u32[]{:S(2)}) %collective-permute-start) | collective-permute-done | bytes 532512 | tf_op jit(solution)/shard_map/ppermute | solution.py:99
  142.6 17.8 %collective-permute-done.1 = bf16[1040,256]{1,0:T(8,128)(2,1)S(1)} collective-permute-done((bf16[1040,256]{1,0:T(8,128)(2,1)S(1)}, bf16[1040,256]{1,0:T(8,128)(2,1)S(1)}, u32[]{:S(2)}, u32[]{:S(2)}) %collective-permute-start.1) | collective-permute-done | bytes 532512 | tf_op jit(solution)/shard_map/ppermute | solution.py:20
  162.9 15.0 %collective-permute-done.2 = bf16[1040,256]{1,0:T(8,128)(2,1)S(1)} collective-permute-done((bf16[1040,256]{1,0:T(8,128)(2,1)S(1)}, bf16[1040,256]{1,0:T(8,128)(2,1)S(1)}, u32[]{:S(2)}, u32[]{:S(2)}) %collective-permute-start.2) | collective-permute-done | bytes 532512 | tf_op jit(solution)/shard_map/ppermute | solution.py:20
  184.5 10.5 %collective-permute-done.3 = bf16[1040,256]{1,0:T(8,128)(2,1)} collective-permute-done((bf16[1040,256]{1,0:T(8,128)(2,1)}, bf16[1040,256]{1,0:T(8,128)(2,1)}, u32[]{:S(2)}, u32[]{:S(2)}) %collective-permute-start.3) | collective-permute-done | bytes 532512 | tf_op jit(solution)/shard_map/ppermute | solution.py:20
  201.5 23.3 %while.25 = (s32[]{:T(128)}, bf16[4,32,256,256]{3,2,1,0:T(8,128)(2,1)}, f32[4,256,32]{1,2,0:T(8,128)}, bf16[4,256,1,256]{3,1,2,0:T(8,128)(2,1)}, bf16[4,256,1,25...) while((s32[]{:T(128)}, bf16[4,32,256,256]{3,2,1,0:T(8,128)(2,1)}, ...), condition=%wide.region_3.4_spmd.clone.clone, body=%wide.region_2.3_spmd.clone.clone.sunk | while | flops 46202880 | bytes 5342301 | solution.py:45
  229.6 4.7 %collective-permute-start.5 = (bf16[16,64,256]{2,1,0:T(8,128)(2,1)}, bf16[16,64,256]{2,1,0:T(8,128)(2,1)S(1)}, u32[]{:S(2)}, u32[]{:S(2)}) collective-permute-start(bf16[16,64,256]{2,1,0:T(8,128)(2,1)} %get-tuple-element.189), channel_id=1, source_target_pairs={{0,8},{8,0},{1,9},{9,1},{2,10},{10,2},{3,11},{11,3},{4,12},{12,4},... | collective-permute-start | bytes 1572872 | tf_op jit(solution)/shard_map/ppermute | solution.py:99
  234.3 12.7 %fusion.22 = f32[4,32,256,64]{2,3,1,0:T(8,128)} fusion(bf16[4,32,256,256]{3,2,1,0:T(8,128)(2,1)} %get-tuple-element.73, bf16[4,256,32,64]{1,0,3,2:T(4,128)(2,1)} %reshape.323), kind=kOutput, calls=%fused_computation.31 | convolution fusion | flops 1073741824 | bytes 29360128 | tf_op jit(solution)/shard_map/khts,kshp->kthp/dot_general | solution.py:55
  247.0 11.9 %collective-permute-done.5 = bf16[16,64,256]{2,1,0:T(8,128)(2,1)S(1)} collective-permute-done((bf16[16,64,256]{2,1,0:T(8,128)(2,1)}, bf16[16,64,256]{2,1,0:T(8,128)(2,1)S(1)}, u32[]{:S(2)}, u32[]{:S(2)}) %collective-permute-start.5) | collective-permute-done | bytes 524320 | tf_op jit(solution)/shard_map/ppermute | solution.py:99
  260.9 10.1 %fusion.13 = bf16[4,256,32,64]{1,3,2,0:T(8,128)(2,1)} fusion(f32[4,32,256,64]{2,3,1,0:T(8,128)} %fusion.22, f32[32]{0:T(128)S(1)} %dynamic_slice.74, f32[4,256,32]{1,2,0:T(8,128)S(1)} %copy-done.6, bf16[4,256,32,64]{1,0,3,2:T(4,128)(2,1)} %reshape.323, bf16[4,256,256,1]{2,1,3,0:T(8,128)(2,1)S(1)} %bitcast.213, f32[4,32,64,256]{3,2,1,0:T(8,128)} %get-tuple-element.74, ...), kind=kOutput, calls=%fused_computation.21 | convolution fusion | flops 1092616192 | bytes 27918976 | tf_op jit(solution)/shard_map/ktgn,kgjpn->ktgjp/dot_general | solution.py:150
  271.0 8.1 %copy.112 = bf16[4,256,32,64]{1,0,3,2:T(4,128)(2,1)} copy(bf16[4,256,32,64]{1,3,2,0:T(8,128)(2,1)} %fusion.13) | data formatting | bytes 8388608 | tf_op jit(solution)/shard_map/convert_element_type | solution.py:156
  279.1 7.2 %reshape.332 = bf16[8,128,2048]{1,0,2:T(8,128)(2,1)} reshape(bf16[4,256,32,64]{1,0,3,2:T(4,128)(2,1)} %copy.112) | data formatting | bytes 8388608 | tf_op jit(solution)/shard_map/reshape | solution.py:158
  286.2 21.8 %constant_dynamic-slice_fusion.1 = (bf16[1,128,2048]{1,0,2:T(2,128)(2,1)S(1)}, bf16[1,128,2048]{1,0,2:T(2,128)(2,1)S(1)}, bf16[1,128,2048]{1,0,2:T(2,128)(2,1)S(...) fusion(bf16[8,128,2048]{1,0,2:T(8,128)(2,1)} %reshape.332, ...), kind=kLoop, calls=%fused_computation.78 | loop fusion | bytes 8388640 | tf_op jit(solution)/shard_map/jit(dynamic_index_in_dim)/dynamic_slice | solution.py:163
  348.8 7.0 %collective-permute-done.9 = bf16[128,2048]{1,0:T(8,128)(2,1)} collective-permute-done((bf16[128,2048]{1,0:T(8,128)(2,1)}, bf16[128,2048]{1,0:T(8,128)(2,1)}, u32[]{:S(2)}, u32[]{:S(2)}) %collective-permute-start.9) | collective-permute-done | bytes 524320 | tf_op jit(solution)/shard_map/ppermute | solution.py:166
  360.3 5.4 %collective-permute-done.11 = bf16[128,2048]{1,0:T(8,128)(2,1)S(1)} collective-permute-done((bf16[128,2048]{1,0:T(8,128)(2,1)S(1)}, bf16[128,2048]{1,0:T(8,128)(2,1)S(1)}, u32[]{:S(2)}, u32[]{:S(2)}) %collective-permute-start.11) | collective-permute-done | bytes 524320 | tf_op jit(solution)/shard_map/ppermute | solution.py:166
  366.5 4.9 %collective-permute-done.12 = bf16[128,2048]{1,0:T(8,128)(2,1)S(1)} collective-permute-done((bf16[128,2048]{1,0:T(8,128)(2,1)S(1)}, bf16[128,2048]{1,0:T(8,128)(2,1)S(1)}, u32[]{:S(2)}, u32[]{:S(2)}) %collective-permute-start.12) | collective-permute-done | bytes 524320 | tf_op jit(solution)/shard_map/ppermute | solution.py:166
  (153 shorter events, 133.9 us)
Async XLA Ops:
  4.7 20.9 %all-to-all-start = ((bf16[128,8,544]{0,2,1:T(8,128)(2,1)}), bf16[128,8,544]{0,2,1:T(8,128)(2,1)S(1)}, u32[]{:S(2)}, u32[]{:S(2)}) async-start(bf16[128,8,544]{0,2,1:T(8,128)(2,1)} %pad_maximum_fusion), calls=%async_computation | async-start | bytes 2228224 | tf_op jit(solution)/shard_map/all_to_all | solution.py:195
  25.6 4.7 %copy-start.8 = (f32[256]{0:T(256)S(1)}, f32[256]{0:T(256)}, u32[]{:S(2)}) copy-start(f32[256]{0:T(256)} %param.14) | copy-start | bytes 3076
  25.6 54.3 %all-to-all-start.1 = ((bf16[128,8,2048]{0,2,1:T(8,128)(2,1)}), bf16[128,8,2048]{0,2,1:T(8,128)(2,1)}, u32[]{:S(2)}, u32[]{:S(2)}) async-start(bf16[128,8,2048]{0,2,1:T(8,128)(2,1)} %bitcast.202), calls=%async_computation.1 | async-start | bytes 8388608 | tf_op jit(solution)/shard_map/all_to_all | solution.py:200
  43.7 50.0 %copy-start.1 = (bf16[1024,256]{1,0:T(8,128)(2,1)}, bf16[1024,256]{1,0:T(8,128)(2,1)S(1)}, u32[]{:S(2)}) copy-start(bf16[1024,256]{1,0:T(8,128)(2,1)S(1)} %copy.101) | copy-start | bytes 1572868
  43.8 42.3 %copy-start.5 = (f32[4,256,32]{1,2,0:T(8,128)}, f32[4,256,32]{1,2,0:T(8,128)S(1)}, u32[]{:S(2)}) copy-start(f32[4,256,32]{1,2,0:T(8,128)S(1)} %bitcast_bitcast_fusion) | copy-start | bytes 393220
  114.9 23.7 %collective-permute-start = (bf16[1040,256]{1,0:T(8,128)(2,1)S(1)}, bf16[1040,256]{1,0:T(8,128)(2,1)S(1)}, u32[]{:S(2)}, u32[]{:S(2)}) collective-permute-start(bf16[1040,256]{1,0:T(8,128)(2,1)S(1)} %fusion.38), channel_id=1, source_target_pairs={{0,8},{8,0},{1,9},{9,1},{2,10},{10,2},{3,11},{11,3},{4,12},{12,4},... | collective-permute-start | bytes 1597448 | tf_op jit(solution)/shard_map/ppermute | solution.py:99
  139.2 21.3 %collective-permute-start.1 = (bf16[1040,256]{1,0:T(8,128)(2,1)S(1)}, bf16[1040,256]{1,0:T(8,128)(2,1)S(1)}, u32[]{:S(2)}, u32[]{:S(2)}) collective-permute-start(bf16[1040,256]{1,0:T(8,128)(2,1)S(1)} %fusion.39), channel_id=1, source_target_pairs={{0,16},{16,32},{32,48},{48,64},{64,80},{80,96},{96,112},{112,128},... | collective-permute-start | bytes 1597448 | tf_op jit(solution)/shard_map/ppermute | solution.py:20
  160.6 21.8 %copy-start.9 = (f32[256]{0:T(256)S(1)}, f32[256]{0:T(256)}, u32[]{:S(2)}) copy-start(f32[256]{0:T(256)} %param.15) | copy-start | bytes 3076
  161.0 16.9 %collective-permute-start.2 = (bf16[1040,256]{1,0:T(8,128)(2,1)S(1)}, bf16[1040,256]{1,0:T(8,128)(2,1)S(1)}, u32[]{:S(2)}, u32[]{:S(2)}) collective-permute-start(bf16[1040,256]{1,0:T(8,128)(2,1)S(1)} %fusion.40), channel_id=1, source_target_pairs={{0,32},{16,48},{32,64},{48,80},{64,96},{80,112},{96,128},{112,144}... | collective-permute-start | bytes 1597448 | tf_op jit(solution)/shard_map/ppermute | solution.py:20
  178.0 0.9 copy-start.7
  178.8 0.8 copy-start
  181.0 14.0 %collective-permute-start.3 = (bf16[1040,256]{1,0:T(8,128)(2,1)}, bf16[1040,256]{1,0:T(8,128)(2,1)}, u32[]{:S(2)}, u32[]{:S(2)}) collective-permute-start(bf16[1040,256]{1,0:T(8,128)(2,1)} %fusion.41), channel_id=1, source_target_pairs={{0,64},{16,80},{32,96},{48,112},{64,128},{80,144},{96,160},{112,17... | collective-permute-start | bytes 1597448 | tf_op jit(solution)/shard_map/ppermute | solution.py:20
  200.0 25.4 %collective-permute-start.4 = (bf16[1040,256]{1,0:T(8,128)(2,1)}, bf16[1040,256]{1,0:T(8,128)(2,1)}, u32[]{:S(2)}, u32[]{:S(2)}) collective-permute-start(bf16[1040,256]{1,0:T(8,128)(2,1)} %fusion.42), channel_id=1, source_target_pairs={{0,128},{16,144},{32,160},{48,176},{64,192},{80,208},{96,224},{112... | collective-permute-start | bytes 1597448 | tf_op jit(solution)/shard_map/ppermute | solution.py:20
  229.6 29.3 %collective-permute-start.5 = (bf16[16,64,256]{2,1,0:T(8,128)(2,1)}, bf16[16,64,256]{2,1,0:T(8,128)(2,1)S(1)}, u32[]{:S(2)}, u32[]{:S(2)}) collective-permute-start(bf16[16,64,256]{2,1,0:T(8,128)(2,1)} %get-tuple-element.189), channel_id=1, source_target_pairs={{0,8},{8,0},{1,9},{9,1},{2,10},{10,2},{3,11},{11,3},{4,12},{12,4},... | collective-permute-start | bytes 1572872 | tf_op jit(solution)/shard_map/ppermute | solution.py:99
  247.0 13.9 %copy-start.2 = (bf16[4,256,1,256]{3,1,2,0:T(8,128)(2,1)S(1)}, bf16[4,256,1,256]{3,1,2,0:T(8,128)(2,1)}, u32[]{:S(2)}) copy-start(bf16[4,256,1,256]{3,1,2,0:T(8,128)(2,1)} %get-tuple-element.322) | copy-start | bytes 1572868
  247.0 13.9 %copy-start.6 = (f32[4,256,32]{1,2,0:T(8,128)S(1)}, f32[4,256,32]{1,2,0:T(8,128)}, u32[]{:S(2)}) copy-start(f32[4,256,32]{1,2,0:T(8,128)} %get-tuple-element.205) | copy-start | bytes 393220
  311.6 26.3 %collective-permute-start.6 = (bf16[128,2048]{1,0:T(8,128)(2,1)}, bf16[128,2048]{1,0:T(8,128)(2,1)}, u32[]{:S(2)}, u32[]{:S(2)}) collective-permute-start(bf16[128,2048]{1,0:T(8,128)(2,1)} %bitcast.231), channel_id=1, source_target_pairs={{0,1},{1,2},{2,3},{3,4},{4,5},{5,6},{6,7},{7,0},{8,9},{9,10},{10,1... | collective-permute-start | bytes 1572872 | tf_op jit(solution)/shard_map/ppermute | solution.py:166
  318.7 22.3 %collective-permute-start.7 = (bf16[128,2048]{1,0:T(8,128)(2,1)}, bf16[128,2048]{1,0:T(8,128)(2,1)}, u32[]{:S(2)}, u32[]{:S(2)}) collective-permute-start(bf16[128,2048]{1,0:T(8,128)(2,1)} %bitcast.237), channel_id=1, source_target_pairs={{0,2},{1,3},{2,4},{3,5},{4,6},{5,7},{6,0},{7,1},{8,10},{9,11},{10,... | collective-permute-start | bytes 1572872 | tf_op jit(solution)/shard_map/ppermute | solution.py:166
  322.9 24.1 %collective-permute-start.8 = (bf16[128,2048]{1,0:T(8,128)(2,1)}, bf16[128,2048]{1,0:T(8,128)(2,1)}, u32[]{:S(2)}, u32[]{:S(2)}) collective-permute-start(bf16[128,2048]{1,0:T(8,128)(2,1)} %bitcast.235), channel_id=1, source_target_pairs={{0,3},{1,4},{2,5},{3,6},{4,7},{5,0},{6,1},{7,2},{8,11},{9,12},{10,... | collective-permute-start | bytes 1572872 | tf_op jit(solution)/shard_map/ppermute | solution.py:166
  327.8 28.1 %collective-permute-start.9 = (bf16[128,2048]{1,0:T(8,128)(2,1)}, bf16[128,2048]{1,0:T(8,128)(2,1)}, u32[]{:S(2)}, u32[]{:S(2)}) collective-permute-start(bf16[128,2048]{1,0:T(8,128)(2,1)} %bitcast.234), channel_id=1, source_target_pairs={{0,4},{1,5},{2,6},{3,7},{4,0},{5,1},{6,2},{7,3},{8,12},{9,13},{10,... | collective-permute-start | bytes 1572872 | tf_op jit(solution)/shard_map/ppermute | solution.py:166
  332.4 3.3 copy-start.4
  332.4 27.1 %collective-permute-start.10 = (bf16[128,2048]{1,0:T(8,128)(2,1)}, bf16[128,2048]{1,0:T(8,128)(2,1)S(1)}, u32[]{:S(2)}, u32[]{:S(2)}) collective-permute-start(bf16[128,2048]{1,0:T(8,128)(2,1)} %bitcast.233), channel_id=1, source_target_pairs={{0,5},{1,6},{2,7},{3,0},{4,1},{5,2},{6,3},{7,4},{8,13},{9,14},{10,... | collective-permute-start | bytes 1572872 | tf_op jit(solution)/shard_map/ppermute | solution.py:166
  337.9 27.8 %collective-permute-start.11 = (bf16[128,2048]{1,0:T(8,128)(2,1)S(1)}, bf16[128,2048]{1,0:T(8,128)(2,1)S(1)}, u32[]{:S(2)}, u32[]{:S(2)}) collective-permute-start(bf16[128,2048]{1,0:T(8,128)(2,1)S(1)} %bitcast.236), channel_id=1, source_target_pairs={{0,6},{1,7},{2,0},{3,1},{4,2},{5,3},{6,4},{7,5},{8,14},{9,15},{10,... | collective-permute-start | bytes 1572872 | tf_op jit(solution)/shard_map/ppermute | solution.py:166
  341.0 30.5 %collective-permute-start.12 = (bf16[128,2048]{1,0:T(8,128)(2,1)S(1)}, bf16[128,2048]{1,0:T(8,128)(2,1)S(1)}, u32[]{:S(2)}, u32[]{:S(2)}) collective-permute-start(bf16[128,2048]{1,0:T(8,128)(2,1)S(1)} %bitcast.232), channel_id=1, source_target_pairs={{0,7},{1,0},{2,1},{3,2},{4,3},{5,4},{6,5},{7,6},{8,15},{9,8},{10,9... | collective-permute-start | bytes 1572872 | tf_op jit(solution)/shard_map/ppermute | solution.py:166
  (1 other events, 0.8 us)

commit v7 on v6

--- a/solution.py
+++ b/solution.py
@@ -62,12 +62,15 @@
     fresh_state = fresh_state.reshape(blocks, local_heads, CHANNEL_WIDTH, SSTATE)
     block_ends = cumul[:, -1, :]
 
-    def carry_step(carry_state, pieces):
-        block_end, fresh_block = pieces
-        return (jnp.exp(block_end)[:, None, None] * carry_state + fresh_block, carry_state)
-
-    empty_state = jnp.zeros((local_heads, CHANNEL_WIDTH, SSTATE), jnp.float32)
-    final_state, starts = lax.scan(carry_step, empty_state, (block_ends, fresh_state))
+    order = jnp.arange(blocks)
+    later = order[:, None] > order[None, :]
+    after_sum = jnp.sum(jnp.where(later[:, :, None], block_ends[:, None, :], 0.0), axis=0)
+    final_state = jnp.sum(jnp.exp(after_sum)[:, :, None, None] * fresh_state, axis=0)
+    between = (order[None, :, None] > order[None, None, :]) & (order[:, None, None] > order[None, None, :])
+    between = between & (order[None, :, None] < order[:, None, None])
+    gap_sum = jnp.einsum("kij,ih->kjh", between.astype(jnp.float32), block_ends)
+    carry_weight = jnp.where(later[:, :, None], jnp.exp(gap_sum), 0.0)
+    starts = jnp.sum(carry_weight[:, :, :, None, None] * fresh_state[None], axis=1)
     before = jnp.cumsum(block_ends, axis=0) - block_ends
     totals = jnp.sum(block_ends, axis=0)
     chain_len = lax.axis_size("chain")
@@ -155,18 +158,9 @@
     gain_heads = lax.dynamic_slice_in_dim(skip_gain, head_start, local_heads)
     result = (within + carried + gain_heads[:, None] * values_wide).astype(jnp.bfloat16)
     head_count = lax.axis_size(LANE)
-    result = result.reshape(head_count, -1, local_heads * CHANNEL_WIDTH)
-    lane = lax.axis_index(LANE)
-    width = result.shape[2]
-    output = jnp.zeros((result.shape[1], head_count * width), result.dtype)
-    for shift in range(head_count):
-        piece = lax.dynamic_index_in_dim(result, (lane + shift) % head_count, keepdims=False)
-        if shift:
-            pairs = [(i, (i + shift) % head_count) for i in range(head_count)]
-            piece = lax.ppermute(piece, LANE, pairs)
-        source = (lane - shift) % head_count
-        output = lax.dynamic_update_slice_in_dim(output, piece, source * width, axis=1)
-    return output
+    result = result.reshape(head_count, -1, local_heads * CHANNEL_WIDTH).transpose(1, 0, 2)
+    result = lax.all_to_all(result, LANE, split_axis=1, concat_axis=1, tiled=True)
+    return result.reshape(result.shape[0], -1)
 
 
 def shards(signal, input_map, output_map, step_size, decay_rate, skip_gain):

time: 378 us -> 356 us (0.942)
  local copies, waits for them, and re-layouts: 113 us -> 59.9 us
  blocking collectives: 0 us -> 52.9 us
  waiting for transfers between devices: 143 us -> 136 us
  starting transfers between devices: 33.3 us -> 26.6 us
  other arithmetic: 47.7 us -> 42.8 us
    all_to_all x0 -> x1, blocking collectives: none -> 52.9 us  [finish(): lax.all_to_all(result, LANE, split_axis=1, concat_axis=1, tiled=True)]
    dynamic_slice x9 -> x0, local copies, waits for them, and re-layouts: 42.7 us -> none  [finish(): lax.dynamic_index_in_dim(result, (lane + shift) % head_count, keepdims=Fa...]
    ppermute x7 -> x0, waiting for transfers between devices: 23.1 us -> none  [finish(): piece = lax.ppermute(piece, LANE, pairs)]
    reduce_sum x0 -> x2, other arithmetic: none -> 11.4 us  [the longest x1 11.3 us: finish(): jnp.sum(carry_weight[:, :, :, None, None] * fresh_state[None], axis=1)]
    dynamic_update_slice x8 -> x0, local copies, waits for them, and re-layouts: 10.9 us -> none  [finish(): lax.dynamic_update_slice_in_dim(output, piece, source * width, axis=1)]
    ppermute x4, waiting for transfers between devices: 43.9 us -> 53.3 us  [from_behind(): return lax.ppermute(array, axis, pairs)]
    all_to_all x1, waiting for transfers between devices: 35.1 us -> 43 us  [shards(): lax.all_to_all(signal, LANE, split_axis=1, concat_axis=0, tiled=True)]
    add x4 -> x0, other arithmetic: 7.87 us -> none  [carry_step(): jnp.exp(block_end)[:, None, None] * carry_state + fresh_block]
  transfers between devices with their start and end apart: 15 -> 8, of which waited for: 13 -> 7; matrix products, arithmetic and copies ran while one was open for 24% -> 17% of each run, Pallas kernels for 0% -> 0%
where the time goes in v7:
time: 356 us; the launch traced here: 354 us
  waiting for transfers between devices  136 us (38%)
  local copies, waits for them, and re-layouts  59.9 us (17%)
  blocking collectives  52.9 us (15%)
  other arithmetic  42.8 us (12%)
  matrix products  34.8 us (10%)
  starting transfers between devices  26.6 us (7%)
    ppermute x4, waiting for transfers between devices, from_behind(): return lax.ppermute(array, axis, pairs)  53.3 us
    all_to_all x1, blocking collectives, finish(): lax.all_to_all(result, LANE, split_axis=1, concat_axis=1, tiled=True)  52.9 us
    all_to_all x1, waiting for transfers between devices, shards(): lax.all_to_all(signal, LANE, split_axis=1, concat_axis=0, tiled=True)  43 us
    ppermute x2, waiting for transfers between devices, swap(): return lax.ppermute(array, 'half', [(0, 1), (1, 0)])  29.7 us
    dynamic_update_slice x4, other arithmetic, prepare(): lax.map(block_weights, (cumul, step_rate, input_groups, output_groups))  15.3 us
    dot_general x1, matrix products, finish(): jnp.einsum('khts,kshp->kthp', weights, values, preferred_element_type=jnp...  12.7 us
    unnamed x33, local copies, waits for them, and re-layouts  11.8 us
    reduce_sum x1, other arithmetic, finish(): jnp.sum(carry_weight[:, :, :, None, None] * fresh_state[None], axis=1)  11.3 us
  transfers between devices with their start and end apart: 8, of which 7 were waited for; matrix products, arithmetic and copies ran while one was open for 17% of the time, Pallas kernels for 0%

profile of v7, /device:TPU:96, one launch (start us, length us, event | category | flops | bytes accessed | tf_op | source)
XLA Modules:
  0.0 353.8 jit_solution(10082425677681608570)
XLA Ops:
  4.7 4.3 %all-to-all-start = ((bf16[128,8,544]{0,2,1:T(8,128)(2,1)}), bf16[128,8,544]{0,2,1:T(8,128)(2,1)S(1)}, u32[]{:S(2)}, u32[]{:S(2)}) async-start(bf16[128,8,544]{0,2,1:T(8,128)(2,1)} %pad_maximum_fusion), calls=%async_computation | async-start | bytes 2228224 | tf_op jit(solution)/shard_map/all_to_all | solution.py:189
  9.0 6.4 %copy.121 = bf16[128,16384]{0,1:T(8,128)(2,1)} copy(bf16[128,16384]{1,0:T(8,128)(2,1)} %param.8) | data formatting | bytes 8388608 | tf_op args[0]
  15.3 10.3 %all-to-all-done = bf16[128,8,544]{0,2,1:T(8,128)(2,1)S(1)} async-done(((bf16[128,8,544]{0,2,1:T(8,128)(2,1)}), bf16[128,8,544]{0,2,1:T(8,128)(2,1)S(1)}, u32[]{:S(2)}, u32[]{:S(2)}) %all-to-all-start) | async-done | bytes 1114144 | tf_op jit(solution)/shard_map/all_to_all | solution.py:189
  25.6 4.7 %all-to-all-start.1 = ((bf16[128,8,2048]{0,2,1:T(8,128)(2,1)}), bf16[128,8,2048]{0,2,1:T(8,128)(2,1)}, u32[]{:S(2)}, u32[]{:S(2)}) async-start(bf16[128,8,2048]{0,2,1:T(8,128)(2,1)} %bitcast.195), calls=%async_computation.1 | async-start | bytes 8388608 | tf_op jit(solution)/shard_map/all_to_all | solution.py:194
  37.0 43.0 %all-to-all-done.1 = bf16[128,8,2048]{0,2,1:T(8,128)(2,1)} async-done(((bf16[128,8,2048]{0,2,1:T(8,128)(2,1)}), bf16[128,8,2048]{0,2,1:T(8,128)(2,1)}, u32[]{:S(2)}, u32[]{:S(2)}) %all-to-all-start.1) | async-done | bytes 4194336 | tf_op jit(solution)/shard_map/all_to_all | solution.py:194
  80.0 6.2 %copy.122 = bf16[8,128,2048]{1,0,2:T(8,128)(2,1)} copy(bf16[8,128,2048]{1,2,0:T(8,128)(2,1)} %bitcast.13) | data formatting | bytes 8388608 | tf_op jit(solution)/shard_map/all_to_all | solution.py:194
  86.1 7.6 %reshape.379 = bf16[4,256,32,64]{1,0,3,2:T(4,128)(2,1)} reshape(bf16[8,128,2048]{1,0,2:T(8,128)(2,1)} %copy.122) | data formatting | bytes 8388608 | tf_op jit(solution)/shard_map/reshape | solution.py:53
  93.7 7.1 %multiply_reduce_fusion.1 = (f32[32,64,256]{2,1,0:T(8,128)S(1)}, f32[4,32,64,256]{3,2,1,0:T(8,128)}) fusion(f32[4,32]{1,0:T(4,128)S(1)} %exp.54, bf16[4,256,256,1]{2,1,3,0:T(8,128)(2,1)S(1)} %bitcast.205, f32[4,256,32]{1,2,0:T(8,128)S(1)} %get-tuple-element.144, bf16[4,256,32,64]{1,0,3,2:T(4,128)(2,1)} %reshape.379), kind=kOutput, calls=%fused_computation.21 | convolution fusion | flops 1083703296 | bytes 15335936 | tf_op jit(solution)/shard_map/ksgjp,ksgn->kgjpn/dot_general | solution.py:59
  100.9 4.6 %collective-permute-start = (bf16[1040,256]{1,0:T(8,128)(2,1)S(1)}, bf16[1040,256]{1,0:T(8,128)(2,1)}, u32[]{:S(2)}, u32[]{:S(2)}) collective-permute-start(bf16[1040,256]{1,0:T(8,128)(2,1)S(1)} %fusion.37), channel_id=1, source_target_pairs={{0,8},{8,0},{1,9},{9,1},{2,10},{10,2},{3,11},{11,3},{4,12},{12,4},... | collective-permute-start | bytes 1597448 | tf_op jit(solution)/shard_map/ppermute | solution.py:102
  105.5 19.2 %collective-permute-done = bf16[1040,256]{1,0:T(8,128)(2,1)} collective-permute-done((bf16[1040,256]{1,0:T(8,128)(2,1)S(1)}, bf16[1040,256]{1,0:T(8,128)(2,1)}, u32[]{:S(2)}, u32[]{:S(2)}) %collective-permute-start) | collective-permute-done | bytes 532512 | tf_op jit(solution)/shard_map/ppermute | solution.py:102
  131.1 17.9 %collective-permute-done.1 = bf16[1040,256]{1,0:T(8,128)(2,1)S(1)} collective-permute-done((bf16[1040,256]{1,0:T(8,128)(2,1)S(1)}, bf16[1040,256]{1,0:T(8,128)(2,1)S(1)}, u32[]{:S(2)}, u32[]{:S(2)}) %collective-permute-start.1) | collective-permute-done | bytes 532512 | tf_op jit(solution)/shard_map/ppermute | solution.py:20
  156.0 11.9 %collective-permute-done.2 = bf16[1040,256]{1,0:T(8,128)(2,1)} collective-permute-done((bf16[1040,256]{1,0:T(8,128)(2,1)}, bf16[1040,256]{1,0:T(8,128)(2,1)}, u32[]{:S(2)}, u32[]{:S(2)}) %collective-permute-start.2) | collective-permute-done | bytes 532512 | tf_op jit(solution)/shard_map/ppermute | solution.py:20
  173.1 20.3 %while.12 = (s32[]{:T(128)}, bf16[4,32,256,256]{3,2,1,0:T(8,128)(2,1)}, f32[4,256,32]{1,2,0:T(8,128)S(1)}, bf16[4,256,1,256]{3,1,2,0:T(8,128)(2,1)}, bf16[4,256,...) while((s32[]{:T(128)}, bf16[4,32,256,256]{3,2,1,0:T(8,128)(2,1)}, ...), condition=%wide.region_3.4_spmd.clone.clone, body=%wide.region_2.3_spmd.clone.clone.sunk | while | flops 46202880 | bytes 5342301 | solution.py:45
  174.4 3.9 %fusion.85 = bf16[4,32,256,256]{3,2,1,0:T(8,128)(2,1)} fusion(bf16[4,32,256,256]{3,2,1,0:T(8,128)(2,1)} %get-tuple-element.199, s32[]{:T(128)S(6)} %copy.162, f32[32,256]{1,0:T(8,128)S(1)} %get-tuple-element.189, f32[256,256]{1,0:T(8,128)S(1)} %fusion.84, f32[32,256]{1,0:T(8,128)S(1)} %get-tuple-element.190, pred[256,256]{1,0:T(8,128)(4,1)S(1)} %iota_compare_fusion.5), kind=kLoop, calls=%fused_computation.2.clone.1 | loop fusion | flops 12582912 | bytes 4620292 | tf_op jit(solution)/shard_map/while/body/jit(dynamic_update_index_in_dim)/dynamic_update_slice | solution.py:45
  200.2 12.7 %fusion.20 = f32[4,32,256,64]{2,3,1,0:T(8,128)} fusion(bf16[4,32,256,256]{3,2,1,0:T(8,128)(2,1)} %get-tuple-element.45, bf16[4,256,32,64]{1,0,3,2:T(4,128)(2,1)} %reshape.379), kind=kOutput, calls=%fused_computation.28 | convolution fusion | flops 1073741824 | bytes 29360128 | tf_op jit(solution)/shard_map/khts,kshp->kthp/dot_general | solution.py:55
  213.0 23.5 %collective-permute-done.4 = bf16[1040,256]{1,0:T(8,128)(2,1)} collective-permute-done((bf16[1040,256]{1,0:T(8,128)(2,1)}, bf16[1040,256]{1,0:T(8,128)(2,1)}, u32[]{:S(2)}, u32[]{:S(2)}) %collective-permute-start.4) | collective-permute-done | bytes 532512 | tf_op jit(solution)/shard_map/ppermute | solution.py:20
  239.5 4.9 %collective-permute-start.5 = (bf16[16,64,256]{2,1,0:T(8,128)(2,1)S(1)}, bf16[16,64,256]{2,1,0:T(8,128)(2,1)S(1)}, u32[]{:S(2)}, u32[]{:S(2)}) collective-permute-start(bf16[16,64,256]{2,1,0:T(8,128)(2,1)S(1)} %get-tuple-element.137), channel_id=1, source_target_pairs={{0,8},{8,0},{1,9},{9,1},{2,10},{10,2},{3,11},{11,3},{4,12},{12,4},... | collective-permute-start | bytes 1572872 | tf_op jit(solution)/shard_map/ppermute | solution.py:102
  244.4 11.3 %multiply_reduce_fusion = f32[4,32,64,256]{3,2,1,0:T(8,128)} fusion(f32[4,32,64,256]{3,2,1,0:T(8,128)} %get-tuple-element.147, f32[4,4,32]{2,1,0:T(4,128)S(1)} %fusion.22), kind=kLoop, calls=%fused_computation.12 | loop fusion | flops 14680064 | bytes 16779264 | tf_op jit(solution)/shard_map/reduce_sum | solution.py:73
  255.7 10.4 %collective-permute-done.5 = bf16[16,64,256]{2,1,0:T(8,128)(2,1)S(1)} collective-permute-done((bf16[16,64,256]{2,1,0:T(8,128)(2,1)S(1)}, bf16[16,64,256]{2,1,0:T(8,128)(2,1)S(1)}, u32[]{:S(2)}, u32[]{:S(2)}) %collective-permute-start.5) | collective-permute-done | bytes 524320 | tf_op jit(solution)/shard_map/ppermute | solution.py:102
  266.5 10.1 %fusion.11 = bf16[4,256,32,64]{1,3,2,0:T(8,128)(2,1)} fusion(f32[4,32,256,64]{2,3,1,0:T(8,128)} %fusion.20, f32[32]{0:T(128)S(1)} %copy-done.6, f32[4,256,32]{1,2,0:T(8,128)S(1)} %copy-done.4, bf16[4,256,32,64]{1,0,3,2:T(4,128)(2,1)} %reshape.379, bf16[4,256,256,1]{2,1,3,0:T(8,128)(2,1)S(1)} %bitcast.208, f32[4,32,64,256]{3,2,1,0:T(8,128)} %multiply_reduce_fusion, ...), kind=kOutput, calls=%fused_computation.17 | convolution fusion | flops 1092616192 | bytes 27918976 | tf_op jit(solution)/shard_map/ktgn,kgjpn->ktgjp/dot_general | solution.py:153
  276.5 8.1 %copy.129 = bf16[4,256,32,64]{1,0,3,2:T(4,128)(2,1)} copy(bf16[4,256,32,64]{1,3,2,0:T(8,128)(2,1)} %fusion.11) | data formatting | bytes 8388608 | tf_op jit(solution)/shard_map/convert_element_type | solution.py:159
  284.6 7.2 %reshape.388 = bf16[8,128,2048]{1,0,2:T(8,128)(2,1)} reshape(bf16[4,256,32,64]{1,0,3,2:T(4,128)(2,1)} %copy.129) | data formatting | bytes 8388608 | tf_op jit(solution)/shard_map/reshape | solution.py:161
  294.5 52.9 %all_to_all.36 = bf16[128,8,2048]{0,2,1:T(8,128)(2,1)} all-to-all(bf16[128,8,2048]{0,2,1:T(8,128)(2,1)S(1)} %copy.130), channel_id=1, replica_groups=mesh['chain'=16,'half'=2,'lane'=8] {'lane'}, dimensions={1} | all-to-all | bytes 8388608 | tf_op jit(solution)/shard_map/all_to_all | solution.py:162
  347.5 6.4 %copy.131 = bf16[128,16384]{1,0:T(8,128)(2,1)} copy(bf16[128,16384]{0,1:T(8,128)(2,1)} %bitcast.197) | data formatting | bytes 8388608 | tf_op jit(solution)/shard_map/reshape | solution.py:163
  (123 shorter events, 58.9 us)
Async XLA Ops:
  4.7 20.9 %all-to-all-start = ((bf16[128,8,544]{0,2,1:T(8,128)(2,1)}), bf16[128,8,544]{0,2,1:T(8,128)(2,1)S(1)}, u32[]{:S(2)}, u32[]{:S(2)}) async-start(bf16[128,8,544]{0,2,1:T(8,128)(2,1)} %pad_maximum_fusion), calls=%async_computation | async-start | bytes 2228224 | tf_op jit(solution)/shard_map/all_to_all | solution.py:189
  25.6 4.7 %copy-start.10 = (f32[256]{0:T(256)S(1)}, f32[256]{0:T(256)}, u32[]{:S(2)}) copy-start(f32[256]{0:T(256)} %param.12) | copy-start | bytes 3076
  25.6 54.3 %all-to-all-start.1 = ((bf16[128,8,2048]{0,2,1:T(8,128)(2,1)}), bf16[128,8,2048]{0,2,1:T(8,128)(2,1)}, u32[]{:S(2)}, u32[]{:S(2)}) async-start(bf16[128,8,2048]{0,2,1:T(8,128)(2,1)} %bitcast.195), calls=%async_computation.1 | async-start | bytes 8388608 | tf_op jit(solution)/shard_map/all_to_all | solution.py:194
  30.9 121.7 %copy-start.7 = (pred[4,4]{1,0:T(4,128)(4,1)}, pred[4,4]{1,0:T(4,128)(4,1)S(1)}, u32[]{:S(2)}) copy-start(pred[4,4]{1,0:T(4,128)(4,1)S(1)} %get-tuple-element.149) | copy-start | bytes 52
  35.7 58.0 %copy-start.1 = (bf16[1024,256]{1,0:T(8,128)(2,1)}, bf16[1024,256]{1,0:T(8,128)(2,1)S(1)}, u32[]{:S(2)}) copy-start(bf16[1024,256]{1,0:T(8,128)(2,1)S(1)} %copy.117) | copy-start | bytes 1572868
  100.9 23.8 %collective-permute-start = (bf16[1040,256]{1,0:T(8,128)(2,1)S(1)}, bf16[1040,256]{1,0:T(8,128)(2,1)}, u32[]{:S(2)}, u32[]{:S(2)}) collective-permute-start(bf16[1040,256]{1,0:T(8,128)(2,1)S(1)} %fusion.37), channel_id=1, source_target_pairs={{0,8},{8,0},{1,9},{9,1},{2,10},{10,2},{3,11},{11,3},{4,12},{12,4},... | collective-permute-start | bytes 1597448 | tf_op jit(solution)/shard_map/ppermute | solution.py:102
  127.2 26.1 %copy-start.11 = (f32[256]{0:T(256)S(1)}, f32[256]{0:T(256)}, u32[]{:S(2)}) copy-start(f32[256]{0:T(256)} %param.13) | copy-start | bytes 3076
  127.6 21.3 %collective-permute-start.1 = (bf16[1040,256]{1,0:T(8,128)(2,1)S(1)}, bf16[1040,256]{1,0:T(8,128)(2,1)S(1)}, u32[]{:S(2)}, u32[]{:S(2)}) collective-permute-start(bf16[1040,256]{1,0:T(8,128)(2,1)S(1)} %fusion.38), channel_id=1, source_target_pairs={{0,16},{16,32},{32,48},{48,64},{64,80},{80,96},{96,112},{112,128},... | collective-permute-start | bytes 1597448 | tf_op jit(solution)/shard_map/ppermute | solution.py:20
  150.7 17.3 %collective-permute-start.2 = (bf16[1040,256]{1,0:T(8,128)(2,1)}, bf16[1040,256]{1,0:T(8,128)(2,1)}, u32[]{:S(2)}, u32[]{:S(2)}) collective-permute-start(bf16[1040,256]{1,0:T(8,128)(2,1)} %fusion.39), channel_id=1, source_target_pairs={{0,32},{16,48},{32,64},{48,80},{64,96},{80,112},{96,128},{112,144}... | collective-permute-start | bytes 1597448 | tf_op jit(solution)/shard_map/ppermute | solution.py:20
  169.7 0.8 copy-start
  171.8 21.9 %collective-permute-start.3 = (bf16[1040,256]{1,0:T(8,128)(2,1)}, bf16[1040,256]{1,0:T(8,128)(2,1)}, u32[]{:S(2)}, u32[]{:S(2)}) collective-permute-start(bf16[1040,256]{1,0:T(8,128)(2,1)} %fusion.40), channel_id=1, source_target_pairs={{0,64},{16,80},{32,96},{48,112},{64,128},{80,144},{96,160},{112,17... | collective-permute-start | bytes 1597448 | tf_op jit(solution)/shard_map/ppermute | solution.py:20
  173.1 20.4 %copy-start.8 = (pred[4,4]{1,0:T(4,128)(4,1)S(1)}, pred[4,4]{1,0:T(4,128)(4,1)}, u32[]{:S(2)}) copy-start(pred[4,4]{1,0:T(4,128)(4,1)} %copy-done.7) | copy-start | bytes 52
  173.1 20.4 %copy-start.12 = (pred[4,4]{1,0:T(4,128)(4,1)S(1)}, pred[4,4]{1,0:T(4,128)(4,1)}, u32[]{:S(2)}) copy-start(pred[4,4]{1,0:T(4,128)(4,1)} %get-tuple-element.148) | copy-start | bytes 52
  173.1 20.3 %copy-start.13 = (pred[4,4]{0,1:T(4,128)(4,1)S(1)}, pred[4,4]{0,1:T(4,128)(4,1)}, u32[]{:S(2)}) copy-start(pred[4,4]{0,1:T(4,128)(4,1)} %copy.124) | copy-start | bytes 52
  173.1 20.6 %copy-start.5 = (f32[16]{0:T(128)S(1)}, f32[16]{0:T(128)}, u32[]{:S(2)}) copy-start(f32[16]{0:T(128)} %get-tuple-element.128) | copy-start | bytes 196
  195.5 0.8 copy-start.3
  198.8 37.7 %collective-permute-start.4 = (bf16[1040,256]{1,0:T(8,128)(2,1)}, bf16[1040,256]{1,0:T(8,128)(2,1)}, u32[]{:S(2)}, u32[]{:S(2)}) collective-permute-start(bf16[1040,256]{1,0:T(8,128)(2,1)} %fusion.41), channel_id=1, source_target_pairs={{0,128},{16,144},{32,160},{48,176},{64,192},{80,208},{96,224},{112... | collective-permute-start | bytes 1597448 | tf_op jit(solution)/shard_map/ppermute | solution.py:20
  200.2 12.7 %copy-start.9 = (f32[32]{0:T(128)S(1)}, f32[32]{0:T(128)}, u32[]{:S(2)}) copy-start(f32[32]{0:T(128)} %get-tuple-element.133) | copy-start | bytes 388
  239.5 26.6 %collective-permute-start.5 = (bf16[16,64,256]{2,1,0:T(8,128)(2,1)S(1)}, bf16[16,64,256]{2,1,0:T(8,128)(2,1)S(1)}, u32[]{:S(2)}, u32[]{:S(2)}) collective-permute-start(bf16[16,64,256]{2,1,0:T(8,128)(2,1)S(1)} %get-tuple-element.137), channel_id=1, source_target_pairs={{0,8},{8,0},{1,9},{9,1},{2,10},{10,2},{3,11},{11,3},{4,12},{12,4},... | collective-permute-start | bytes 1572872 | tf_op jit(solution)/shard_map/ppermute | solution.py:102
  255.7 10.8 %copy-start.2 = (bf16[4,256,1,256]{3,1,2,0:T(8,128)(2,1)S(1)}, bf16[4,256,1,256]{3,1,2,0:T(8,128)(2,1)}, u32[]{:S(2)}) copy-start(bf16[4,256,1,256]{3,1,2,0:T(8,128)(2,1)} %get-tuple-element.214) | copy-start | bytes 1572868
  255.7 10.8 %copy-start.4 = (f32[4,256,32]{1,2,0:T(8,128)S(1)}, f32[4,256,32]{1,2,0:T(8,128)}, u32[]{:S(2)}) copy-start(f32[4,256,32]{1,2,0:T(8,128)} %get-tuple-element.145) | copy-start | bytes 393220
  255.7 10.8 %copy-start.6 = (f32[32]{0:T(128)S(1)}, f32[32]{0:T(128)}, u32[]{:S(2)}) copy-start(f32[32]{0:T(128)} %dynamic_slice.41) | copy-start | bytes 388

commit v8 on v6

--- a/solution.py
+++ b/solution.py
@@ -155,18 +155,12 @@
     gain_heads = lax.dynamic_slice_in_dim(skip_gain, head_start, local_heads)
     result = (within + carried + gain_heads[:, None] * values_wide).astype(jnp.bfloat16)
     head_count = lax.axis_size(LANE)
-    result = result.reshape(head_count, -1, local_heads * CHANNEL_WIDTH)
-    lane = lax.axis_index(LANE)
-    width = result.shape[2]
-    output = jnp.zeros((result.shape[1], head_count * width), result.dtype)
-    for shift in range(head_count):
-        piece = lax.dynamic_index_in_dim(result, (lane + shift) % head_count, keepdims=False)
-        if shift:
-            pairs = [(i, (i + shift) % head_count) for i in range(head_count)]
-            piece = lax.ppermute(piece, LANE, pairs)
-        source = (lane - shift) % head_count
-        output = lax.dynamic_update_slice_in_dim(output, piece, source * width, axis=1)
-    return output
+    parts = []
+    for piece in jnp.split(result, 2, axis=2):
+        piece = piece.reshape(head_count, -1, piece.shape[2] * CHANNEL_WIDTH).transpose(1, 0, 2)
+        parts.append(lax.all_to_all(piece, LANE, split_axis=1, concat_axis=1, tiled=True))
+    result = jnp.concatenate(parts, axis=2)
+    return result.reshape(result.shape[0], -1)
 
 
 def shards(signal, input_map, output_map, step_size, decay_rate, skip_gain):

time: 378 us -> 356 us (0.942)
  local copies, waits for them, and re-layouts: 113 us -> 67.6 us
  blocking collectives: 0 us -> 29.6 us
    dynamic_slice x9 -> x0, local copies, waits for them, and re-layouts: 42.7 us -> none  [finish(): lax.dynamic_index_in_dim(result, (lane + shift) % head_count, keepdims=Fa...]
    all_to_all x0 -> x1, blocking collectives: none -> 29.6 us  [finish(): lax.all_to_all(piece, LANE, split_axis=1, concat_axis=1, tiled=True)]
    ppermute x7 -> x0, waiting for transfers between devices: 23.1 us -> none  [finish(): piece = lax.ppermute(piece, LANE, pairs)]
    all_to_all x0 -> x1, waiting for transfers between devices: none -> 19.7 us  [finish(): lax.all_to_all(piece, LANE, split_axis=1, concat_axis=1, tiled=True)]
    dynamic_update_slice x8 -> x0, local copies, waits for them, and re-layouts: 10.9 us -> none  [finish(): lax.dynamic_update_slice_in_dim(output, piece, source * width, axis=1)]
    split x0 -> x3, local copies, waits for them, and re-layouts: none -> 9.23 us  [finish(): jnp.split(result, 2, axis=2)]
    convert_element_type x1 -> x0, local copies, waits for them, and re-layouts: 8.09 us -> none  [finish(): (within + carried + gain_heads[:, None] * values_wide).astype(jnp.bfloat16)]
    ppermute x7 -> x0, starting transfers between devices: 6.85 us -> none  [finish(): piece = lax.ppermute(piece, LANE, pairs)]
  transfers between devices with their start and end apart: 15 -> 9, of which waited for: 13 -> 9; matrix products, arithmetic and copies ran while one was open for 24% -> 19% of each run, Pallas kernels for 0% -> 0%
where the time goes in v8:
time: 356 us; the launch traced here: 353 us
  waiting for transfers between devices  140 us (39%)
  local copies, waits for them, and re-layouts  67.6 us (19%)
  other arithmetic  49.8 us (14%)
  matrix products  34.1 us (10%)
  starting transfers between devices  30.8 us (9%)
  blocking collectives  29.6 us (8%)
    ppermute x4, waiting for transfers between devices, from_behind(): return lax.ppermute(array, axis, pairs)  43.9 us
    all_to_all x1, waiting for transfers between devices, shards(): lax.all_to_all(signal, LANE, split_axis=1, concat_axis=0, tiled=True)  35.1 us
    ppermute x2, waiting for transfers between devices, swap(): return lax.ppermute(array, 'half', [(0, 1), (1, 0)])  31.1 us
    all_to_all x1, blocking collectives, finish(): lax.all_to_all(piece, LANE, split_axis=1, concat_axis=1, tiled=True)  29.6 us
    all_to_all x1, waiting for transfers between devices, finish(): lax.all_to_all(piece, LANE, split_axis=1, concat_axis=1, tiled=True)  19.7 us
    dynamic_update_slice x4, other arithmetic, prepare(): lax.map(block_weights, (cumul, step_rate, input_groups, output_groups))  15.4 us
    unnamed x25, local copies, waits for them, and re-layouts  13.5 us
    dot_general x1, matrix products, finish(): jnp.einsum('khts,kshp->kthp', weights, values, preferred_element_type=jnp...  12.7 us
  transfers between devices with their start and end apart: 9, of which 9 were waited for; matrix products, arithmetic and copies ran while one was open for 19% of the time, Pallas kernels for 0%

profile of v8, /device:TPU:96, one launch (start us, length us, event | category | flops | bytes accessed | tf_op | source)
XLA Modules:
  0.0 352.6 jit_solution(2914376831834950873)
XLA Ops:
  4.7 4.3 %all-to-all-start = ((bf16[128,8,544]{0,2,1:T(8,128)(2,1)}), bf16[128,8,544]{0,2,1:T(8,128)(2,1)S(1)}, u32[]{:S(2)}, u32[]{:S(2)}) async-start(bf16[128,8,544]{0,2,1:T(8,128)(2,1)} %pad_maximum_fusion.1), calls=%async_computation | async-start | bytes 2228224 | tf_op jit(solution)/shard_map/all_to_all | solution.py:189
  9.0 6.4 %copy.97 = bf16[128,16384]{0,1:T(8,128)(2,1)} copy(bf16[128,16384]{1,0:T(8,128)(2,1)} %param.10) | data formatting | bytes 8388608 | tf_op args[0]
  15.3 10.3 %all-to-all-done = bf16[128,8,544]{0,2,1:T(8,128)(2,1)S(1)} async-done(((bf16[128,8,544]{0,2,1:T(8,128)(2,1)}), bf16[128,8,544]{0,2,1:T(8,128)(2,1)S(1)}, u32[]{:S(2)}, u32[]{:S(2)}) %all-to-all-start) | async-done | bytes 1114144 | tf_op jit(solution)/shard_map/all_to_all | solution.py:189
  25.6 4.7 %all-to-all-start.1 = ((bf16[128,8,2048]{0,2,1:T(8,128)(2,1)}), bf16[128,8,2048]{0,2,1:T(8,128)(2,1)}, u32[]{:S(2)}, u32[]{:S(2)}) async-start(bf16[128,8,2048]{0,2,1:T(8,128)(2,1)} %bitcast.198), calls=%async_computation.1 | async-start | bytes 8388608 | tf_op jit(solution)/shard_map/all_to_all | solution.py:194
  35.2 4.3 %reduce-window.6 = f32[4,32,2,128]{3,1,2,0:T(8,128)S(1)} reduce-window(f32[4,32,2,128]{3,1,2,0:T(8,128)} %copy.88, f32[]{:T(128)} %constant.53.clone.1), window={size=1x1x1x128 pad=0_0x0_0x0_0x127_0}, to_apply=%region_0.0 | reduce-window | flops 4161536 | bytes 262148 | tf_op jit(solution)/shard_map/reduce-window
  44.8 35.1 %all-to-all-done.1 = bf16[128,8,2048]{0,2,1:T(8,128)(2,1)} async-done(((bf16[128,8,2048]{0,2,1:T(8,128)(2,1)}), bf16[128,8,2048]{0,2,1:T(8,128)(2,1)}, u32[]{:S(2)}, u32[]{:S(2)}) %all-to-all-start.1) | async-done | bytes 4194336 | tf_op jit(solution)/shard_map/all_to_all | solution.py:194
  80.0 6.2 %copy.98 = bf16[8,128,2048]{1,0,2:T(8,128)(2,1)} copy(bf16[8,128,2048]{1,2,0:T(8,128)(2,1)} %bitcast.13) | data formatting | bytes 8388608 | tf_op jit(solution)/shard_map/all_to_all | solution.py:194
  86.1 7.6 %reshape.329 = bf16[4,256,32,64]{1,0,3,2:T(4,128)(2,1)} reshape(bf16[8,128,2048]{1,0,2:T(8,128)(2,1)} %copy.98) | data formatting | bytes 8388608 | tf_op jit(solution)/shard_map/reshape | solution.py:53
  93.7 6.7 %fusion.16 = f32[4,32,64,256]{3,2,1,0:T(8,128)} fusion(bf16[4,256,256,1]{2,1,3,0:T(8,128)(2,1)S(1)} %bitcast.209, f32[4,256,32]{1,2,0:T(8,128)S(1)} %get-tuple-element.198, bf16[4,256,32,64]{1,0,3,2:T(4,128)(2,1)} %reshape.329), kind=kOutput, calls=%fused_computation.26 | convolution fusion | flops 1080033280 | bytes 13238272 | tf_op jit(solution)/shard_map/ksgjp,ksgn->kgjpn/dot_general | solution.py:59
  100.4 14.0 %while.26 = (s32[]{:T(128)}, f32[32,64,256]{2,1,0:T(8,128)S(1)}, f32[4,32,64,256]{3,2,1,0:T(8,128)}, f32[4,32]{1,0:T(4,128)S(1)}, f32[4,32,64,256]{3,2,1,0:T(8,128)}, /*index=5*/s32[]{:T(128)}, s32[]{:T(128)}) while((s32[]{:T(128)}, f32[32,64,256]{2,1,0:T(8,128)S(1)}, f32[4,32,64,256]{3,2,1,0:T(8,128)}, f32[4,32]{1,0:T(4,128)S(1)}, ...), condition=%wide.region_5.6_spmd.clone, body=%wide.region_4.5_spmd.clone.sunk | while | flops 2097155 | bytes 10486252 | solution.py:70
  114.6 4.6 %collective-permute-start = (bf16[1040,256]{1,0:T(8,128)(2,1)S(1)}, bf16[1040,256]{1,0:T(8,128)(2,1)S(1)}, u32[]{:S(2)}, u32[]{:S(2)}) collective-permute-start(bf16[1040,256]{1,0:T(8,128)(2,1)S(1)} %fusion.38), channel_id=1, source_target_pairs={{0,8},{8,0},{1,9},{9,1},{2,10},{10,2},{3,11},{11,3},{4,12},{12,4},... | collective-permute-start | bytes 1597448 | tf_op jit(solution)/shard_map/ppermute | solution.py:99
  119.1 19.2 %collective-permute-done = bf16[1040,256]{1,0:T(8,128)(2,1)S(1)} collective-permute-done((bf16[1040,256]{1,0:T(8,128)(2,1)S(1)}, bf16[1040,256]{1,0:T(8,128)(2,1)S(1)}, u32[]{:S(2)}, u32[]{:S(2)}) %collective-permute-start) | collective-permute-done | bytes 532512 | tf_op jit(solution)/shard_map/ppermute | solution.py:99
  142.4 17.8 %collective-permute-done.1 = bf16[1040,256]{1,0:T(8,128)(2,1)S(1)} collective-permute-done((bf16[1040,256]{1,0:T(8,128)(2,1)S(1)}, bf16[1040,256]{1,0:T(8,128)(2,1)S(1)}, u32[]{:S(2)}, u32[]{:S(2)}) %collective-permute-start.1) | collective-permute-done | bytes 532512 | tf_op jit(solution)/shard_map/ppermute | solution.py:20
  162.6 15.0 %collective-permute-done.2 = bf16[1040,256]{1,0:T(8,128)(2,1)S(1)} collective-permute-done((bf16[1040,256]{1,0:T(8,128)(2,1)S(1)}, bf16[1040,256]{1,0:T(8,128)(2,1)S(1)}, u32[]{:S(2)}, u32[]{:S(2)}) %collective-permute-start.2) | collective-permute-done | bytes 532512 | tf_op jit(solution)/shard_map/ppermute | solution.py:20
  184.1 10.6 %collective-permute-done.3 = bf16[1040,256]{1,0:T(8,128)(2,1)} collective-permute-done((bf16[1040,256]{1,0:T(8,128)(2,1)}, bf16[1040,256]{1,0:T(8,128)(2,1)}, u32[]{:S(2)}, u32[]{:S(2)}) %collective-permute-start.3) | collective-permute-done | bytes 532512 | tf_op jit(solution)/shard_map/ppermute | solution.py:20
  201.2 23.4 %while.25 = (s32[]{:T(128)}, bf16[4,32,256,256]{3,2,1,0:T(8,128)(2,1)}, f32[4,256,32]{1,2,0:T(8,128)}, bf16[4,256,1,256]{3,1,2,0:T(8,128)(2,1)}, bf16[4,256,1,25...) while((s32[]{:T(128)}, bf16[4,32,256,256]{3,2,1,0:T(8,128)(2,1)}, ...), condition=%wide.region_3.4_spmd.clone.clone, body=%wide.region_2.3_spmd.clone.clone.sunk | while | flops 46202880 | bytes 5342301 | solution.py:45
  229.4 4.7 %collective-permute-start.5 = (bf16[16,64,256]{2,1,0:T(8,128)(2,1)}, bf16[16,64,256]{2,1,0:T(8,128)(2,1)S(1)}, u32[]{:S(2)}, u32[]{:S(2)}) collective-permute-start(bf16[16,64,256]{2,1,0:T(8,128)(2,1)} %get-tuple-element.189), channel_id=1, source_target_pairs={{0,8},{8,0},{1,9},{9,1},{2,10},{10,2},{3,11},{11,3},{4,12},{12,4},... | collective-permute-start | bytes 1572872 | tf_op jit(solution)/shard_map/ppermute | solution.py:99
  234.1 12.7 %fusion.22 = f32[4,32,256,64]{2,3,1,0:T(8,128)} fusion(bf16[4,32,256,256]{3,2,1,0:T(8,128)(2,1)} %get-tuple-element.73, bf16[4,256,32,64]{1,0,3,2:T(4,128)(2,1)} %reshape.329), kind=kOutput, calls=%fused_computation.32 | convolution fusion | flops 1073741824 | bytes 29360128 | tf_op jit(solution)/shard_map/khts,kshp->kthp/dot_general | solution.py:55
  246.8 12.0 %collective-permute-done.5 = bf16[16,64,256]{2,1,0:T(8,128)(2,1)S(1)} collective-permute-done((bf16[16,64,256]{2,1,0:T(8,128)(2,1)}, bf16[16,64,256]{2,1,0:T(8,128)(2,1)S(1)}, u32[]{:S(2)}, u32[]{:S(2)}) %collective-permute-start.5) | collective-permute-done | bytes 524320 | tf_op jit(solution)/shard_map/ppermute | solution.py:99
  259.9 10.1 %fusion.13 = bf16[4,256,32,64]{1,3,2,0:T(8,128)(2,1)} fusion(f32[4,32,256,64]{2,3,1,0:T(8,128)} %fusion.22, f32[32]{0:T(128)S(1)} %dynamic_slice.49, f32[4,256,32]{1,2,0:T(8,128)S(1)} %copy-done.6, bf16[4,256,32,64]{1,0,3,2:T(4,128)(2,1)} %reshape.329, bf16[4,256,256,1]{2,1,3,0:T(8,128)(2,1)S(1)} %bitcast.212, f32[4,32,64,256]{3,2,1,0:T(8,128)} %get-tuple-element.74, ...), kind=kOutput, calls=%fused_computation.21 | convolution fusion | flops 1092616192 | bytes 27918976 | tf_op jit(solution)/shard_map/ktgn,kgjpn->ktgjp/dot_general | solution.py:150
  281.2 4.4 %all-to-all-start.3 = ((bf16[128,8,1024]{0,2,1:T(8,128)(2,1)}), bf16[128,8,1024]{0,2,1:T(8,128)(2,1)}, u32[]{:S(2)}, u32[]{:S(2)}) async-start(bf16[128,8,1024]{0,2,1:T(8,128)(2,1)} %copy.107), calls=%async_computation.3 | async-start | bytes 4194304 | tf_op jit(solution)/shard_map/all_to_all | solution.py:161
  293.1 19.7 %all-to-all-done.3 = bf16[128,8,1024]{0,2,1:T(8,128)(2,1)} async-done(((bf16[128,8,1024]{0,2,1:T(8,128)(2,1)}), bf16[128,8,1024]{0,2,1:T(8,128)(2,1)}, u32[]{:S(2)}, u32[]{:S(2)}) %all-to-all-start.3) | async-done | bytes 2097184 | tf_op jit(solution)/shard_map/all_to_all | solution.py:161
  312.8 29.6 %all_to_all.41 = bf16[128,8,1024]{0,2,1:T(8,128)(2,1)S(1)} all-to-all(bf16[128,8,1024]{0,2,1:T(8,128)(2,1)S(1)} %copy.105), channel_id=1, replica_groups=mesh['chain'=16,'half'=2,'lane'=8] {'lane'}, dimensions={1} | all-to-all | bytes 4194304 | tf_op jit(solution)/shard_map/all_to_all | solution.py:161
  346.3 6.4 %copy.108 = bf16[128,16384]{1,0:T(8,128)(2,1)} copy(bf16[128,16384]{0,1:T(8,128)(2,1)} %bitcast.199) | data formatting | bytes 8388608 | tf_op jit(solution)/shard_map/reshape | solution.py:163
  (131 shorter events, 99.9 us)
Async XLA Ops:
  4.7 20.9 %all-to-all-start = ((bf16[128,8,544]{0,2,1:T(8,128)(2,1)}), bf16[128,8,544]{0,2,1:T(8,128)(2,1)S(1)}, u32[]{:S(2)}, u32[]{:S(2)}) async-start(bf16[128,8,544]{0,2,1:T(8,128)(2,1)} %pad_maximum_fusion.1), calls=%async_computation | async-start | bytes 2228224 | tf_op jit(solution)/shard_map/all_to_all | solution.py:189
  25.6 4.7 %copy-start.8 = (f32[256]{0:T(256)S(1)}, f32[256]{0:T(256)}, u32[]{:S(2)}) copy-start(f32[256]{0:T(256)} %param.14) | copy-start | bytes 3076
  25.6 54.3 %all-to-all-start.1 = ((bf16[128,8,2048]{0,2,1:T(8,128)(2,1)}), bf16[128,8,2048]{0,2,1:T(8,128)(2,1)}, u32[]{:S(2)}, u32[]{:S(2)}) async-start(bf16[128,8,2048]{0,2,1:T(8,128)(2,1)} %bitcast.198), calls=%async_computation.1 | async-start | bytes 8388608 | tf_op jit(solution)/shard_map/all_to_all | solution.py:194
  43.7 50.1 %copy-start.1 = (bf16[1024,256]{1,0:T(8,128)(2,1)}, bf16[1024,256]{1,0:T(8,128)(2,1)S(1)}, u32[]{:S(2)}) copy-start(bf16[1024,256]{1,0:T(8,128)(2,1)S(1)} %copy.93) | copy-start | bytes 1572868
  43.8 42.3 %copy-start.5 = (f32[4,256,32]{1,2,0:T(8,128)}, f32[4,256,32]{1,2,0:T(8,128)S(1)}, u32[]{:S(2)}) copy-start(f32[4,256,32]{1,2,0:T(8,128)S(1)} %bitcast_bitcast_fusion) | copy-start | bytes 393220
  114.6 23.7 %collective-permute-start = (bf16[1040,256]{1,0:T(8,128)(2,1)S(1)}, bf16[1040,256]{1,0:T(8,128)(2,1)S(1)}, u32[]{:S(2)}, u32[]{:S(2)}) collective-permute-start(bf16[1040,256]{1,0:T(8,128)(2,1)S(1)} %fusion.38), channel_id=1, source_target_pairs={{0,8},{8,0},{1,9},{9,1},{2,10},{10,2},{3,11},{11,3},{4,12},{12,4},... | collective-permute-start | bytes 1597448 | tf_op jit(solution)/shard_map/ppermute | solution.py:99
  138.9 21.3 %collective-permute-start.1 = (bf16[1040,256]{1,0:T(8,128)(2,1)S(1)}, bf16[1040,256]{1,0:T(8,128)(2,1)S(1)}, u32[]{:S(2)}, u32[]{:S(2)}) collective-permute-start(bf16[1040,256]{1,0:T(8,128)(2,1)S(1)} %fusion.39), channel_id=1, source_target_pairs={{0,16},{16,32},{32,48},{48,64},{64,80},{80,96},{96,112},{112,128},... | collective-permute-start | bytes 1597448 | tf_op jit(solution)/shard_map/ppermute | solution.py:20
  160.7 16.9 %collective-permute-start.2 = (bf16[1040,256]{1,0:T(8,128)(2,1)S(1)}, bf16[1040,256]{1,0:T(8,128)(2,1)S(1)}, u32[]{:S(2)}, u32[]{:S(2)}) collective-permute-start(bf16[1040,256]{1,0:T(8,128)(2,1)S(1)} %fusion.40), channel_id=1, source_target_pairs={{0,32},{16,48},{32,64},{48,80},{64,96},{80,112},{96,128},{112,144}... | collective-permute-start | bytes 1597448 | tf_op jit(solution)/shard_map/ppermute | solution.py:20
  177.7 0.9 copy-start.7
  178.5 0.8 copy-start
  178.5 3.5 copy-start.9
  180.7 14.0 %collective-permute-start.3 = (bf16[1040,256]{1,0:T(8,128)(2,1)}, bf16[1040,256]{1,0:T(8,128)(2,1)}, u32[]{:S(2)}, u32[]{:S(2)}) collective-permute-start(bf16[1040,256]{1,0:T(8,128)(2,1)} %fusion.41), channel_id=1, source_target_pairs={{0,64},{16,80},{32,96},{48,112},{64,128},{80,144},{96,160},{112,17... | collective-permute-start | bytes 1597448 | tf_op jit(solution)/shard_map/ppermute | solution.py:20
  196.5 0.8 copy-start.3
  199.8 25.4 %collective-permute-start.4 = (bf16[1040,256]{1,0:T(8,128)(2,1)}, bf16[1040,256]{1,0:T(8,128)(2,1)}, u32[]{:S(2)}, u32[]{:S(2)}) collective-permute-start(bf16[1040,256]{1,0:T(8,128)(2,1)} %fusion.42), channel_id=1, source_target_pairs={{0,128},{16,144},{32,160},{48,176},{64,192},{80,208},{96,224},{112... | collective-permute-start | bytes 1597448 | tf_op jit(solution)/shard_map/ppermute | solution.py:20
  229.4 29.4 %collective-permute-start.5 = (bf16[16,64,256]{2,1,0:T(8,128)(2,1)}, bf16[16,64,256]{2,1,0:T(8,128)(2,1)S(1)}, u32[]{:S(2)}, u32[]{:S(2)}) collective-permute-start(bf16[16,64,256]{2,1,0:T(8,128)(2,1)} %get-tuple-element.189), channel_id=1, source_target_pairs={{0,8},{8,0},{1,9},{9,1},{2,10},{10,2},{3,11},{11,3},{4,12},{12,4},... | collective-permute-start | bytes 1572872 | tf_op jit(solution)/shard_map/ppermute | solution.py:99
  246.8 12.1 %copy-start.4 = (f32[16,64,256]{2,1,0:T(8,128)S(1)}, f32[16,64,256]{2,1,0:T(8,128)}, u32[]{:S(2)}) copy-start(f32[16,64,256]{2,1,0:T(8,128)} %get-tuple-element.188) | copy-start | bytes 3145732
  258.9 1.0 copy-start.2
  258.9 1.1 copy-start.6
  281.2 31.6 %all-to-all-start.3 = ((bf16[128,8,1024]{0,2,1:T(8,128)(2,1)}), bf16[128,8,1024]{0,2,1:T(8,128)(2,1)}, u32[]{:S(2)}, u32[]{:S(2)}) async-start(bf16[128,8,1024]{0,2,1:T(8,128)(2,1)} %copy.107), calls=%async_computation.3 | async-start | bytes 4194304 | tf_op jit(solution)/shard_map/all_to_all | solution.py:161
